TPU v7x, 512 devices: a whole 4x4x16 slice. The times are simulated.
512 devices in a mesh: pts: 32 (over z_hi, y, core), lists: 16 (over x, z_lo).
Axes of the slice: x: 4, y: 4, z: 16 (z_hi: 4, z_lo: 4; z = z_hi * 4 + z_lo), core: 2. Of those that a mesh axis runs over, the one named last changes fastest.
Arguments:
- points: bfloat16 [12288, 256], P('pts'), may hold values from -4 to 4
- centroids: bfloat16 [65536, 256], P('lists'), may hold values from -0.375 to 0.375
- prior: int32 [12288], P('pts'), may hold values from 0 to 65535
- loads: int32 [65536], P('lists'), may hold values from 2 to 14, as said below
Outputs:
- centroid_means: float32 [256, 65536], P('pts', 'lists')
- log_col_scale: float32 [65536], P('lists')
Inputs may be any that keep to these rules, and one draw needn't show every extreme that they name: Lists 2k and 2k + 1 have loads 8 + e and 8 - e for some e of 0 to 6, so all loads sum to 524288.
All inputs are finite; a program needn't handle non-finite values.
Results may differ from a plain program's by a relative error of at most 0.003.
Values sent between devices are 32-bit elements; how exact they have to be, the bound alone decides.
No kernel may reach another device: no remote copies, remote signals or barrier semaphores. Data moves between devices by JAX's collectives and lax.ppermute only.
A program may use at most 64 MiB of HBM per device.

v0:
```python
import jax
import jax.numpy as jnp
from jax import lax
from jax.sharding import PartitionSpec as P

ITERS = 3
BLOCK = 512


def kernel_tile(points, cent_block, prior, start):
    score = lax.dot_general(
        points, cent_block, (((1,), (1,)), ((), ())), preferred_element_type=jnp.float32
    )
    cols = start + lax.iota(jnp.int32, cent_block.shape[0])
    hit = (prior[:, None] == cols[None, :]).astype(jnp.float32)
    return jnp.exp(3.0 * score + 10.0 * hit)


def point_mass(partial_value):
    return lax.psum(partial_value, "lists")


def list_mass(partial_value):
    return lax.psum(partial_value, "pts")


def local(points, centroids, prior, loads):
    n_lists = centroids.shape[0]
    count = n_lists // BLOCK
    offset = lax.axis_index("lists") * n_lists
    total_pts = points.shape[0] * lax.axis_size("pts")
    total_lists = n_lists * lax.axis_size("lists")
    target = loads.astype(jnp.float32) * (total_pts / (8.0 * total_lists))

    def tile(index):
        block = centroids[index * BLOCK : (index + 1) * BLOCK]
        return kernel_tile(points, block, prior, offset + index * BLOCK)

    col_scale = jnp.ones((n_lists,), jnp.float32)
    row_scale = jnp.ones((points.shape[0],), jnp.float32)
    for step in range(ITERS):
        partial_value = jnp.zeros((points.shape[0],), jnp.float32)
        for index in range(count):
            partial_value = partial_value + jnp.sum(
                tile(index) * col_scale[None, index * BLOCK : (index + 1) * BLOCK], axis=1
            )
        row_scale = 1.0 / point_mass(partial_value)
        pieces = [jnp.sum(tile(index) * row_scale[:, None], axis=0) for index in range(count)]
        col_scale = target / list_mass(jnp.concatenate(pieces))
    plan = jnp.concatenate(
        [
            (
                tile(index)
                * row_scale[:, None]
                * col_scale[None, index * BLOCK : (index + 1) * BLOCK]
            ).astype(jnp.bfloat16)
            for index in range(count)
        ],
        axis=1,
    )
    sums = lax.psum_scatter(
        lax.dot_general(points, plan, (((0,), (0,)), ((), ())), preferred_element_type=jnp.float32),
        "pts",
        scatter_dimension=0,
        tiled=True,
    )
    return (sums / target[None, :], jnp.log(col_scale))


def solution(mesh):
    return jax.shard_map(
        local,
        mesh=mesh,
        in_specs=(P("pts", None), P("lists", None), P("pts"), P("lists")),
        out_specs=(P("pts", "lists"), P("lists")),
        check_vma=False,
    )
```

profile of v0, /device:TPU:1, one launch (start us, length us, event | category | flops | bytes accessed | tf_op | source)
XLA Modules:
  0.0 817.4 jit_solution(7566929456988969409)
XLA Ops:
  7.2 0.0 copy-start
  7.2 0.0 reduce-scatter.4.cloned.1.call-start
  7.4 0.7 copy-done
  8.1 1.4 fusion.40
  9.5 1.4 fusion.41
  10.9 0.4 fusion.42
  11.3 0.4 fusion.43
  11.7 1.2 fusion.44
  13.0 1.2 fusion.45
  14.2 1.2 fusion.47
  15.5 1.2 fusion.46
  16.7 38.5 %psum.42 = f32[384]{0:T(512)S(1)} all-reduce(f32[384]{0:T(512)S(1)} %add_add_fusion.2), channel_id=1, replica_groups=mesh['pts'=32,'lists'=16] {'lists'}, use_global_device_ids=true, to_apply=%region_8.0 | all-reduce | flops 384 | bytes 3072 | tf_op jit(solution)/shard_map/psum | solution.py:20
  55.2 2.7 multiply_reduce_fusion.24
  58.1 169.3 %psum.43 = f32[4096]{0:T(1024)S(1)} all-reduce(f32[4096]{0:T(1024)S(1)} %constant_dynamic-update-slice_fusion.3), channel_id=1, replica_groups=mesh['pts'=32,'lists'=16] {'pts'}, use_global_device_ids=true, to_apply=%region_17.0 | all-reduce | flops 4096 | bytes 32768 | tf_op jit(solution)/shard_map/psum | solution.py:24
  227.4 1.7 multiply_reduce_fusion.22
  229.1 0.2 multiply_reduce_fusion.16
  229.3 0.2 multiply_reduce_fusion.18
  229.5 0.2 multiply_reduce_fusion.20
  229.7 31.0 %psum.44 = f32[384]{0:T(512)S(1)} all-reduce(f32[384]{0:T(512)S(1)} %add_add_fusion.1), channel_id=1, replica_groups=mesh['pts'=32,'lists'=16] {'lists'}, use_global_device_ids=true, to_apply=%region_26.0 | all-reduce | flops 384 | bytes 3072 | tf_op jit(solution)/shard_map/psum | solution.py:20
  260.7 2.7 multiply_reduce_fusion.8
  263.6 173.9 %psum.45 = f32[4096]{0:T(1024)S(1)} all-reduce(f32[4096]{0:T(1024)S(1)} %constant_dynamic-update-slice_fusion.4), channel_id=1, replica_groups=mesh['pts'=32,'lists'=16] {'pts'}, use_global_device_ids=true, to_apply=%region_35.0 | all-reduce | flops 4096 | bytes 32768 | tf_op jit(solution)/shard_map/psum | solution.py:24
  437.5 1.4 multiply_reduce_fusion.6
  438.9 0.2 multiply_reduce_fusion
  439.1 0.2 multiply_reduce_fusion.1
  439.2 0.2 multiply_reduce_fusion.2
  439.4 0.2 multiply_reduce_fusion.3
  439.5 0.2 multiply_reduce_fusion.4
  439.7 0.2 multiply_reduce_fusion.5
  439.8 0.2 multiply_reduce_fusion.7
  440.0 32.8 %psum.46 = f32[384]{0:T(512)S(1)} all-reduce(f32[384]{0:T(512)S(1)} %add_add_fusion), channel_id=1, replica_groups=mesh['pts'=32,'lists'=16] {'lists'}, use_global_device_ids=true, to_apply=%region_44.0 | all-reduce | flops 384 | bytes 3072 | tf_op jit(solution)/shard_map/psum | solution.py:20
  472.8 2.7 multiply_reduce_fusion.32
  475.6 174.3 %psum.47 = f32[4096]{0:T(1024)S(1)} all-reduce(f32[4096]{0:T(1024)S(1)} %constant_dynamic-update-slice_fusion.5), channel_id=1, replica_groups=mesh['pts'=32,'lists'=16] {'pts'}, use_global_device_ids=true, to_apply=%region_53.0 | all-reduce | flops 4096 | bytes 32768 | tf_op jit(solution)/shard_map/psum | solution.py:24
  650.0 0.6 fusion.35
  650.6 1.3 fusion.16
  651.9 1.3 fusion.17
  653.1 1.3 fusion.18
  654.4 0.1 fusion.19
  654.5 0.1 fusion.20
  654.7 0.1 fusion.21
  654.8 0.1 fusion.22
  655.0 0.1 fusion.23
  655.1 3.3 convolution_bitcast_fusion
  658.4 5.6 copy.8
  664.0 0.0 reduce-scatter.4.cloned.1.call-update
  664.0 140.4 %reduce-scatter.4.cloned.1.call-done = f32[8,4096]{1,0:T(8,128)} async-done(((f32[256,4096]{1,0:T(8,128)}), f32[8,4096]{1,0:T(8,128)}) %reduce-scatter.4.cloned.1.call-update) | async-done | bytes 131088
  804.4 1.5 copy.9
  805.9 1.8 broadcast_divide_fusion
  807.7 2.8 copy.7
  (64 shorter events, 0.3 us)
Async XLA Ops:
  7.2 0.9 copy-start
  7.2 3.7 copy-start.9
  7.2 797.2 %reduce-scatter.4.cloned.1.call-start = ((), (), s32[]{:S(2)}) async-start(), calls=%async_computation.1 | async-start | bytes 4325376
  7.3 3.6 copy-start.8
  55.2 172.2 %copy-start.7 = (s32[4096]{0:T(1024)S(1)}, s32[4096]{0:T(1024)}, u32[]{:S(2)}) copy-start(s32[4096]{0:T(1024)} %param.7) | copy-start | bytes 49156
  227.4 2.1 copy-start.1
  227.4 2.1 copy-start.4
  437.4 2.1 copy-start.2
  437.4 2.2 copy-start.5
  437.4 2.4 copy-start.6
  650.0 4.4 copy-start.3
Sparse Core Ops, SparseCore 0:
  664.1 140.2 reduce-scatter.3
where the time goes:
time: 818 us; the launch traced here: 817 us
  blocking collectives  620 us (76%)
  waiting for transfers between devices  140 us (17%)
  other arithmetic  19.9 us (2%)
  between operations  14.5 us (2%)
  matrix products  11.8 us (1%)
  local copies, waits for them, and re-layouts  10.8 us (1%)
    psum x3, blocking collectives, list_mass(): return lax.psum(partial_value, 'pts')  518 us
    unnamed x2, waiting for transfers between devices  140 us
    psum x3, blocking collectives, point_mass(): return lax.psum(partial_value, 'lists')  102 us
  transfers between devices with their start and end apart: 1, of which 1 were waited for; matrix products, arithmetic and copies ran while one was open for 0% of the time, Pallas kernels for 0%

commit v1 on v0

--- a/solution.py
+++ b/solution.py
@@ -1,7 +1,7 @@
 import jax
 import jax.numpy as jnp
 from jax import lax
-from jax.sharding import PartitionSpec as P
+from jax.sharding import Mesh, PartitionSpec as P
 
 ITERS = 3
 BLOCK = 512
@@ -16,20 +16,40 @@
     return jnp.exp(3.0 * score + 10.0 * hit)
 
 
+PTS_AXES = (("z_hi", 4), ("y", 4), ("core", 2))
+LISTS_AXES = (("x", 4), ("z_lo", 4))
+PTS = tuple(name for name, _ in PTS_AXES)
+LISTS = tuple(name for name, _ in LISTS_AXES)
+
+
 def point_mass(partial_value):
-    return lax.psum(partial_value, "lists")
+    return lax.psum(lax.psum(partial_value, "z_lo"), "x")
 
 
 def list_mass(partial_value):
-    return lax.psum(partial_value, "pts")
+    return lax.psum(lax.psum(lax.psum(partial_value, "core"), "y"), "z_hi")
+
+
+def scatter_rows(points):
+    n = points.shape[0]
+    sizes = [size for _, size in PTS_AXES]
+    rows = points.shape[1] // (sizes[0] * sizes[1] * sizes[2])
+    blocked = points.reshape(n, sizes[0], sizes[1], sizes[2], rows)
+    return blocked.transpose(0, 3, 2, 1, 4).reshape(n, points.shape[1])
+
+
+def sum_scatter(value):
+    for name in ("core", "y", "z_hi"):
+        value = lax.psum_scatter(value, name, scatter_dimension=0, tiled=True)
+    return value
 
 
 def local(points, centroids, prior, loads):
     n_lists = centroids.shape[0]
     count = n_lists // BLOCK
-    offset = lax.axis_index("lists") * n_lists
-    total_pts = points.shape[0] * lax.axis_size("pts")
-    total_lists = n_lists * lax.axis_size("lists")
+    offset = (lax.axis_index("x") * lax.axis_size("z_lo") + lax.axis_index("z_lo")) * n_lists
+    total_pts = points.shape[0] * lax.axis_size(PTS)
+    total_lists = n_lists * lax.axis_size(LISTS)
     target = loads.astype(jnp.float32) * (total_pts / (8.0 * total_lists))
 
     def tile(index):
@@ -58,20 +78,21 @@
         ],
         axis=1,
     )
-    sums = lax.psum_scatter(
-        lax.dot_general(points, plan, (((0,), (0,)), ((), ())), preferred_element_type=jnp.float32),
-        "pts",
-        scatter_dimension=0,
-        tiled=True,
+    sums = sum_scatter(
+        lax.dot_general(scatter_rows(points), plan, (((0,), (0,)), ((), ())), preferred_element_type=jnp.float32)
     )
     return (sums / target[None, :], jnp.log(col_scale))
 
 
 def solution(mesh):
+    sizes = [size for _, size in PTS_AXES + LISTS_AXES]
+    assert mesh.shape["pts"] == sizes[0] * sizes[1] * sizes[2]
+    assert mesh.shape["lists"] == sizes[3] * sizes[4]
+    fine = Mesh(mesh.devices.reshape(sizes), PTS + LISTS)
     return jax.shard_map(
         local,
-        mesh=mesh,
-        in_specs=(P("pts", None), P("lists", None), P("pts"), P("lists")),
-        out_specs=(P("pts", "lists"), P("lists")),
+        mesh=fine,
+        in_specs=(P(PTS, None), P(LISTS, None), P(PTS), P(LISTS)),
+        out_specs=(P(PTS, LISTS), P(LISTS)),
         check_vma=False,
     )

time: 818 us -> 359 us (0.44)
  blocking collectives: 620 us -> 183 us
  waiting for transfers between devices: 140 us -> 107 us
  matrix products: 11.8 us -> 21.1 us
    psum x6 -> x15, blocking collectives: 620 us -> 183 us  [the longest x9 134 us: list_mass(): return lax.psum(lax.psum(lax.psum(partial_value, 'core'), 'y'), 'z_hi')]
    unnamed x2 -> x5, waiting for transfers between devices: 140 us -> 84.6 us
    reduce_scatter x0 -> x1, waiting for transfers between devices: none -> 22.5 us  [sum_scatter(): value = lax.psum_scatter(value, name, scatter_dimension=0, tiled=True)]
    dot_general x8, matrix products: 8.58 us -> 17.9 us  [kernel_tile(): lax.dot_general(points, cent_block, (((1,), (1,)), ((), ())), preferred_e...]
  transfers between devices with their start and end apart: 1 -> 3, of which waited for: 1 -> 3; matrix products, arithmetic and copies ran while one was open for 0% -> 0% of each run, Pallas kernels for 0% -> 0%
where the time goes in v1:
time: 359 us; the launch traced here: 358 us
  blocking collectives  183 us (51%)
  waiting for transfers between devices  107 us (30%)
  other arithmetic  23.9 us (7%)
  matrix products  21.1 us (6%)
  between operations  14.2 us (4%)
  local copies, waits for them, and re-layouts  8.55 us (2%)
    psum x9, blocking collectives, list_mass(): return lax.psum(lax.psum(lax.psum(partial_value, 'core'), 'y'), 'z_hi')  134 us
    unnamed x5, waiting for transfers between devices  84.6 us
    psum x6, blocking collectives, point_mass(): return lax.psum(lax.psum(partial_value, 'z_lo'), 'x')  49 us
    reduce_scatter x1, waiting for transfers between devices, sum_scatter(): value = lax.psum_scatter(value, name, scatter_dimension=0, tiled=True)  22.5 us
    dot_general x8, matrix products, kernel_tile(): lax.dot_general(points, cent_block, (((1,), (1,)), ((), ())), preferred_e...  17.9 us
    reduce_sum x12, other arithmetic, local(): jnp.sum(tile(index) * col_scale[None, index * BLOCK:(index + 1) * BLOCK],...  9.25 us
    unnamed x51, local copies, waits for them, and re-layouts  8.49 us
    reduce_sum x3, other arithmetic, local(): jnp.sum(tile(index) * row_scale[:, None], axis=0)  8.23 us
  transfers between devices with their start and end apart: 3, of which 3 were waited for; matrix products, arithmetic and copies ran while one was open for 0% of the time, Pallas kernels for 0%

profile of v1, /device:TPU:1, one launch (start us, length us, event | category | flops | bytes accessed | tf_op | source)
XLA Modules:
  0.0 358.1 jit_solution(12672845887132442647)
XLA Ops:
  7.3 0.6 iota_add_fusion.7
  7.9 1.1 copy.10
  9.0 2.0 fusion.40
  11.0 2.0 fusion.41
  13.0 2.0 fusion.42
  15.0 2.0 fusion.43
  17.0 2.7 fusion.44
  19.7 2.8 fusion.45
  22.5 2.2 fusion.47
  24.7 2.2 fusion.46
  27.0 11.8 %psum.105 = f32[384]{0:T(512)S(1)} all-reduce(f32[384]{0:T(512)S(1)} %add_add_fusion.2), channel_id=1, replica_groups=mesh['z_hi'=4,'y'=4,'core'=2,'x'=4,'z_lo'=4] {'z_lo'}, use_global_device_ids=true, to_apply=%region_8.0 | all-reduce | flops 384 | bytes 3072 | tf_op jit(solution)/shard_map/psum | solution.py:26
  38.8 8.5 %psum.106 = f32[384]{0:T(512)S(1)} all-reduce(f32[384]{0:T(512)S(1)} %psum.105), channel_id=1, replica_groups=mesh['z_hi'=4,'y'=4,'core'=2,'x'=4,'z_lo'=4] {'x'}, use_global_device_ids=true, to_apply=%region_9.0 | all-reduce | flops 384 | bytes 3072 | tf_op jit(solution)/shard_map/psum | solution.py:26
  47.3 2.8 multiply_reduce_fusion.24
  50.1 7.9 %psum.107 = f32[4096]{0:T(1024)S(1)} all-reduce(f32[4096]{0:T(1024)S(1)} %constant_dynamic-update-slice_fusion.3), channel_id=1, replica_groups=mesh['z_hi'=4,'y'=4,'core'=2,'x'=4,'z_lo'=4] {'core'}, use_global_device_ids=true, to_apply=%region_18.0 | all-reduce | flops 4096 | bytes 32768 | tf_op jit(solution)/shard_map/psum | solution.py:30
  58.0 13.4 %psum.108 = f32[4096]{0:T(1024)S(1)} all-reduce(f32[4096]{0:T(1024)S(1)} %psum.107), channel_id=1, replica_groups=mesh['z_hi'=4,'y'=4,'core'=2,'x'=4,'z_lo'=4] {'y'}, use_global_device_ids=true, to_apply=%region_19.0 | all-reduce | flops 4096 | bytes 32768 | tf_op jit(solution)/shard_map/psum | solution.py:30
  71.4 23.9 %psum.109 = f32[4096]{0:T(1024)S(1)} all-reduce(f32[4096]{0:T(1024)S(1)} %psum.108), channel_id=1, replica_groups=mesh['z_hi'=4,'y'=4,'core'=2,'x'=4,'z_lo'=4] {'z_hi'}, use_global_device_ids=true, to_apply=%region_20.0 | all-reduce | flops 4096 | bytes 32768 | tf_op jit(solution)/shard_map/psum | solution.py:30
  95.3 1.6 multiply_reduce_fusion.22
  96.9 1.6 multiply_reduce_fusion.20
  98.5 0.2 multiply_reduce_fusion.18
  98.7 0.2 multiply_reduce_fusion.16
  98.9 6.6 %psum.110 = f32[384]{0:T(512)S(1)} all-reduce(f32[384]{0:T(512)S(1)} %add_add_fusion.1), channel_id=1, replica_groups=mesh['z_hi'=4,'y'=4,'core'=2,'x'=4,'z_lo'=4] {'z_lo'}, use_global_device_ids=true, to_apply=%region_29.0 | all-reduce | flops 384 | bytes 3072 | tf_op jit(solution)/shard_map/psum | solution.py:26
  105.5 6.0 %psum.111 = f32[384]{0:T(512)S(1)} all-reduce(f32[384]{0:T(512)S(1)} %psum.110), channel_id=1, replica_groups=mesh['z_hi'=4,'y'=4,'core'=2,'x'=4,'z_lo'=4] {'x'}, use_global_device_ids=true, to_apply=%region_30.0 | all-reduce | flops 384 | bytes 3072 | tf_op jit(solution)/shard_map/psum | solution.py:26
  111.5 2.7 multiply_reduce_fusion.8
  114.4 14.4 %psum.112 = f32[4096]{0:T(1024)S(1)} all-reduce(f32[4096]{0:T(1024)S(1)} %constant_dynamic-update-slice_fusion.4), channel_id=1, replica_groups=mesh['z_hi'=4,'y'=4,'core'=2,'x'=4,'z_lo'=4] {'core'}, use_global_device_ids=true, to_apply=%region_39.0 | all-reduce | flops 4096 | bytes 32768 | tf_op jit(solution)/shard_map/psum | solution.py:30
  128.8 11.1 %psum.113 = f32[4096]{0:T(1024)S(1)} all-reduce(f32[4096]{0:T(1024)S(1)} %psum.112), channel_id=1, replica_groups=mesh['z_hi'=4,'y'=4,'core'=2,'x'=4,'z_lo'=4] {'y'}, use_global_device_ids=true, to_apply=%region_40.0 | all-reduce | flops 4096 | bytes 32768 | tf_op jit(solution)/shard_map/psum | solution.py:30
  139.9 19.3 %psum.114 = f32[4096]{0:T(1024)S(1)} all-reduce(f32[4096]{0:T(1024)S(1)} %psum.113), channel_id=1, replica_groups=mesh['z_hi'=4,'y'=4,'core'=2,'x'=4,'z_lo'=4] {'z_hi'}, use_global_device_ids=true, to_apply=%region_41.0 | all-reduce | flops 4096 | bytes 32768 | tf_op jit(solution)/shard_map/psum | solution.py:30
  159.2 1.3 multiply_reduce_fusion.6
  160.5 1.3 multiply_reduce_fusion.7
  161.8 1.3 multiply_reduce_fusion.5
  163.1 1.3 multiply_reduce_fusion.4
  164.4 0.2 multiply_reduce_fusion.3
  165.0 8.3 %psum.115 = f32[384]{0:T(512)S(1)} all-reduce(f32[384]{0:T(512)S(1)} %add_add_fusion), channel_id=1, replica_groups=mesh['z_hi'=4,'y'=4,'core'=2,'x'=4,'z_lo'=4] {'z_lo'}, use_global_device_ids=true, to_apply=%region_50.0 | all-reduce | flops 384 | bytes 3072 | tf_op jit(solution)/shard_map/psum | solution.py:26
  173.3 7.8 %psum.116 = f32[384]{0:T(512)S(1)} all-reduce(f32[384]{0:T(512)S(1)} %psum.115), channel_id=1, replica_groups=mesh['z_hi'=4,'y'=4,'core'=2,'x'=4,'z_lo'=4] {'x'}, use_global_device_ids=true, to_apply=%region_51.0 | all-reduce | flops 384 | bytes 3072 | tf_op jit(solution)/shard_map/psum | solution.py:26
  181.2 2.7 multiply_reduce_fusion.32
  184.0 14.2 %psum.117 = f32[4096]{0:T(1024)S(1)} all-reduce(f32[4096]{0:T(1024)S(1)} %constant_dynamic-update-slice_fusion.5), channel_id=1, replica_groups=mesh['z_hi'=4,'y'=4,'core'=2,'x'=4,'z_lo'=4] {'core'}, use_global_device_ids=true, to_apply=%region_60.0 | all-reduce | flops 4096 | bytes 32768 | tf_op jit(solution)/shard_map/psum | solution.py:30
  198.2 11.7 %psum.118 = f32[4096]{0:T(1024)S(1)} all-reduce(f32[4096]{0:T(1024)S(1)} %psum.117), channel_id=1, replica_groups=mesh['z_hi'=4,'y'=4,'core'=2,'x'=4,'z_lo'=4] {'y'}, use_global_device_ids=true, to_apply=%region_61.0 | all-reduce | flops 4096 | bytes 32768 | tf_op jit(solution)/shard_map/psum | solution.py:30
  209.8 18.2 %psum.119 = f32[4096]{0:T(1024)S(1)} all-reduce(f32[4096]{0:T(1024)S(1)} %psum.118), channel_id=1, replica_groups=mesh['z_hi'=4,'y'=4,'core'=2,'x'=4,'z_lo'=4] {'z_hi'}, use_global_device_ids=true, to_apply=%region_62.0 | all-reduce | flops 4096 | bytes 32768 | tf_op jit(solution)/shard_map/psum | solution.py:30
  228.0 0.6 fusion.35
  228.6 1.3 fusion.16
  229.9 1.3 fusion.17
  232.1 3.2 convolution_bitcast_fusion
  235.4 22.5 %reduce-scatter.8.cloned.1.call-done = f32[128,4096]{0,1:T(8,128)} async-done(((f32[256,4096]{0,1:T(8,128)}), f32[128,4096]{0,1:T(8,128)}) %reduce-scatter.8.cloned.1.call-update) | async-done | bytes 2097168 | tf_op jit(solution)/shard_map/reduce_scatter | solution.py:43
  257.9 2.9 copy.13
  260.9 37.7 %reduce-scatter.10.cloned.1.call-done = f32[32,4096]{1,0:T(8,128)} async-done(((f32[128,4096]{1,0:T(8,128)}), f32[32,4096]{1,0:T(8,128)}) %reduce-scatter.10.cloned.1.call-update) | async-done | bytes 524304
  298.6 46.9 %reduce-scatter.12.cloned.1.call-done = f32[8,4096]{1,0:T(8,128)} async-done(((f32[32,4096]{1,0:T(8,128)}), f32[8,4096]{1,0:T(8,128)}) %reduce-scatter.12.cloned.1.call-update) | async-done | bytes 131088
  345.4 1.5 copy.16
  347.0 1.8 broadcast_divide_fusion
  348.7 2.8 copy.12
  (87 shorter events, 1.7 us)
Async XLA Ops:
  7.2 5.8 %copy-start.2 = (bf16[384,256]{1,0:T(8,128)(2,1)S(1)}, bf16[384,256]{1,0:T(8,128)(2,1)}, u32[]{:S(2)}) copy-start(bf16[384,256]{1,0:T(8,128)(2,1)} %param.4) | copy-start | bytes 589828
  7.2 5.8 %copy-start.12 = (s32[384]{0:T(512)S(1)}, s32[384]{0:T(512)}, u32[]{:S(2)}) copy-start(s32[384]{0:T(512)} %param.6) | copy-start | bytes 4612
  7.2 250.7 %reduce-scatter.8.cloned.1.call-start = ((), (), s32[]{:S(2)}) async-start(), calls=%async_computation.3 | async-start | bytes 6291456 | tf_op jit(solution)/shard_map/reduce_scatter | solution.py:43
  22.5 4.4 %copy-start.6 = (f32[384]{0:T(512)S(1)}, f32[384]{0:T(512)}, u32[]{:S(2)}) copy-start(f32[384]{0:T(512)} %get-tuple-element.60) | copy-start | bytes 4612
  22.5 4.4 %copy-start.7 = (f32[384]{0:T(512)S(1)}, f32[384]{0:T(512)}, u32[]{:S(2)}) copy-start(f32[384]{0:T(512)} %get-tuple-element.62) | copy-start | bytes 4612
  22.5 4.4 %copy-start.8 = (f32[384]{0:T(512)S(1)}, f32[384]{0:T(512)}, u32[]{:S(2)}) copy-start(f32[384]{0:T(512)} %get-tuple-element.64) | copy-start | bytes 4612
  22.5 4.4 %copy-start.9 = (f32[384]{0:T(512)S(1)}, f32[384]{0:T(512)}, u32[]{:S(2)}) copy-start(f32[384]{0:T(512)} %get-tuple-element.66) | copy-start | bytes 4612
  22.5 4.4 %copy-start.10 = (f32[384]{0:T(512)S(1)}, f32[384]{0:T(512)}, u32[]{:S(2)}) copy-start(f32[384]{0:T(512)} %get-tuple-element.68) | copy-start | bytes 4612
  22.5 4.4 %copy-start.11 = (f32[384]{0:T(512)S(1)}, f32[384]{0:T(512)}, u32[]{:S(2)}) copy-start(f32[384]{0:T(512)} %get-tuple-element.70) | copy-start | bytes 4612
  47.3 2.8 copy-start.5
  47.3 48.1 %copy-start.3 = (s32[4096]{0:T(1024)S(1)}, s32[4096]{0:T(1024)}, u32[]{:S(2)}) copy-start(s32[4096]{0:T(1024)} %param.7) | copy-start | bytes 49156
  111.5 2.8 copy-start.4
  228.0 3.2 copy-start.1
  228.0 3.4 copy-start
  235.3 63.2 %reduce-scatter.10.cloned.1.call-start = ((), (), s32[]{:S(2)}) async-start(), calls=%async_computation.4 | async-start | bytes 2621440
  260.8 84.6 %reduce-scatter.12.cloned.1.call-start = ((), (), s32[]{:S(2)}) async-start(), calls=%async_computation.5 | async-start | bytes 655360
Sparse Core Ops, SparseCore 0:
  235.4 22.3 reduce-scatter.7
  261.0 37.5 reduce-scatter.9
  301.4 44.0 reduce-scatter.11

commit v2 on v1

--- a/solution.py
+++ b/solution.py
@@ -40,7 +40,9 @@
 
 def sum_scatter(value):
     for name in ("core", "y", "z_hi"):
-        value = lax.psum_scatter(value, name, scatter_dimension=0, tiled=True)
+        n = lax.axis_size(name)
+        blocks = value.reshape(n, value.shape[0] // n, value.shape[1])
+        value = jnp.sum(lax.all_to_all(blocks, name, 0, 0), axis=0)
     return value
 
 

time: 359 us -> 313 us (0.87)
  waiting for transfers between devices: 107 us -> 0 us
  blocking collectives: 183 us -> 261 us
  between operations: 14.2 us -> 1.12 us
  local copies, waits for them, and re-layouts: 8.55 us -> 1.31 us
    unnamed x5 -> x0, waiting for transfers between devices: 84.6 us -> none
    all_to_all x0 -> x3, blocking collectives: none -> 78.4 us  [sum_scatter(): value = jnp.sum(lax.all_to_all(blocks, name, 0, 0), axis=0)]
    reduce_scatter x1 -> x0, waiting for transfers between devices: 22.5 us -> none  [sum_scatter(): value = lax.psum_scatter(value, name, scatter_dimension=0, tiled=True)]
    unnamed x51 -> x48, local copies, waits for them, and re-layouts: 8.49 us -> 1.26 us
    reduce_sum x0 -> x3, other arithmetic: none -> 4.47 us  [sum_scatter(): value = jnp.sum(lax.all_to_all(blocks, name, 0, 0), axis=0)]
  transfers between devices with their start and end apart: 3 -> 0, of which waited for: 3 -> 0; matrix products, arithmetic and copies ran while one was open for 0% -> 0% of each run, Pallas kernels for 0% -> 0%
where the time goes in v2:
time: 313 us; the launch traced here: 310 us
  blocking collectives  261 us (83%)
  other arithmetic  27.3 us (9%)
  matrix products  19.2 us (6%)
    psum x9, blocking collectives, list_mass(): return lax.psum(lax.psum(lax.psum(partial_value, 'core'), 'y'), 'z_hi')  134 us
    all_to_all x3, blocking collectives, sum_scatter(): value = jnp.sum(lax.all_to_all(blocks, name, 0, 0), axis=0)  78.4 us
    psum x6, blocking collectives, point_mass(): return lax.psum(lax.psum(partial_value, 'z_lo'), 'x')  49 us
    dot_general x8, matrix products, kernel_tile(): lax.dot_general(points, cent_block, (((1,), (1,)), ((), ())), preferred_e...  17.9 us
    reduce_sum x12, other arithmetic, local(): jnp.sum(tile(index) * col_scale[None, index * BLOCK:(index + 1) * BLOCK],...  9.25 us
    reduce_sum x3, other arithmetic, local(): jnp.sum(tile(index) * row_scale[:, None], axis=0)  8.23 us

profile of v2, /device:TPU:1, one launch (start us, length us, event | category | flops | bytes accessed | tf_op | source)
XLA Modules:
  0.0 310.3 jit_solution(11819051623203954163)
XLA Ops:
  0.7 0.6 iota_add_fusion.7
  1.3 1.1 copy.8
  2.4 2.0 fusion.40
  4.4 2.0 fusion.41
  6.4 2.0 fusion.42
  8.4 2.0 fusion.43
  10.4 2.7 fusion.44
  13.1 2.8 fusion.45
  16.0 2.2 fusion.47
  18.2 2.2 fusion.46
  20.4 11.8 %psum.105 = f32[384]{0:T(512)S(1)} all-reduce(f32[384]{0:T(512)S(1)} %add_add_fusion.2), channel_id=1, replica_groups=mesh['z_hi'=4,'y'=4,'core'=2,'x'=4,'z_lo'=4] {'z_lo'}, use_global_device_ids=true, to_apply=%region_8.0 | all-reduce | flops 384 | bytes 3072 | tf_op jit(solution)/shard_map/psum | solution.py:26
  32.2 8.5 %psum.106 = f32[384]{0:T(512)S(1)} all-reduce(f32[384]{0:T(512)S(1)} %psum.105), channel_id=1, replica_groups=mesh['z_hi'=4,'y'=4,'core'=2,'x'=4,'z_lo'=4] {'x'}, use_global_device_ids=true, to_apply=%region_9.0 | all-reduce | flops 384 | bytes 3072 | tf_op jit(solution)/shard_map/psum | solution.py:26
  40.7 2.8 multiply_reduce_fusion.24
  43.5 7.9 %psum.107 = f32[4096]{0:T(1024)S(1)} all-reduce(f32[4096]{0:T(1024)S(1)} %constant_dynamic-update-slice_fusion.3), channel_id=1, replica_groups=mesh['z_hi'=4,'y'=4,'core'=2,'x'=4,'z_lo'=4] {'core'}, use_global_device_ids=true, to_apply=%region_18.0 | all-reduce | flops 4096 | bytes 32768 | tf_op jit(solution)/shard_map/psum | solution.py:30
  51.5 13.4 %psum.108 = f32[4096]{0:T(1024)S(1)} all-reduce(f32[4096]{0:T(1024)S(1)} %psum.107), channel_id=1, replica_groups=mesh['z_hi'=4,'y'=4,'core'=2,'x'=4,'z_lo'=4] {'y'}, use_global_device_ids=true, to_apply=%region_19.0 | all-reduce | flops 4096 | bytes 32768 | tf_op jit(solution)/shard_map/psum | solution.py:30
  64.8 23.9 %psum.109 = f32[4096]{0:T(1024)S(1)} all-reduce(f32[4096]{0:T(1024)S(1)} %psum.108), channel_id=1, replica_groups=mesh['z_hi'=4,'y'=4,'core'=2,'x'=4,'z_lo'=4] {'z_hi'}, use_global_device_ids=true, to_apply=%region_20.0 | all-reduce | flops 4096 | bytes 32768 | tf_op jit(solution)/shard_map/psum | solution.py:30
  88.8 1.6 multiply_reduce_fusion.22
  90.3 1.6 multiply_reduce_fusion.20
  91.9 0.2 multiply_reduce_fusion.18
  92.1 0.2 multiply_reduce_fusion.16
  92.3 6.6 %psum.110 = f32[384]{0:T(512)S(1)} all-reduce(f32[384]{0:T(512)S(1)} %add_add_fusion.1), channel_id=1, replica_groups=mesh['z_hi'=4,'y'=4,'core'=2,'x'=4,'z_lo'=4] {'z_lo'}, use_global_device_ids=true, to_apply=%region_29.0 | all-reduce | flops 384 | bytes 3072 | tf_op jit(solution)/shard_map/psum | solution.py:26
  98.9 6.0 %psum.111 = f32[384]{0:T(512)S(1)} all-reduce(f32[384]{0:T(512)S(1)} %psum.110), channel_id=1, replica_groups=mesh['z_hi'=4,'y'=4,'core'=2,'x'=4,'z_lo'=4] {'x'}, use_global_device_ids=true, to_apply=%region_30.0 | all-reduce | flops 384 | bytes 3072 | tf_op jit(solution)/shard_map/psum | solution.py:26
  104.9 2.7 multiply_reduce_fusion.8
  107.8 14.4 %psum.112 = f32[4096]{0:T(1024)S(1)} all-reduce(f32[4096]{0:T(1024)S(1)} %constant_dynamic-update-slice_fusion.4), channel_id=1, replica_groups=mesh['z_hi'=4,'y'=4,'core'=2,'x'=4,'z_lo'=4] {'core'}, use_global_device_ids=true, to_apply=%region_39.0 | all-reduce | flops 4096 | bytes 32768 | tf_op jit(solution)/shard_map/psum | solution.py:30
  122.2 11.1 %psum.113 = f32[4096]{0:T(1024)S(1)} all-reduce(f32[4096]{0:T(1024)S(1)} %psum.112), channel_id=1, replica_groups=mesh['z_hi'=4,'y'=4,'core'=2,'x'=4,'z_lo'=4] {'y'}, use_global_device_ids=true, to_apply=%region_40.0 | all-reduce | flops 4096 | bytes 32768 | tf_op jit(solution)/shard_map/psum | solution.py:30
  133.3 19.3 %psum.114 = f32[4096]{0:T(1024)S(1)} all-reduce(f32[4096]{0:T(1024)S(1)} %psum.113), channel_id=1, replica_groups=mesh['z_hi'=4,'y'=4,'core'=2,'x'=4,'z_lo'=4] {'z_hi'}, use_global_device_ids=true, to_apply=%region_41.0 | all-reduce | flops 4096 | bytes 32768 | tf_op jit(solution)/shard_map/psum | solution.py:30
  152.7 1.3 multiply_reduce_fusion.6
  153.9 1.3 multiply_reduce_fusion.7
  155.2 1.3 multiply_reduce_fusion.5
  156.5 1.3 multiply_reduce_fusion.4
  157.8 0.2 multiply_reduce_fusion.3
  158.3 0.2 multiply_reduce_fusion
  158.4 8.3 %psum.115 = f32[384]{0:T(512)S(1)} all-reduce(f32[384]{0:T(512)S(1)} %add_add_fusion), channel_id=1, replica_groups=mesh['z_hi'=4,'y'=4,'core'=2,'x'=4,'z_lo'=4] {'z_lo'}, use_global_device_ids=true, to_apply=%region_50.0 | all-reduce | flops 384 | bytes 3072 | tf_op jit(solution)/shard_map/psum | solution.py:26
  166.8 7.8 %psum.116 = f32[384]{0:T(512)S(1)} all-reduce(f32[384]{0:T(512)S(1)} %psum.115), channel_id=1, replica_groups=mesh['z_hi'=4,'y'=4,'core'=2,'x'=4,'z_lo'=4] {'x'}, use_global_device_ids=true, to_apply=%region_51.0 | all-reduce | flops 384 | bytes 3072 | tf_op jit(solution)/shard_map/psum | solution.py:26
  174.6 2.7 multiply_reduce_fusion.32
  177.4 14.1 %psum.117 = f32[4096]{0:T(1024)S(1)} all-reduce(f32[4096]{0:T(1024)S(1)} %constant_dynamic-update-slice_fusion.5), channel_id=1, replica_groups=mesh['z_hi'=4,'y'=4,'core'=2,'x'=4,'z_lo'=4] {'core'}, use_global_device_ids=true, to_apply=%region_60.0 | all-reduce | flops 4096 | bytes 32768 | tf_op jit(solution)/shard_map/psum | solution.py:30
  191.6 11.7 %psum.118 = f32[4096]{0:T(1024)S(1)} all-reduce(f32[4096]{0:T(1024)S(1)} %psum.117), channel_id=1, replica_groups=mesh['z_hi'=4,'y'=4,'core'=2,'x'=4,'z_lo'=4] {'y'}, use_global_device_ids=true, to_apply=%region_61.0 | all-reduce | flops 4096 | bytes 32768 | tf_op jit(solution)/shard_map/psum | solution.py:30
  203.2 18.2 %psum.119 = f32[4096]{0:T(1024)S(1)} all-reduce(f32[4096]{0:T(1024)S(1)} %psum.118), channel_id=1, replica_groups=mesh['z_hi'=4,'y'=4,'core'=2,'x'=4,'z_lo'=4] {'z_hi'}, use_global_device_ids=true, to_apply=%region_62.0 | all-reduce | flops 4096 | bytes 32768 | tf_op jit(solution)/shard_map/psum | solution.py:30
  221.4 0.6 fusion.35
  222.1 1.3 fusion.16
  223.4 1.3 fusion.17
  225.5 1.2 fusion.48
  226.7 15.5 %all_to_all.15 = f32[2,128,4096]{2,1,0:T(8,128)} all-to-all(f32[2,128,4096]{2,1,0:T(8,128)S(1)} %bitcast.19), channel_id=1, replica_groups=mesh['z_hi'=4,'y'=4,'core'=2,'x'=4,'z_lo'=4] {'core'}, dimensions={0} | all-to-all | bytes 8388608 | tf_op jit(solution)/shard_map/all_to_all | solution.py:45
  242.2 2.7 reduce_sum.507
  244.9 29.3 %all_to_all.16 = f32[4,32,4096]{2,1,0:T(8,128)} all-to-all(f32[4,32,4096]{2,1,0:T(8,128)S(1)} %bitcast.20), channel_id=1, replica_groups=mesh['z_hi'=4,'y'=4,'core'=2,'x'=4,'z_lo'=4] {'y'}, dimensions={0} | all-to-all | bytes 4194304 | tf_op jit(solution)/shard_map/all_to_all | solution.py:45
  274.2 1.8 reduce_sum.508
  276.0 33.6 %all_to_all.17 = f32[4,8,4096]{2,1,0:T(8,128)S(1)} all-to-all(f32[4,8,4096]{2,1,0:T(8,128)S(1)} %bitcast.21), channel_id=1, replica_groups=mesh['z_hi'=4,'y'=4,'core'=2,'x'=4,'z_lo'=4] {'z_hi'}, dimensions={0} | all-to-all | bytes 1048576 | tf_op jit(solution)/shard_map/all_to_all | solution.py:45
  309.6 0.7 broadcast_divide_fusion
  (81 shorter events, 1.5 us)
Async XLA Ops:
  0.6 5.8 %copy-start.2 = (bf16[384,256]{1,0:T(8,128)(2,1)S(1)}, bf16[384,256]{1,0:T(8,128)(2,1)}, u32[]{:S(2)}) copy-start(bf16[384,256]{1,0:T(8,128)(2,1)} %param.4) | copy-start | bytes 589828
  0.6 5.8 %copy-start.12 = (s32[384]{0:T(512)S(1)}, s32[384]{0:T(512)}, u32[]{:S(2)}) copy-start(s32[384]{0:T(512)} %param.6) | copy-start | bytes 4612
  15.9 4.4 %copy-start.6 = (f32[384]{0:T(512)S(1)}, f32[384]{0:T(512)}, u32[]{:S(2)}) copy-start(f32[384]{0:T(512)} %get-tuple-element.54) | copy-start | bytes 4612
  15.9 4.4 %copy-start.7 = (f32[384]{0:T(512)S(1)}, f32[384]{0:T(512)}, u32[]{:S(2)}) copy-start(f32[384]{0:T(512)} %get-tuple-element.56) | copy-start | bytes 4612
  15.9 4.4 %copy-start.8 = (f32[384]{0:T(512)S(1)}, f32[384]{0:T(512)}, u32[]{:S(2)}) copy-start(f32[384]{0:T(512)} %get-tuple-element.58) | copy-start | bytes 4612
  15.9 4.4 %copy-start.9 = (f32[384]{0:T(512)S(1)}, f32[384]{0:T(512)}, u32[]{:S(2)}) copy-start(f32[384]{0:T(512)} %get-tuple-element.60) | copy-start | bytes 4612
  15.9 4.4 %copy-start.10 = (f32[384]{0:T(512)S(1)}, f32[384]{0:T(512)}, u32[]{:S(2)}) copy-start(f32[384]{0:T(512)} %get-tuple-element.62) | copy-start | bytes 4612
  15.9 4.4 %copy-start.11 = (f32[384]{0:T(512)S(1)}, f32[384]{0:T(512)}, u32[]{:S(2)}) copy-start(f32[384]{0:T(512)} %get-tuple-element.64) | copy-start | bytes 4612
  40.7 2.8 copy-start.5
  40.7 48.1 %copy-start.3 = (s32[4096]{0:T(1024)S(1)}, s32[4096]{0:T(1024)}, u32[]{:S(2)}) copy-start(s32[4096]{0:T(1024)} %param.7) | copy-start | bytes 49156
  104.9 2.8 copy-start.4
  221.4 3.2 %copy-start.1 = (f32[384,512]{1,0:T(8,128)S(1)}, f32[384,512]{1,0:T(8,128)}, u32[]{:S(2)}) copy-start(f32[384,512]{1,0:T(8,128)} %get-tuple-element.65) | copy-start | bytes 2359300
  221.4 3.4 %copy-start = (f32[384,512]{1,0:T(8,128)S(1)}, f32[384,512]{1,0:T(8,128)}, u32[]{:S(2)}) copy-start(f32[384,512]{1,0:T(8,128)} %get-tuple-element.63) | copy-start | bytes 2359300

commit v3 on v2

--- a/solution.py
+++ b/solution.py
@@ -22,12 +22,20 @@
 LISTS = tuple(name for name, _ in LISTS_AXES)
 
 
+def exchange_sum(value, names):
+    n = lax.axis_size(names)
+    copies = jnp.broadcast_to(value[None], (n,) + value.shape)
+    return jnp.sum(lax.all_to_all(copies, names, 0, 0), axis=0)
+
+
 def point_mass(partial_value):
-    return lax.psum(lax.psum(partial_value, "z_lo"), "x")
+    return exchange_sum(partial_value, LISTS)
 
 
 def list_mass(partial_value):
-    return lax.psum(lax.psum(lax.psum(partial_value, "core"), "y"), "z_hi")
+    for name in ("core", "y", "z_hi"):
+        partial_value = exchange_sum(partial_value, name)
+    return partial_value
 
 
 def scatter_rows(points):

time: 313 us -> 258 us (0.82)
  the two profiles are of different devices: /device:TPU:1 before, /device:TPU:33 now
where the time goes in v3:
time: 258 us; the launch traced here: 257 us
  blocking collectives  158 us (61%)
  other arithmetic  30.7 us (12%)
  waiting for transfers between devices  29.1 us (11%)
  starting transfers between devices  19.1 us (7%)
  matrix products  15.7 us (6%)
  local copies, waits for them, and re-layouts  3.12 us (1%)
    all_to_all x8, blocking collectives, exchange_sum(): return jnp.sum(lax.all_to_all(copies, names, 0, 0), axis=0)  82.7 us
    all_to_all x3, blocking collectives, sum_scatter(): value = jnp.sum(lax.all_to_all(blocks, name, 0, 0), axis=0)  75 us
    all_to_all x4, waiting for transfers between devices, exchange_sum(): return jnp.sum(lax.all_to_all(copies, names, 0, 0), axis=0)  29.1 us
    all_to_all x4, starting transfers between devices, exchange_sum(): return jnp.sum(lax.all_to_all(copies, names, 0, 0), axis=0)  19.1 us
    dot_general x8, matrix products, kernel_tile(): lax.dot_general(points, cent_block, (((1,), (1,)), ((), ())), preferred_e...  14.4 us
    reduce_sum x12, other arithmetic, local(): jnp.sum(tile(index) * col_scale[None, index * BLOCK:(index + 1) * BLOCK],...  9.25 us
    reduce_sum x3, other arithmetic, local(): jnp.sum(tile(index) * row_scale[:, None], axis=0)  8.21 us
  transfers between devices with their start and end apart: 4, of which 4 were waited for; matrix products, arithmetic and copies ran while one was open for 0% of the time, Pallas kernels for 0%

profile of v3, /device:TPU:33, one launch (start us, length us, event | category | flops | bytes accessed | tf_op | source)
XLA Modules:
  0.0 256.6 jit_solution(2158113597618424274)
XLA Ops:
  0.7 1.5 fusion.40
  2.2 1.4 fusion.41
  3.6 1.4 fusion.42
  5.0 1.4 fusion.43
  6.4 2.2 fusion.44
  8.6 2.2 fusion.45
  10.8 2.2 fusion.47
  13.0 2.2 fusion.46
  15.2 0.6 broadcast_in_dim.24
  15.8 7.9 %all-to-all-start = ((f32[16,1,384]{2,1,0:T(1,128)}), f32[16,1,384]{2,1,0:T(1,128)S(1)}, u32[]{:S(2)}, u32[]{:S(2)}) async-start(f32[16,1,384]{2,1,0:T(1,128)} %broadcast_in_dim.24), calls=%async_computation | async-start | bytes 49152 | tf_op jit(solution)/shard_map/all_to_all | solution.py:28
  23.8 5.7 %all-to-all-done = f32[16,1,384]{2,1,0:T(1,128)S(1)} async-done(((f32[16,1,384]{2,1,0:T(1,128)}), f32[16,1,384]{2,1,0:T(1,128)S(1)}, u32[]{:S(2)}, u32[]{:S(2)}) %all-to-all-start) | async-done | bytes 24608 | tf_op jit(solution)/shard_map/all_to_all | solution.py:28
  29.5 2.7 %multiply_reduce_fusion.24 = (f32[512]{0:T(512)S(1)}, f32[512]{0:T(512)S(1)}, f32[512]{0:T(512)S(1)}, f32[512]{0:T(512)S(1)}, f32[512]{0:T(512)S(1)}, /*index=5*/f32[512]{0:T(512)S(1)}, f32[512]{0:T(512)S(1)}, f32[512]{0:T(512)S(1)}) fusion(f32[384,512]{1,0:T(8,128)S(1)} %get-tuple-element.55, f32[384]{0:T(512)S(1)} %broadcast_divide_fusion.3, ...), kind=kLoop, calls=%fused_computation.56 | loop fusion | flops 3141632 | bytes 6309376 | tf_op jit(solution)/shard_map/reduce_sum | solution.py:78
  32.3 5.9 %all_to_all.87 = f32[2,1,4096]{2,1,0:T(1,128)S(1)} all-to-all(f32[2,1,4096]{2,1,0:T(1,128)S(1)} %broadcast_in_dim.25), channel_id=1, replica_groups=mesh['z_hi'=4,'y'=4,'core'=2,'x'=4,'z_lo'=4] {'core'}, dimensions={0} | all-to-all | bytes 65536 | tf_op jit(solution)/shard_map/all_to_all | solution.py:28
  38.3 8.1 %all_to_all.88 = f32[4,1,4096]{2,1,0:T(1,128)S(1)} all-to-all(f32[4,1,4096]{2,1,0:T(1,128)S(1)} %broadcast_in_dim.26), channel_id=1, replica_groups=mesh['z_hi'=4,'y'=4,'core'=2,'x'=4,'z_lo'=4] {'y'}, dimensions={0} | all-to-all | bytes 131072 | tf_op jit(solution)/shard_map/all_to_all | solution.py:28
  46.5 24.6 %all_to_all.89 = f32[4,1,4096]{2,1,0:T(1,128)S(1)} all-to-all(f32[4,1,4096]{2,1,0:T(1,128)S(1)} %broadcast_in_dim.27), channel_id=1, replica_groups=mesh['z_hi'=4,'y'=4,'core'=2,'x'=4,'z_lo'=4] {'z_hi'}, dimensions={0} | all-to-all | bytes 131072 | tf_op jit(solution)/shard_map/all_to_all | solution.py:28
  71.9 1.6 multiply_reduce_fusion.22
  73.4 1.6 multiply_reduce_fusion.20
  76.0 3.6 %all-to-all-start.4 = ((f32[16,1,384]{2,1,0:T(1,128)}), f32[16,1,384]{2,1,0:T(1,128)S(1)}, u32[]{:S(2)}, u32[]{:S(2)}) async-start(f32[16,1,384]{2,1,0:T(1,128)} %broadcast_in_dim.28), calls=%async_computation.4 | async-start | bytes 49152 | tf_op jit(solution)/shard_map/all_to_all | solution.py:28
  79.5 5.7 %all-to-all-done.4 = f32[16,1,384]{2,1,0:T(1,128)S(1)} async-done(((f32[16,1,384]{2,1,0:T(1,128)}), f32[16,1,384]{2,1,0:T(1,128)S(1)}, u32[]{:S(2)}, u32[]{:S(2)}) %all-to-all-start.4) | async-done | bytes 24608 | tf_op jit(solution)/shard_map/all_to_all | solution.py:28
  85.3 2.7 %multiply_reduce_fusion.8 = (f32[512]{0:T(512)S(1)}, f32[512]{0:T(512)S(1)}, f32[512]{0:T(512)S(1)}, f32[512]{0:T(512)S(1)}, f32[512]{0:T(512)S(1)}, /*index=5*/f32[512]{0:T(512)S(1)}, f32[512]{0:T(512)S(1)}, f32[512]{0:T(512)S(1)}) fusion(f32[384,512]{1,0:T(8,128)S(1)} %get-tuple-element.55, f32[384]{0:T(512)S(1)} %broadcast_divide_fusion.2, ...), kind=kLoop, calls=%fused_computation.40 | loop fusion | flops 3141632 | bytes 6309376 | tf_op jit(solution)/shard_map/reduce_sum | solution.py:78
  88.2 7.9 %all_to_all.90 = f32[2,1,4096]{2,1,0:T(1,128)S(1)} all-to-all(f32[2,1,4096]{2,1,0:T(1,128)S(1)} %broadcast_in_dim.29), channel_id=1, replica_groups=mesh['z_hi'=4,'y'=4,'core'=2,'x'=4,'z_lo'=4] {'core'}, dimensions={0} | all-to-all | bytes 65536 | tf_op jit(solution)/shard_map/all_to_all | solution.py:28
  96.1 6.8 %all_to_all.91 = f32[4,1,4096]{2,1,0:T(1,128)S(1)} all-to-all(f32[4,1,4096]{2,1,0:T(1,128)S(1)} %broadcast_in_dim.30), channel_id=1, replica_groups=mesh['z_hi'=4,'y'=4,'core'=2,'x'=4,'z_lo'=4] {'y'}, dimensions={0} | all-to-all | bytes 131072 | tf_op jit(solution)/shard_map/all_to_all | solution.py:28
  103.1 15.1 %all_to_all.92 = f32[4,1,4096]{2,1,0:T(1,128)S(1)} all-to-all(f32[4,1,4096]{2,1,0:T(1,128)S(1)} %broadcast_in_dim.31), channel_id=1, replica_groups=mesh['z_hi'=4,'y'=4,'core'=2,'x'=4,'z_lo'=4] {'z_hi'}, dimensions={0} | all-to-all | bytes 131072 | tf_op jit(solution)/shard_map/all_to_all | solution.py:28
  118.3 1.3 multiply_reduce_fusion.6
  119.6 1.3 multiply_reduce_fusion.7
  120.9 1.3 multiply_reduce_fusion.5
  122.2 1.3 multiply_reduce_fusion.4
  124.1 0.6 broadcast_in_dim.32
  124.7 3.5 %all-to-all-start.8 = ((f32[16,1,384]{2,1,0:T(1,128)}), f32[16,1,384]{2,1,0:T(1,128)S(1)}, u32[]{:S(2)}, u32[]{:S(2)}) async-start(f32[16,1,384]{2,1,0:T(1,128)} %broadcast_in_dim.32), calls=%async_computation.8 | async-start | bytes 49152 | tf_op jit(solution)/shard_map/all_to_all | solution.py:28
  128.2 5.7 %all-to-all-done.8 = f32[16,1,384]{2,1,0:T(1,128)S(1)} async-done(((f32[16,1,384]{2,1,0:T(1,128)}), f32[16,1,384]{2,1,0:T(1,128)S(1)}, u32[]{:S(2)}, u32[]{:S(2)}) %all-to-all-start.8) | async-done | bytes 24608 | tf_op jit(solution)/shard_map/all_to_all | solution.py:28
  134.0 2.7 %multiply_reduce_fusion.32 = (f32[512]{0:T(512)S(1)}, f32[512]{0:T(512)S(1)}, f32[512]{0:T(512)S(1)}, f32[512]{0:T(512)S(1)}, f32[512]{0:T(512)S(1)}, /*index=5*/f32[512]{0:T(512)S(1)}, f32[512]{0:T(512)S(1)}, f32[512]{0:T(512)S(1)}) fusion(f32[384,512]{1,0:T(8,128)S(1)} %get-tuple-element.55, f32[384]{0:T(512)S(1)} %broadcast_divide_fusion.1, ...), kind=kLoop, calls=%fused_computation.64 | loop fusion | flops 3141632 | bytes 6309376 | tf_op jit(solution)/shard_map/reduce_sum | solution.py:78
  136.8 7.5 %all_to_all.93 = f32[2,1,4096]{2,1,0:T(1,128)S(1)} all-to-all(f32[2,1,4096]{2,1,0:T(1,128)S(1)} %broadcast_in_dim.33), channel_id=1, replica_groups=mesh['z_hi'=4,'y'=4,'core'=2,'x'=4,'z_lo'=4] {'core'}, dimensions={0} | all-to-all | bytes 65536 | tf_op jit(solution)/shard_map/all_to_all | solution.py:28
  144.4 6.8 %all_to_all.94 = f32[4,1,4096]{2,1,0:T(1,128)S(1)} all-to-all(f32[4,1,4096]{2,1,0:T(1,128)S(1)} %broadcast_in_dim.34), channel_id=1, replica_groups=mesh['z_hi'=4,'y'=4,'core'=2,'x'=4,'z_lo'=4] {'y'}, dimensions={0} | all-to-all | bytes 131072 | tf_op jit(solution)/shard_map/all_to_all | solution.py:28
  151.3 0.7 broadcast_in_dim.35
  152.0 4.1 %all-to-all-start.11 = ((f32[4,1,4096]{2,1,0:T(1,128)}), f32[4,1,4096]{2,1,0:T(1,128)}, u32[]{:S(2)}, u32[]{:S(2)}) async-start(f32[4,1,4096]{2,1,0:T(1,128)} %broadcast_in_dim.35), calls=%async_computation.11 | async-start | bytes 131072 | tf_op jit(solution)/shard_map/all_to_all | solution.py:28
  156.2 12.0 %all-to-all-done.11 = f32[4,1,4096]{2,1,0:T(1,128)} async-done(((f32[4,1,4096]{2,1,0:T(1,128)}), f32[4,1,4096]{2,1,0:T(1,128)}, u32[]{:S(2)}, u32[]{:S(2)}) %all-to-all-start.11) | async-done | bytes 65568 | tf_op jit(solution)/shard_map/all_to_all | solution.py:28
  168.2 0.9 reduce_sum.626
  169.2 1.4 fusion.35
  170.6 1.3 fusion.16
  171.9 1.3 fusion.17
  173.1 1.3 fusion.18
  175.1 1.3 fusion.48
  176.4 10.9 %all_to_all.95 = f32[2,128,4096]{2,1,0:T(8,128)} all-to-all(f32[2,128,4096]{2,1,0:T(8,128)S(1)} %bitcast.19), channel_id=1, replica_groups=mesh['z_hi'=4,'y'=4,'core'=2,'x'=4,'z_lo'=4] {'core'}, dimensions={0} | all-to-all | bytes 8388608 | tf_op jit(solution)/shard_map/all_to_all | solution.py:53
  187.3 2.7 %reduce_sum.627 = f32[128,4096]{1,0:T(8,128)S(1)} reduce(f32[2,128,4096]{2,1,0:T(8,128)} %all_to_all.95, f32[]{:T(128)} %constant.33.clone.1), dimensions={0}, to_apply=%region_60.0 | reduce | flops 524288 | bytes 6291460 | tf_op jit(solution)/shard_map/reduce_sum | solution.py:53
  189.9 29.3 %all_to_all.96 = f32[4,32,4096]{2,1,0:T(8,128)} all-to-all(f32[4,32,4096]{2,1,0:T(8,128)S(1)} %bitcast.20), channel_id=1, replica_groups=mesh['z_hi'=4,'y'=4,'core'=2,'x'=4,'z_lo'=4] {'y'}, dimensions={0} | all-to-all | bytes 4194304 | tf_op jit(solution)/shard_map/all_to_all | solution.py:53
  219.3 1.8 reduce_sum.628
  221.0 34.8 %all_to_all.97 = f32[4,8,4096]{2,1,0:T(8,128)S(1)} all-to-all(f32[4,8,4096]{2,1,0:T(8,128)S(1)} %bitcast.21), channel_id=1, replica_groups=mesh['z_hi'=4,'y'=4,'core'=2,'x'=4,'z_lo'=4] {'z_hi'}, dimensions={0} | all-to-all | bytes 1048576 | tf_op jit(solution)/shard_map/all_to_all | solution.py:53
  255.9 0.7 broadcast_divide_fusion
  (90 shorter events, 4.2 us)
Async XLA Ops:
  0.6 3.0 %copy-start.1 = (bf16[384,256]{1,0:T(8,128)(2,1)S(1)}, bf16[384,256]{1,0:T(8,128)(2,1)}, u32[]{:S(2)}) copy-start(bf16[384,256]{1,0:T(8,128)(2,1)} %param.4) | copy-start | bytes 589828
  0.6 3.0 %copy-start.4 = (s32[384]{0:T(512)S(1)}, s32[384]{0:T(512)}, u32[]{:S(2)}) copy-start(s32[384]{0:T(512)} %param.6) | copy-start | bytes 4612
  15.8 13.6 %all-to-all-start = ((f32[16,1,384]{2,1,0:T(1,128)}), f32[16,1,384]{2,1,0:T(1,128)S(1)}, u32[]{:S(2)}, u32[]{:S(2)}) async-start(f32[16,1,384]{2,1,0:T(1,128)} %broadcast_in_dim.24), calls=%async_computation | async-start | bytes 49152 | tf_op jit(solution)/shard_map/all_to_all | solution.py:28
  29.5 41.8 %copy-start.2 = (s32[4096]{0:T(1024)S(1)}, s32[4096]{0:T(1024)}, u32[]{:S(2)}) copy-start(s32[4096]{0:T(1024)} %param.7) | copy-start | bytes 49156
  76.0 9.3 %all-to-all-start.4 = ((f32[16,1,384]{2,1,0:T(1,128)}), f32[16,1,384]{2,1,0:T(1,128)S(1)}, u32[]{:S(2)}, u32[]{:S(2)}) async-start(f32[16,1,384]{2,1,0:T(1,128)} %broadcast_in_dim.28), calls=%async_computation.4 | async-start | bytes 49152 | tf_op jit(solution)/shard_map/all_to_all | solution.py:28
  124.7 9.2 %all-to-all-start.8 = ((f32[16,1,384]{2,1,0:T(1,128)}), f32[16,1,384]{2,1,0:T(1,128)S(1)}, u32[]{:S(2)}, u32[]{:S(2)}) async-start(f32[16,1,384]{2,1,0:T(1,128)} %broadcast_in_dim.32), calls=%async_computation.8 | async-start | bytes 49152 | tf_op jit(solution)/shard_map/all_to_all | solution.py:28
  152.0 16.3 %all-to-all-start.11 = ((f32[4,1,4096]{2,1,0:T(1,128)}), f32[4,1,4096]{2,1,0:T(1,128)}, u32[]{:S(2)}, u32[]{:S(2)}) async-start(f32[4,1,4096]{2,1,0:T(1,128)} %broadcast_in_dim.35), calls=%async_computation.11 | async-start | bytes 131072 | tf_op jit(solution)/shard_map/all_to_all | solution.py:28
  169.2 5.2 %copy-start = (f32[384,512]{1,0:T(8,128)S(1)}, f32[384,512]{1,0:T(8,128)}, u32[]{:S(2)}) copy-start(f32[384,512]{1,0:T(8,128)} %get-tuple-element.63) | copy-start | bytes 2359300
  219.3 36.6 %copy-start.3 = (f32[4096]{0:T(1024)S(1)}, f32[4096]{0:T(1024)}, u32[]{:S(2)}) copy-start(f32[4096]{0:T(1024)} %get-tuple-element.28) | copy-start | bytes 49156

commit v4 on v3

--- a/solution.py
+++ b/solution.py
@@ -33,9 +33,7 @@
 
 
 def list_mass(partial_value):
-    for name in ("core", "y", "z_hi"):
-        partial_value = exchange_sum(partial_value, name)
-    return partial_value
+    return exchange_sum(exchange_sum(partial_value, ("y", "core")), "z_hi")
 
 
 def scatter_rows(points):

time: 258 us -> 248 us (0.961)
  the two profiles are of different devices: /device:TPU:33 before, /device:TPU:32 now
where the time goes in v4:
time: 248 us; the launch traced here: 247 us
  blocking collectives  142 us (57%)
  waiting for transfers between devices  33 us (13%)
  other arithmetic  30.6 us (12%)
  starting transfers between devices  21.6 us (9%)
  matrix products  15.7 us (6%)
  local copies, waits for them, and re-layouts  3.17 us (1%)
    all_to_all x3, blocking collectives, sum_scatter(): value = jnp.sum(lax.all_to_all(blocks, name, 0, 0), axis=0)  72.8 us
    all_to_all x5, blocking collectives, exchange_sum(): return jnp.sum(lax.all_to_all(copies, names, 0, 0), axis=0)  68.8 us
    all_to_all x4, waiting for transfers between devices, exchange_sum(): return jnp.sum(lax.all_to_all(copies, names, 0, 0), axis=0)  33 us
    all_to_all x4, starting transfers between devices, exchange_sum(): return jnp.sum(lax.all_to_all(copies, names, 0, 0), axis=0)  21.6 us
    dot_general x8, matrix products, kernel_tile(): lax.dot_general(points, cent_block, (((1,), (1,)), ((), ())), preferred_e...  14.4 us
    reduce_sum x12, other arithmetic, local(): jnp.sum(tile(index) * col_scale[None, index * BLOCK:(index + 1) * BLOCK],...  9.25 us
    reduce_sum x3, other arithmetic, local(): jnp.sum(tile(index) * row_scale[:, None], axis=0)  8.21 us
  transfers between devices with their start and end apart: 4, of which 4 were waited for; matrix products, arithmetic and copies ran while one was open for 0% of the time, Pallas kernels for 0%

profile of v4, /device:TPU:32, one launch (start us, length us, event | category | flops | bytes accessed | tf_op | source)
XLA Modules:
  0.0 247.0 jit_solution(8946267671165785619)
XLA Ops:
  0.7 1.5 fusion.40
  2.2 1.4 fusion.41
  3.6 1.4 fusion.42
  5.0 1.4 fusion.43
  6.4 2.2 fusion.44
  8.6 2.2 fusion.45
  10.8 2.2 fusion.47
  13.0 2.2 fusion.46
  15.2 0.6 broadcast_in_dim.18
  15.8 8.8 %all-to-all-start = ((f32[16,1,384]{2,1,0:T(1,128)}), f32[16,1,384]{2,1,0:T(1,128)S(1)}, u32[]{:S(2)}, u32[]{:S(2)}) async-start(f32[16,1,384]{2,1,0:T(1,128)} %broadcast_in_dim.18), calls=%async_computation | async-start | bytes 49152 | tf_op jit(solution)/shard_map/all_to_all | solution.py:28
  24.6 6.6 %all-to-all-done = f32[16,1,384]{2,1,0:T(1,128)S(1)} async-done(((f32[16,1,384]{2,1,0:T(1,128)}), f32[16,1,384]{2,1,0:T(1,128)S(1)}, u32[]{:S(2)}, u32[]{:S(2)}) %all-to-all-start) | async-done | bytes 24608 | tf_op jit(solution)/shard_map/all_to_all | solution.py:28
  31.2 2.7 %multiply_reduce_fusion.24 = (f32[512]{0:T(512)S(1)}, f32[512]{0:T(512)S(1)}, f32[512]{0:T(512)S(1)}, f32[512]{0:T(512)S(1)}, f32[512]{0:T(512)S(1)}, /*index=5*/f32[512]{0:T(512)S(1)}, f32[512]{0:T(512)S(1)}, f32[512]{0:T(512)S(1)}) fusion(f32[384,512]{1,0:T(8,128)S(1)} %get-tuple-element.55, f32[384]{0:T(512)S(1)} %broadcast_divide_fusion.3, ...), kind=kLoop, calls=%fused_computation.56 | loop fusion | flops 3141632 | bytes 6309376 | tf_op jit(solution)/shard_map/reduce_sum | solution.py:76
  34.2 10.1 %all_to_all.69 = f32[8,1,4096]{2,1,0:T(1,128)S(1)} all-to-all(f32[8,1,4096]{2,1,0:T(1,128)S(1)} %broadcast_in_dim.19), channel_id=1, replica_groups=mesh['z_hi'=4,'y'=4,'core'=2,'x'=4,'z_lo'=4] {'y','core'}, dimensions={0} | all-to-all | bytes 262144 | tf_op jit(solution)/shard_map/all_to_all | solution.py:28
  44.4 25.7 %all_to_all.70 = f32[4,1,4096]{2,1,0:T(1,128)S(1)} all-to-all(f32[4,1,4096]{2,1,0:T(1,128)S(1)} %broadcast_in_dim.20), channel_id=1, replica_groups=mesh['z_hi'=4,'y'=4,'core'=2,'x'=4,'z_lo'=4] {'z_hi'}, dimensions={0} | all-to-all | bytes 131072 | tf_op jit(solution)/shard_map/all_to_all | solution.py:28
  70.2 0.6 convert_multiply_fusion
  70.8 1.6 multiply_reduce_fusion.22
  72.3 1.6 multiply_reduce_fusion.20
  74.1 0.2 multiply_reduce_fusion.16
  74.3 0.6 broadcast_in_dim.21
  74.9 4.4 %all-to-all-start.3 = ((f32[16,1,384]{2,1,0:T(1,128)}), f32[16,1,384]{2,1,0:T(1,128)S(1)}, u32[]{:S(2)}, u32[]{:S(2)}) async-start(f32[16,1,384]{2,1,0:T(1,128)} %broadcast_in_dim.21), calls=%async_computation.3 | async-start | bytes 49152 | tf_op jit(solution)/shard_map/all_to_all | solution.py:28
  79.3 6.5 %all-to-all-done.3 = f32[16,1,384]{2,1,0:T(1,128)S(1)} async-done(((f32[16,1,384]{2,1,0:T(1,128)}), f32[16,1,384]{2,1,0:T(1,128)S(1)}, u32[]{:S(2)}, u32[]{:S(2)}) %all-to-all-start.3) | async-done | bytes 24608 | tf_op jit(solution)/shard_map/all_to_all | solution.py:28
  85.9 2.7 %multiply_reduce_fusion.8 = (f32[512]{0:T(512)S(1)}, f32[512]{0:T(512)S(1)}, f32[512]{0:T(512)S(1)}, f32[512]{0:T(512)S(1)}, f32[512]{0:T(512)S(1)}, /*index=5*/f32[512]{0:T(512)S(1)}, f32[512]{0:T(512)S(1)}, f32[512]{0:T(512)S(1)}) fusion(f32[384,512]{1,0:T(8,128)S(1)} %get-tuple-element.55, f32[384]{0:T(512)S(1)} %broadcast_divide_fusion.2, ...), kind=kLoop, calls=%fused_computation.40 | loop fusion | flops 3141632 | bytes 6309376 | tf_op jit(solution)/shard_map/reduce_sum | solution.py:76
  88.8 8.5 %all_to_all.71 = f32[8,1,4096]{2,1,0:T(1,128)S(1)} all-to-all(f32[8,1,4096]{2,1,0:T(1,128)S(1)} %broadcast_in_dim.22), channel_id=1, replica_groups=mesh['z_hi'=4,'y'=4,'core'=2,'x'=4,'z_lo'=4] {'y','core'}, dimensions={0} | all-to-all | bytes 262144 | tf_op jit(solution)/shard_map/all_to_all | solution.py:28
  97.5 16.0 %all_to_all.72 = f32[4,1,4096]{2,1,0:T(1,128)S(1)} all-to-all(f32[4,1,4096]{2,1,0:T(1,128)S(1)} %broadcast_in_dim.23), channel_id=1, replica_groups=mesh['z_hi'=4,'y'=4,'core'=2,'x'=4,'z_lo'=4] {'z_hi'}, dimensions={0} | all-to-all | bytes 131072 | tf_op jit(solution)/shard_map/all_to_all | solution.py:28
  113.6 1.3 multiply_reduce_fusion.6
  114.9 1.3 multiply_reduce_fusion.7
  116.2 1.3 multiply_reduce_fusion.5
  117.5 1.3 multiply_reduce_fusion.4
  119.4 0.6 broadcast_in_dim.24
  120.0 4.4 %all-to-all-start.6 = ((f32[16,1,384]{2,1,0:T(1,128)}), f32[16,1,384]{2,1,0:T(1,128)S(1)}, u32[]{:S(2)}, u32[]{:S(2)}) async-start(f32[16,1,384]{2,1,0:T(1,128)} %broadcast_in_dim.24), calls=%async_computation.6 | async-start | bytes 49152 | tf_op jit(solution)/shard_map/all_to_all | solution.py:28
  124.4 6.5 %all-to-all-done.6 = f32[16,1,384]{2,1,0:T(1,128)S(1)} async-done(((f32[16,1,384]{2,1,0:T(1,128)}), f32[16,1,384]{2,1,0:T(1,128)S(1)}, u32[]{:S(2)}, u32[]{:S(2)}) %all-to-all-start.6) | async-done | bytes 24608 | tf_op jit(solution)/shard_map/all_to_all | solution.py:28
  131.0 2.7 %multiply_reduce_fusion.32 = (f32[512]{0:T(512)S(1)}, f32[512]{0:T(512)S(1)}, f32[512]{0:T(512)S(1)}, f32[512]{0:T(512)S(1)}, f32[512]{0:T(512)S(1)}, /*index=5*/f32[512]{0:T(512)S(1)}, f32[512]{0:T(512)S(1)}, f32[512]{0:T(512)S(1)}) fusion(f32[384,512]{1,0:T(8,128)S(1)} %get-tuple-element.55, f32[384]{0:T(512)S(1)} %broadcast_divide_fusion.1, ...), kind=kLoop, calls=%fused_computation.64 | loop fusion | flops 3141632 | bytes 6309376 | tf_op jit(solution)/shard_map/reduce_sum | solution.py:76
  133.9 8.5 %all_to_all.73 = f32[8,1,4096]{2,1,0:T(1,128)S(1)} all-to-all(f32[8,1,4096]{2,1,0:T(1,128)S(1)} %broadcast_in_dim.25), channel_id=1, replica_groups=mesh['z_hi'=4,'y'=4,'core'=2,'x'=4,'z_lo'=4] {'y','core'}, dimensions={0} | all-to-all | bytes 262144 | tf_op jit(solution)/shard_map/all_to_all | solution.py:28
  142.5 0.7 broadcast_in_dim.26
  143.2 4.1 %all-to-all-start.8 = ((f32[4,1,4096]{2,1,0:T(1,128)}), f32[4,1,4096]{2,1,0:T(1,128)}, u32[]{:S(2)}, u32[]{:S(2)}) async-start(f32[4,1,4096]{2,1,0:T(1,128)} %broadcast_in_dim.26), calls=%async_computation.8 | async-start | bytes 131072 | tf_op jit(solution)/shard_map/all_to_all | solution.py:28
  147.4 13.4 %all-to-all-done.8 = f32[4,1,4096]{2,1,0:T(1,128)} async-done(((f32[4,1,4096]{2,1,0:T(1,128)}), f32[4,1,4096]{2,1,0:T(1,128)}, u32[]{:S(2)}, u32[]{:S(2)}) %all-to-all-start.8) | async-done | bytes 65568 | tf_op jit(solution)/shard_map/all_to_all | solution.py:28
  160.9 0.9 reduce_sum.596
  161.8 1.4 fusion.35
  163.2 1.3 fusion.16
  164.5 1.3 fusion.17
  165.7 1.3 fusion.18
  167.7 1.3 fusion.48
  169.0 8.2 %all_to_all.74 = f32[2,128,4096]{2,1,0:T(8,128)} all-to-all(f32[2,128,4096]{2,1,0:T(8,128)S(1)} %bitcast.19), channel_id=1, replica_groups=mesh['z_hi'=4,'y'=4,'core'=2,'x'=4,'z_lo'=4] {'core'}, dimensions={0} | all-to-all | bytes 8388608 | tf_op jit(solution)/shard_map/all_to_all | solution.py:51
  177.2 2.7 %reduce_sum.597 = f32[128,4096]{1,0:T(8,128)S(1)} reduce(f32[2,128,4096]{2,1,0:T(8,128)} %all_to_all.74, f32[]{:T(128)} %constant.33.clone.1), dimensions={0}, to_apply=%region_57.0 | reduce | flops 524288 | bytes 6291460 | tf_op jit(solution)/shard_map/reduce_sum | solution.py:51
  179.9 30.1 %all_to_all.75 = f32[4,32,4096]{2,1,0:T(8,128)} all-to-all(f32[4,32,4096]{2,1,0:T(8,128)S(1)} %bitcast.20), channel_id=1, replica_groups=mesh['z_hi'=4,'y'=4,'core'=2,'x'=4,'z_lo'=4] {'y'}, dimensions={0} | all-to-all | bytes 4194304 | tf_op jit(solution)/shard_map/all_to_all | solution.py:51
  210.0 1.8 reduce_sum.598
  211.8 34.5 %all_to_all.76 = f32[4,8,4096]{2,1,0:T(8,128)S(1)} all-to-all(f32[4,8,4096]{2,1,0:T(8,128)S(1)} %bitcast.21), channel_id=1, replica_groups=mesh['z_hi'=4,'y'=4,'core'=2,'x'=4,'z_lo'=4] {'z_hi'}, dimensions={0} | all-to-all | bytes 1048576 | tf_op jit(solution)/shard_map/all_to_all | solution.py:51
  246.3 0.7 broadcast_divide_fusion
  (81 shorter events, 2.8 us)
Async XLA Ops:
  0.6 3.0 %copy-start.1 = (bf16[384,256]{1,0:T(8,128)(2,1)S(1)}, bf16[384,256]{1,0:T(8,128)(2,1)}, u32[]{:S(2)}) copy-start(bf16[384,256]{1,0:T(8,128)(2,1)} %param.4) | copy-start | bytes 589828
  0.6 3.0 %copy-start.4 = (s32[384]{0:T(512)S(1)}, s32[384]{0:T(512)}, u32[]{:S(2)}) copy-start(s32[384]{0:T(512)} %param.6) | copy-start | bytes 4612
  15.8 15.4 %all-to-all-start = ((f32[16,1,384]{2,1,0:T(1,128)}), f32[16,1,384]{2,1,0:T(1,128)S(1)}, u32[]{:S(2)}, u32[]{:S(2)}) async-start(f32[16,1,384]{2,1,0:T(1,128)} %broadcast_in_dim.18), calls=%async_computation | async-start | bytes 49152 | tf_op jit(solution)/shard_map/all_to_all | solution.py:28
  31.2 38.9 %copy-start.2 = (s32[4096]{0:T(1024)S(1)}, s32[4096]{0:T(1024)}, u32[]{:S(2)}) copy-start(s32[4096]{0:T(1024)} %param.7) | copy-start | bytes 49156
  74.9 10.9 %all-to-all-start.3 = ((f32[16,1,384]{2,1,0:T(1,128)}), f32[16,1,384]{2,1,0:T(1,128)S(1)}, u32[]{:S(2)}, u32[]{:S(2)}) async-start(f32[16,1,384]{2,1,0:T(1,128)} %broadcast_in_dim.21), calls=%async_computation.3 | async-start | bytes 49152 | tf_op jit(solution)/shard_map/all_to_all | solution.py:28
  120.0 10.9 %all-to-all-start.6 = ((f32[16,1,384]{2,1,0:T(1,128)}), f32[16,1,384]{2,1,0:T(1,128)S(1)}, u32[]{:S(2)}, u32[]{:S(2)}) async-start(f32[16,1,384]{2,1,0:T(1,128)} %broadcast_in_dim.24), calls=%async_computation.6 | async-start | bytes 49152 | tf_op jit(solution)/shard_map/all_to_all | solution.py:28
  143.2 17.7 %all-to-all-start.8 = ((f32[4,1,4096]{2,1,0:T(1,128)}), f32[4,1,4096]{2,1,0:T(1,128)}, u32[]{:S(2)}, u32[]{:S(2)}) async-start(f32[4,1,4096]{2,1,0:T(1,128)} %broadcast_in_dim.26), calls=%async_computation.8 | async-start | bytes 131072 | tf_op jit(solution)/shard_map/all_to_all | solution.py:28
  161.8 5.2 %copy-start = (f32[384,512]{1,0:T(8,128)S(1)}, f32[384,512]{1,0:T(8,128)}, u32[]{:S(2)}) copy-start(f32[384,512]{1,0:T(8,128)} %get-tuple-element.63) | copy-start | bytes 2359300
  210.0 36.3 %copy-start.3 = (f32[4096]{0:T(1024)S(1)}, f32[4096]{0:T(1024)}, u32[]{:S(2)}) copy-start(f32[4096]{0:T(1024)} %get-tuple-element.28) | copy-start | bytes 49156

commit v5 on v4

--- a/solution.py
+++ b/solution.py
@@ -4,7 +4,6 @@
 from jax.sharding import Mesh, PartitionSpec as P
 
 ITERS = 3
-BLOCK = 512
 
 
 def kernel_tile(points, cent_block, prior, start):
@@ -54,38 +53,19 @@
 
 def local(points, centroids, prior, loads):
     n_lists = centroids.shape[0]
-    count = n_lists // BLOCK
     offset = (lax.axis_index("x") * lax.axis_size("z_lo") + lax.axis_index("z_lo")) * n_lists
     total_pts = points.shape[0] * lax.axis_size(PTS)
     total_lists = n_lists * lax.axis_size(LISTS)
     target = loads.astype(jnp.float32) * (total_pts / (8.0 * total_lists))
 
-    def tile(index):
-        block = centroids[index * BLOCK : (index + 1) * BLOCK]
-        return kernel_tile(points, block, prior, offset + index * BLOCK)
+    kernel = kernel_tile(points, centroids, prior, offset)
 
     col_scale = jnp.ones((n_lists,), jnp.float32)
     row_scale = jnp.ones((points.shape[0],), jnp.float32)
     for step in range(ITERS):
-        partial_value = jnp.zeros((points.shape[0],), jnp.float32)
-        for index in range(count):
-            partial_value = partial_value + jnp.sum(
-                tile(index) * col_scale[None, index * BLOCK : (index + 1) * BLOCK], axis=1
-            )
-        row_scale = 1.0 / point_mass(partial_value)
-        pieces = [jnp.sum(tile(index) * row_scale[:, None], axis=0) for index in range(count)]
-        col_scale = target / list_mass(jnp.concatenate(pieces))
-    plan = jnp.concatenate(
-        [
-            (
-                tile(index)
-                * row_scale[:, None]
-                * col_scale[None, index * BLOCK : (index + 1) * BLOCK]
-            ).astype(jnp.bfloat16)
-            for index in range(count)
-        ],
-        axis=1,
-    )
+        row_scale = 1.0 / point_mass(jnp.sum(kernel * col_scale[None, :], axis=1))
+        col_scale = target / list_mass(jnp.sum(kernel * row_scale[:, None], axis=0))
+    plan = (kernel * row_scale[:, None] * col_scale[None, :]).astype(jnp.bfloat16)
     sums = sum_scatter(
         lax.dot_general(scatter_rows(points), plan, (((0,), (0,)), ((), ())), preferred_element_type=jnp.float32)
     )

time: 248 us -> 236 us (0.952)
  blocking collectives: 142 us -> 180 us
  waiting for transfers between devices: 33 us -> 13.4 us
  starting transfers between devices: 21.6 us -> 3.28 us
  matrix products: 15.7 us -> 9.5 us
  other arithmetic: 30.6 us -> 25.4 us
    all_to_all x5 -> x8, blocking collectives: 68.8 us -> 105 us  [exchange_sum(): return jnp.sum(lax.all_to_all(copies, names, 0, 0), axis=0)]
    all_to_all x4 -> x1, waiting for transfers between devices: 33 us -> 13.4 us  [exchange_sum(): return jnp.sum(lax.all_to_all(copies, names, 0, 0), axis=0)]
    all_to_all x4 -> x1, starting transfers between devices: 21.6 us -> 3.28 us  [exchange_sum(): return jnp.sum(lax.all_to_all(copies, names, 0, 0), axis=0)]
    dot_general x8 -> x1, matrix products: 14.4 us -> 5.34 us  [kernel_tile(): lax.dot_general(points, cent_block, (((1,), (1,)), ((), ())), preferred_e...]
    unnamed x10 -> x0, other arithmetic: 4.33 us -> none
    dot_general x1, matrix products: 1.27 us -> 4.16 us  [local(): lax.dot_general(scatter_rows(points), plan, (((0,), (0,)), ((), ())), pre...]
    reduce_sum x15 -> x5, other arithmetic: 17.5 us -> 17.6 us  [the longest x3 10.9 us: local(): col_scale = target / list_mass(jnp.sum(kernel * row_scale[:, None], axis=0))]
  transfers between devices with their start and end apart: 4 -> 1, of which waited for: 4 -> 1; matrix products, arithmetic and copies ran while one was open for 0% -> 0% of each run, Pallas kernels for 0% -> 0%
where the time goes in v5:
time: 236 us; the launch traced here: 235 us
  blocking collectives  180 us (76%)
  other arithmetic  25.4 us (11%)
  waiting for transfers between devices  13.4 us (6%)
  matrix products  9.5 us (4%)
  starting transfers between devices  3.28 us (1%)
  local copies, waits for them, and re-layouts  2.76 us (1%)
    all_to_all x8, blocking collectives, exchange_sum(): return jnp.sum(lax.all_to_all(copies, names, 0, 0), axis=0)  105 us
    all_to_all x3, blocking collectives, sum_scatter(): value = jnp.sum(lax.all_to_all(blocks, name, 0, 0), axis=0)  74.1 us
    all_to_all x1, waiting for transfers between devices, exchange_sum(): return jnp.sum(lax.all_to_all(copies, names, 0, 0), axis=0)  13.4 us
    reduce_sum x3, other arithmetic, local(): col_scale = target / list_mass(jnp.sum(kernel * row_scale[:, None], axis=0))  10.9 us
    reduce_sum x2, other arithmetic, local(): row_scale = 1.0 / point_mass(jnp.sum(kernel * col_scale[None, :], axis=1))  6.67 us
    reduce_sum x3, other arithmetic, sum_scatter(): value = jnp.sum(lax.all_to_all(blocks, name, 0, 0), axis=0)  5.8 us
    dot_general x1, matrix products, kernel_tile(): lax.dot_general(points, cent_block, (((1,), (1,)), ((), ())), preferred_e...  5.34 us
  transfers between devices with their start and end apart: 1, of which 1 were waited for; matrix products, arithmetic and copies ran while one was open for 0% of the time, Pallas kernels for 0%

profile of v5, /device:TPU:32, one launch (start us, length us, event | category | flops | bytes accessed | tf_op | source)
XLA Modules:
  0.0 234.7 jit_solution(16301738450914762959)
XLA Ops:
  0.6 0.0 copy-start
  0.7 1.6 copy-done
  2.2 5.3 %fusion.8 = (f32[384]{0:T(512)S(1)}, f32[384,4096]{1,0:T(8,128)}) fusion(s32[4096]{0:T(1024)S(1)} %iota_add_fusion, s32[384]{0:T(512)} %param.6, bf16[384,256]{1,0:T(8,128)(2,1)} %param.4, bf16[4096,256]{1,0:T(8,128)(2,1)S(1)} %copy-done), kind=kOutput, calls=%fused_computation.20 | convolution fusion | flops 813170304 | bytes 8604672 | tf_op jit(solution)/shard_map/dot_general | solution.py:10
  7.6 0.0 copy-start.2
  7.6 14.8 %all_to_all.69 = f32[16,1,384]{2,1,0:T(1,128)S(1)} all-to-all(f32[16,1,384]{2,1,0:T(1,128)S(1)} %broadcast_in_dim.18), channel_id=1, replica_groups=mesh['z_hi'=4,'y'=4,'core'=2,'x'=4,'z_lo'=4] {'x','z_lo'}, dimensions={0} | all-to-all | bytes 49152 | tf_op jit(solution)/shard_map/all_to_all | solution.py:27
  22.4 3.6 %multiply_reduce_fusion.3 = f32[4096]{0:T(1024)S(1)} fusion(f32[384,4096]{1,0:T(8,128)} %get-tuple-element.7, f32[384]{0:T(512)S(1)} %broadcast_divide_fusion.3), kind=kLoop, calls=%fused_computation.4 | loop fusion | flops 3141632 | bytes 6309376 | tf_op jit(solution)/shard_map/reduce_sum | solution.py:67
  26.1 0.1 broadcast_in_dim.19
  26.2 10.4 %all_to_all.70 = f32[8,1,4096]{2,1,0:T(1,128)S(1)} all-to-all(f32[8,1,4096]{2,1,0:T(1,128)S(1)} %broadcast_in_dim.19), channel_id=1, replica_groups=mesh['z_hi'=4,'y'=4,'core'=2,'x'=4,'z_lo'=4] {'y','core'}, dimensions={0} | all-to-all | bytes 262144 | tf_op jit(solution)/shard_map/all_to_all | solution.py:27
  36.6 0.1 reduce_sum.165
  36.7 25.7 %all_to_all.71 = f32[4,1,4096]{2,1,0:T(1,128)S(1)} all-to-all(f32[4,1,4096]{2,1,0:T(1,128)S(1)} %broadcast_in_dim.20), channel_id=1, replica_groups=mesh['z_hi'=4,'y'=4,'core'=2,'x'=4,'z_lo'=4] {'z_hi'}, dimensions={0} | all-to-all | bytes 131072 | tf_op jit(solution)/shard_map/all_to_all | solution.py:27
  62.4 0.1 reduce_sum.166
  62.5 0.0 copy-done.2
  62.5 3.3 %multiply_reduce_fusion.2 = f32[384]{0:T(512)S(1)} fusion(f32[384,4096]{1,0:T(8,128)} %get-tuple-element.7, f32[4096]{0:T(1024)S(1)} %get-tuple-element.5), kind=kLoop, calls=%fused_computation.3 | loop fusion | flops 3145344 | bytes 6309376 | tf_op jit(solution)/shard_map/reduce_sum | solution.py:66
  65.9 10.7 %all_to_all.72 = f32[16,1,384]{2,1,0:T(1,128)S(1)} all-to-all(f32[16,1,384]{2,1,0:T(1,128)S(1)} %broadcast_in_dim.21), channel_id=1, replica_groups=mesh['z_hi'=4,'y'=4,'core'=2,'x'=4,'z_lo'=4] {'x','z_lo'}, dimensions={0} | all-to-all | bytes 49152 | tf_op jit(solution)/shard_map/all_to_all | solution.py:27
  76.7 3.6 %multiply_reduce_fusion.1 = f32[4096]{0:T(1024)S(1)} fusion(f32[384,4096]{1,0:T(8,128)} %get-tuple-element.7, f32[384]{0:T(512)S(1)} %broadcast_divide_fusion.2), kind=kLoop, calls=%fused_computation.2 | loop fusion | flops 3141632 | bytes 6309376 | tf_op jit(solution)/shard_map/reduce_sum | solution.py:67
  80.3 0.1 broadcast_in_dim.22
  80.4 8.5 %all_to_all.73 = f32[8,1,4096]{2,1,0:T(1,128)S(1)} all-to-all(f32[8,1,4096]{2,1,0:T(1,128)S(1)} %broadcast_in_dim.22), channel_id=1, replica_groups=mesh['z_hi'=4,'y'=4,'core'=2,'x'=4,'z_lo'=4] {'y','core'}, dimensions={0} | all-to-all | bytes 262144 | tf_op jit(solution)/shard_map/all_to_all | solution.py:27
  88.9 0.1 reduce_sum.170
  89.1 16.0 %all_to_all.74 = f32[4,1,4096]{2,1,0:T(1,128)S(1)} all-to-all(f32[4,1,4096]{2,1,0:T(1,128)S(1)} %broadcast_in_dim.23), channel_id=1, replica_groups=mesh['z_hi'=4,'y'=4,'core'=2,'x'=4,'z_lo'=4] {'z_hi'}, dimensions={0} | all-to-all | bytes 131072 | tf_op jit(solution)/shard_map/all_to_all | solution.py:27
  105.1 0.1 reduce_sum.171
  105.2 0.0 copy-start.1
  105.2 3.3 %multiply_reduce_fusion = f32[384]{0:T(512)S(1)} fusion(f32[384,4096]{1,0:T(8,128)} %get-tuple-element.7, f32[4096]{0:T(1024)S(1)} %fusion.4), kind=kLoop, calls=%fused_computation.1 | loop fusion | flops 3145344 | bytes 6309376 | tf_op jit(solution)/shard_map/reduce_sum | solution.py:66
  108.5 10.7 %all_to_all.75 = f32[16,1,384]{2,1,0:T(1,128)S(1)} all-to-all(f32[16,1,384]{2,1,0:T(1,128)S(1)} %broadcast_in_dim.24), channel_id=1, replica_groups=mesh['z_hi'=4,'y'=4,'core'=2,'x'=4,'z_lo'=4] {'x','z_lo'}, dimensions={0} | all-to-all | bytes 49152 | tf_op jit(solution)/shard_map/all_to_all | solution.py:27
  119.3 3.6 %multiply_reduce_fusion.4 = f32[4096]{0:T(1024)S(1)} fusion(f32[384,4096]{1,0:T(8,128)} %get-tuple-element.7, f32[384]{0:T(512)S(1)} %broadcast_divide_fusion.1), kind=kLoop, calls=%fused_computation.6 | loop fusion | flops 3141632 | bytes 6309376 | tf_op jit(solution)/shard_map/reduce_sum | solution.py:67
  122.9 0.1 broadcast_in_dim.25
  123.0 8.5 %all_to_all.76 = f32[8,1,4096]{2,1,0:T(1,128)S(1)} all-to-all(f32[8,1,4096]{2,1,0:T(1,128)S(1)} %broadcast_in_dim.25), channel_id=1, replica_groups=mesh['z_hi'=4,'y'=4,'core'=2,'x'=4,'z_lo'=4] {'y','core'}, dimensions={0} | all-to-all | bytes 262144 | tf_op jit(solution)/shard_map/all_to_all | solution.py:27
  131.5 0.1 reduce_sum.175
  131.6 0.7 broadcast_in_dim.26
  132.3 3.3 %all-to-all-start.8 = ((f32[4,1,4096]{2,1,0:T(1,128)}), f32[4,1,4096]{2,1,0:T(1,128)S(1)}, u32[]{:S(2)}, u32[]{:S(2)}) async-start(f32[4,1,4096]{2,1,0:T(1,128)} %broadcast_in_dim.26), calls=%async_computation.8 | async-start | bytes 131072 | tf_op jit(solution)/shard_map/all_to_all | solution.py:27
  135.6 0.0 copy-done.1
  135.6 0.2 copy.19
  135.8 13.4 %all-to-all-done.8 = f32[4,1,4096]{2,1,0:T(1,128)S(1)} async-done(((f32[4,1,4096]{2,1,0:T(1,128)}), f32[4,1,4096]{2,1,0:T(1,128)S(1)}, u32[]{:S(2)}, u32[]{:S(2)}) %all-to-all-start.8) | async-done | bytes 65568 | tf_op jit(solution)/shard_map/all_to_all | solution.py:27
  149.2 0.1 reduce_sum.176
  149.3 0.6 fusion.6
  149.9 4.2 %fusion = f32[4096,256]{0,1:T(8,128)S(1)} fusion(bf16[384,256]{0,1:T(8,128)(2,1)S(1)} %bitcast.16, f32[384,4096]{1,0:T(8,128)} %get-tuple-element.7, f32[4096]{0:T(1024)S(1)} %get-tuple-element.3, f32[384]{0:T(512)S(1)} %broadcast_divide_fusion.1), kind=kOutput, calls=%fused_computation.7 | convolution fusion | flops 810024960 | bytes 10700288 | tf_op jit(solution)/shard_map/dot_general | solution.py:70
  154.1 8.2 %all_to_all.77 = f32[2,128,4096]{2,1,0:T(8,128)} all-to-all(f32[2,128,4096]{2,1,0:T(8,128)S(1)} %bitcast.12), channel_id=1, replica_groups=mesh['z_hi'=4,'y'=4,'core'=2,'x'=4,'z_lo'=4] {'core'}, dimensions={0} | all-to-all | bytes 8388608 | tf_op jit(solution)/shard_map/all_to_all | solution.py:50
  162.3 4.0 %reduce_sum.177 = f32[128,4096]{1,0:T(8,128)} reduce(f32[2,128,4096]{2,1,0:T(8,128)} %all_to_all.77, f32[]{:T(128)} %constant.19.clone.1), dimensions={0}, to_apply=%region_15.0 | reduce | flops 524288 | bytes 6291460 | tf_op jit(solution)/shard_map/reduce_sum | solution.py:50
  166.3 31.4 %all_to_all.78 = f32[4,32,4096]{2,1,0:T(8,128)} all-to-all(f32[4,32,4096]{2,1,0:T(8,128)} %bitcast.13), channel_id=1, replica_groups=mesh['z_hi'=4,'y'=4,'core'=2,'x'=4,'z_lo'=4] {'y'}, dimensions={0} | all-to-all | bytes 4194304 | tf_op jit(solution)/shard_map/all_to_all | solution.py:50
  197.6 1.8 reduce_sum.178
  199.4 34.6 %all_to_all.79 = f32[4,8,4096]{2,1,0:T(8,128)S(1)} all-to-all(f32[4,8,4096]{2,1,0:T(8,128)S(1)} %bitcast.14), channel_id=1, replica_groups=mesh['z_hi'=4,'y'=4,'core'=2,'x'=4,'z_lo'=4] {'z_hi'}, dimensions={0} | all-to-all | bytes 1048576 | tf_op jit(solution)/shard_map/all_to_all | solution.py:50
  234.0 0.7 broadcast_divide_fusion
  (16 shorter events, 0.3 us)
Async XLA Ops:
  0.6 1.6 copy-start
  7.6 54.9 %copy-start.2 = (s32[4096]{0:T(1024)S(1)}, s32[4096]{0:T(1024)}, u32[]{:S(2)}) copy-start(s32[4096]{0:T(1024)} %param.7) | copy-start | bytes 49156
  105.2 30.4 %copy-start.1 = (bf16[384,256]{1,0:T(8,128)(2,1)S(1)}, bf16[384,256]{1,0:T(8,128)(2,1)}, u32[]{:S(2)}) copy-start(bf16[384,256]{1,0:T(8,128)(2,1)} %param.4) | copy-start | bytes 589828
  132.3 16.9 %all-to-all-start.8 = ((f32[4,1,4096]{2,1,0:T(1,128)}), f32[4,1,4096]{2,1,0:T(1,128)S(1)}, u32[]{:S(2)}, u32[]{:S(2)}) async-start(f32[4,1,4096]{2,1,0:T(1,128)} %broadcast_in_dim.26), calls=%async_computation.8 | async-start | bytes 131072 | tf_op jit(solution)/shard_map/all_to_all | solution.py:27

commit v6 on v5

--- a/solution.py
+++ b/solution.py
@@ -61,15 +61,32 @@
     kernel = kernel_tile(points, centroids, prior, offset)
 
     col_scale = jnp.ones((n_lists,), jnp.float32)
-    row_scale = jnp.ones((points.shape[0],), jnp.float32)
-    for step in range(ITERS):
+    for step in range(ITERS - 1):
         row_scale = 1.0 / point_mass(jnp.sum(kernel * col_scale[None, :], axis=1))
         col_scale = target / list_mass(jnp.sum(kernel * row_scale[:, None], axis=0))
-    plan = (kernel * row_scale[:, None] * col_scale[None, :]).astype(jnp.bfloat16)
-    sums = sum_scatter(
-        lax.dot_general(scatter_rows(points), plan, (((0,), (0,)), ((), ())), preferred_element_type=jnp.float32)
+    row_scale = 1.0 / point_mass(jnp.sum(kernel * col_scale[None, :], axis=1))
+    col_part = jnp.sum(kernel * row_scale[:, None], axis=0)
+
+    weighted = scatter_rows(points).astype(jnp.float32) * row_scale[:, None]
+    sums = lax.dot_general(
+        weighted,
+        kernel,
+        (((0,), (0,)), ((), ())),
+        precision=lax.Precision.HIGHEST,
+        preferred_element_type=jnp.float32,
     )
-    return (sums / target[None, :], jnp.log(col_scale))
+    blocks = lax.axis_size(PTS)
+    rows = sums.shape[0] // blocks
+    packed = jnp.concatenate(
+        [
+            sums.reshape(blocks, rows, n_lists),
+            jnp.broadcast_to(col_part[None, None, :], (blocks, 1, n_lists)),
+        ],
+        axis=1,
+    ).reshape(blocks * (rows + 1), n_lists)
+    reduced = sum_scatter(packed)
+    col_total = reduced[rows]
+    return (reduced[:rows] / col_total[None, :], jnp.log(target / col_total))
 
 
 def solution(mesh):

time: 236 us -> 264 us (1.12)
  the two profiles are of different devices: /device:TPU:32 before, /device:TPU:1 now
where the time goes in v6:
time: 264 us; the launch traced here: 263 us
  blocking collectives  179 us (68%)
  other arithmetic  30 us (11%)
  waiting for transfers between devices  18.2 us (7%)
  matrix products  14.4 us (5%)
  local copies, waits for them, and re-layouts  13.8 us (5%)
  starting transfers between devices  6.78 us (3%)
    all_to_all x3, blocking collectives, sum_scatter(): value = jnp.sum(lax.all_to_all(blocks, name, 0, 0), axis=0)  107 us
    all_to_all x5, blocking collectives, exchange_sum(): return jnp.sum(lax.all_to_all(copies, names, 0, 0), axis=0)  72.2 us
    all_to_all x2, waiting for transfers between devices, exchange_sum(): return jnp.sum(lax.all_to_all(copies, names, 0, 0), axis=0)  18.2 us
    dot_general x1, matrix products, local(): lax.dot_general(weighted, kernel, (((0,), (0,)), ((), ())), precision=lax...  9.03 us
    reduce_sum x2, other arithmetic, local(): col_scale = target / list_mass(jnp.sum(kernel * row_scale[:, None], axis=0))  7.28 us
    all_to_all x2, starting transfers between devices, exchange_sum(): return jnp.sum(lax.all_to_all(copies, names, 0, 0), axis=0)  6.78 us
    reduce_sum x2, other arithmetic, local(): row_scale = 1.0 / point_mass(jnp.sum(kernel * col_scale[None, :], axis=1))  6.62 us
    reduce_sum x3, other arithmetic, sum_scatter(): value = jnp.sum(lax.all_to_all(blocks, name, 0, 0), axis=0)  6.37 us
  transfers between devices with their start and end apart: 2, of which 2 were waited for; matrix products, arithmetic and copies ran while one was open for 0% of the time, Pallas kernels for 0%

profile of v6, /device:TPU:1, one launch (start us, length us, event | category | flops | bytes accessed | tf_op | source)
XLA Modules:
  0.0 262.9 jit_solution(4650149780749702654)
XLA Ops:
  0.6 0.0 copy-start
  0.7 1.6 copy-done
  2.2 5.3 %fusion.5 = (f32[384]{0:T(512)S(1)}, f32[384,4096]{1,0:T(8,128)}) fusion(s32[4096]{0:T(1024)S(1)} %iota_add_fusion, s32[384]{0:T(512)} %param.6, bf16[384,256]{1,0:T(8,128)(2,1)} %param.4, bf16[4096,256]{1,0:T(8,128)(2,1)S(1)} %copy-done), kind=kOutput, calls=%fused_computation.21 | convolution fusion | flops 813170304 | bytes 8604672 | tf_op jit(solution)/shard_map/dot_general | solution.py:10
  7.6 0.0 copy-start.2
  7.6 15.6 %all_to_all.57 = f32[16,1,384]{2,1,0:T(1,128)S(1)} all-to-all(f32[16,1,384]{2,1,0:T(1,128)S(1)} %broadcast_in_dim.16), channel_id=1, replica_groups=mesh['z_hi'=4,'y'=4,'core'=2,'x'=4,'z_lo'=4] {'x','z_lo'}, dimensions={0} | all-to-all | bytes 49152 | tf_op jit(solution)/shard_map/all_to_all | solution.py:27
  23.3 3.6 %multiply_reduce_fusion.4 = f32[4096]{0:T(1024)S(1)} fusion(f32[384,4096]{1,0:T(8,128)} %get-tuple-element.3, f32[384]{0:T(512)S(1)} %broadcast_divide_fusion.2), kind=kLoop, calls=%fused_computation.7 | loop fusion | flops 3141632 | bytes 6309376 | tf_op jit(solution)/shard_map/reduce_sum | solution.py:66
  26.9 0.1 broadcast_in_dim.17
  27.0 11.7 %all_to_all.58 = f32[8,1,4096]{2,1,0:T(1,128)S(1)} all-to-all(f32[8,1,4096]{2,1,0:T(1,128)S(1)} %broadcast_in_dim.17), channel_id=1, replica_groups=mesh['z_hi'=4,'y'=4,'core'=2,'x'=4,'z_lo'=4] {'y','core'}, dimensions={0} | all-to-all | bytes 262144 | tf_op jit(solution)/shard_map/all_to_all | solution.py:27
  38.6 0.1 reduce_sum.147
  38.8 24.2 %all_to_all.59 = f32[4,1,4096]{2,1,0:T(1,128)S(1)} all-to-all(f32[4,1,4096]{2,1,0:T(1,128)S(1)} %broadcast_in_dim.18), channel_id=1, replica_groups=mesh['z_hi'=4,'y'=4,'core'=2,'x'=4,'z_lo'=4] {'z_hi'}, dimensions={0} | all-to-all | bytes 131072 | tf_op jit(solution)/shard_map/all_to_all | solution.py:27
  63.0 0.1 reduce_sum.148
  63.1 0.0 copy-done.2
  63.1 0.0 copy-start.1
  63.1 3.3 %multiply_reduce_fusion.3 = f32[384]{0:T(512)S(1)} fusion(f32[384,4096]{1,0:T(8,128)} %get-tuple-element.3, f32[4096]{0:T(1024)S(1)} %fusion.4), kind=kLoop, calls=%fused_computation.6 | loop fusion | flops 3145344 | bytes 6309376 | tf_op jit(solution)/shard_map/reduce_sum | solution.py:65
  66.5 9.4 %all_to_all.60 = f32[16,1,384]{2,1,0:T(1,128)S(1)} all-to-all(f32[16,1,384]{2,1,0:T(1,128)S(1)} %broadcast_in_dim.19), channel_id=1, replica_groups=mesh['z_hi'=4,'y'=4,'core'=2,'x'=4,'z_lo'=4] {'x','z_lo'}, dimensions={0} | all-to-all | bytes 49152 | tf_op jit(solution)/shard_map/all_to_all | solution.py:27
  75.9 3.6 %multiply_reduce_fusion.2 = f32[4096]{0:T(1024)S(1)} fusion(f32[384,4096]{1,0:T(8,128)} %get-tuple-element.3, f32[384]{0:T(512)S(1)} %broadcast_divide_fusion.1), kind=kLoop, calls=%fused_computation.5 | loop fusion | flops 3141632 | bytes 6309376 | tf_op jit(solution)/shard_map/reduce_sum | solution.py:66
  79.5 0.1 broadcast_in_dim.20
  79.6 11.4 %all_to_all.61 = f32[8,1,4096]{2,1,0:T(1,128)S(1)} all-to-all(f32[8,1,4096]{2,1,0:T(1,128)S(1)} %broadcast_in_dim.20), channel_id=1, replica_groups=mesh['z_hi'=4,'y'=4,'core'=2,'x'=4,'z_lo'=4] {'y','core'}, dimensions={0} | all-to-all | bytes 262144 | tf_op jit(solution)/shard_map/all_to_all | solution.py:27
  91.0 0.1 reduce_sum.152
  91.1 0.7 broadcast_in_dim.21
  91.7 3.3 %all-to-all-start.5 = ((f32[4,1,4096]{2,1,0:T(1,128)}), f32[4,1,4096]{2,1,0:T(1,128)S(1)}, u32[]{:S(2)}, u32[]{:S(2)}) async-start(f32[4,1,4096]{2,1,0:T(1,128)} %broadcast_in_dim.21), calls=%async_computation.5 | async-start | bytes 131072 | tf_op jit(solution)/shard_map/all_to_all | solution.py:27
  95.0 0.0 copy-done.1
  95.0 0.2 copy.10
  95.2 11.5 %all-to-all-done.5 = f32[4,1,4096]{2,1,0:T(1,128)S(1)} async-done(((f32[4,1,4096]{2,1,0:T(1,128)}), f32[4,1,4096]{2,1,0:T(1,128)S(1)}, u32[]{:S(2)}, u32[]{:S(2)}) %all-to-all-start.5) | async-done | bytes 65568 | tf_op jit(solution)/shard_map/all_to_all | solution.py:27
  106.7 0.1 reduce_sum.153
  106.8 3.3 %multiply_reduce_fusion.1 = f32[384]{0:T(512)S(1)} fusion(f32[384,4096]{1,0:T(8,128)} %get-tuple-element.3, f32[4096]{0:T(1024)S(1)} %fusion.3), kind=kLoop, calls=%fused_computation.4 | loop fusion | flops 3145344 | bytes 6309376 | tf_op jit(solution)/shard_map/reduce_sum | solution.py:67
  110.1 0.6 broadcast_in_dim.22
  110.7 3.5 %all-to-all-start.6 = ((f32[16,1,384]{2,1,0:T(1,128)}), f32[16,1,384]{2,1,0:T(1,128)S(1)}, u32[]{:S(2)}, u32[]{:S(2)}) async-start(f32[16,1,384]{2,1,0:T(1,128)} %broadcast_in_dim.22), calls=%async_computation.6 | async-start | bytes 49152 | tf_op jit(solution)/shard_map/all_to_all | solution.py:27
  114.3 6.7 %all-to-all-done.6 = f32[16,1,384]{2,1,0:T(1,128)S(1)} async-done(((f32[16,1,384]{2,1,0:T(1,128)}), f32[16,1,384]{2,1,0:T(1,128)S(1)}, u32[]{:S(2)}, u32[]{:S(2)}) %all-to-all-start.6) | async-done | bytes 24608 | tf_op jit(solution)/shard_map/all_to_all | solution.py:27
  121.0 3.6 %multiply_reduce_fusion = f32[4096]{0:T(1024)S(1)} fusion(f32[384,4096]{1,0:T(8,128)} %get-tuple-element.3, f32[384]{0:T(512)S(1)} %broadcast_divide_fusion), kind=kLoop, calls=%fused_computation.3 | loop fusion | flops 3141632 | bytes 6309376 | tf_op jit(solution)/shard_map/reduce_sum | solution.py:68
  124.7 9.0 %fusion = f32[32,8,4096]{2,1,0:T(8,128)S(1)} fusion(f32[384,4096]{1,0:T(8,128)} %get-tuple-element.3, f32[384,256]{0,1:T(8,128)S(1)} %bitcast_multiply_fusion), kind=kOutput, calls=%fused_computation.1 | convolution fusion | flops 4831838208 | bytes 10878976 | tf_op jit(solution)/shard_map/dot_general | solution.py:71
  133.7 0.5 broadcast_in_dim.23
  134.2 4.2 %pad_maximum_fusion = f32[32,9,4096]{2,1,0:T(8,128)} fusion(f32[32,1,4096]{2,1,0:T(1,128)S(1)} %broadcast_in_dim.23, f32[32,8,4096]{2,1,0:T(8,128)S(1)} %fusion), kind=kLoop, calls=%fused_computation | loop fusion | flops 1179648 | bytes 9437184 | tf_op jit(solution)/shard_map/concatenate | solution.py:80
  138.4 6.1 %reshape_reshape.3 = f32[2,144,4096]{2,1,0:T(8,128)} reshape(f32[32,9,4096]{2,1,0:T(8,128)} %pad_maximum_fusion) | data formatting | bytes 9437184 | tf_op jit(solution)/shard_map/reshape;reshape | solution.py:49
  144.5 15.9 %all_to_all.62 = f32[2,144,4096]{2,1,0:T(8,128)} all-to-all(f32[2,144,4096]{2,1,0:T(8,128)} %reshape_reshape.3), channel_id=1, replica_groups=mesh['z_hi'=4,'y'=4,'core'=2,'x'=4,'z_lo'=4] {'core'}, dimensions={0} | all-to-all | bytes 9437184 | tf_op jit(solution)/shard_map/all_to_all | solution.py:50
  160.4 4.3 %reduce_sum.157 = f32[144,4096]{1,0:T(8,128)} reduce(f32[2,144,4096]{2,1,0:T(8,128)} %all_to_all.62, f32[]{:T(128)} %constant.20.clone.1), dimensions={0}, to_apply=%region_13.0 | reduce | flops 589824 | bytes 7077892 | tf_op jit(solution)/shard_map/reduce_sum | solution.py:50
  164.7 2.9 %reshape.79 = f32[4,36,4096]{2,1,0:T(8,128)} reshape(f32[144,4096]{1,0:T(8,128)} %reduce_sum.157) | data formatting | bytes 4718592 | tf_op jit(solution)/shard_map/reshape | solution.py:49
  167.6 36.2 %all_to_all.63 = f32[4,36,4096]{2,1,0:T(8,128)} all-to-all(f32[4,36,4096]{2,1,0:T(8,128)} %reshape.79), channel_id=1, replica_groups=mesh['z_hi'=4,'y'=4,'core'=2,'x'=4,'z_lo'=4] {'y'}, dimensions={0} | all-to-all | bytes 4718592 | tf_op jit(solution)/shard_map/all_to_all | solution.py:50
  203.8 2.0 reduce_sum.158
  205.8 1.1 reshape.80
  206.8 54.7 %all_to_all.64 = f32[4,9,4096]{2,1,0:T(8,128)S(1)} all-to-all(f32[4,9,4096]{2,1,0:T(8,128)} %reshape.80), channel_id=1, replica_groups=mesh['z_hi'=4,'y'=4,'core'=2,'x'=4,'z_lo'=4] {'z_hi'}, dimensions={0} | all-to-all | bytes 1179648 | tf_op jit(solution)/shard_map/all_to_all | solution.py:50
  261.5 0.1 reduce_sum.159
  261.6 0.7 slice_divide_fusion
  262.3 0.6 divide_log_fusion
  (16 shorter events, 0.3 us)
Async XLA Ops:
  0.6 1.6 copy-start
  7.6 55.5 %copy-start.2 = (s32[4096]{0:T(1024)S(1)}, s32[4096]{0:T(1024)}, u32[]{:S(2)}) copy-start(s32[4096]{0:T(1024)} %param.7) | copy-start | bytes 49156
  63.1 31.9 %copy-start.1 = (bf16[384,256]{1,0:T(8,128)(2,1)S(1)}, bf16[384,256]{1,0:T(8,128)(2,1)}, u32[]{:S(2)}) copy-start(bf16[384,256]{1,0:T(8,128)(2,1)} %param.4) | copy-start | bytes 589828
  91.7 14.9 %all-to-all-start.5 = ((f32[4,1,4096]{2,1,0:T(1,128)}), f32[4,1,4096]{2,1,0:T(1,128)S(1)}, u32[]{:S(2)}, u32[]{:S(2)}) async-start(f32[4,1,4096]{2,1,0:T(1,128)} %broadcast_in_dim.21), calls=%async_computation.5 | async-start | bytes 131072 | tf_op jit(solution)/shard_map/all_to_all | solution.py:27
  110.7 10.3 %all-to-all-start.6 = ((f32[16,1,384]{2,1,0:T(1,128)}), f32[16,1,384]{2,1,0:T(1,128)S(1)}, u32[]{:S(2)}, u32[]{:S(2)}) async-start(f32[16,1,384]{2,1,0:T(1,128)} %broadcast_in_dim.22), calls=%async_computation.6 | async-start | bytes 49152 | tf_op jit(solution)/shard_map/all_to_all | solution.py:27

commit v7 on v6

--- a/solution.py
+++ b/solution.py
@@ -68,25 +68,28 @@
     col_part = jnp.sum(kernel * row_scale[:, None], axis=0)
 
     weighted = scatter_rows(points).astype(jnp.float32) * row_scale[:, None]
+    lanes = 512
+    chunks = n_lists // lanes
     sums = lax.dot_general(
         weighted,
-        kernel,
+        kernel.reshape(kernel.shape[0], chunks, lanes),
         (((0,), (0,)), ((), ())),
-        precision=lax.Precision.HIGHEST,
+        precision=lax.Precision.HIGH,
         preferred_element_type=jnp.float32,
     )
     blocks = lax.axis_size(PTS)
     rows = sums.shape[0] // blocks
     packed = jnp.concatenate(
         [
-            sums.reshape(blocks, rows, n_lists),
-            jnp.broadcast_to(col_part[None, None, :], (blocks, 1, n_lists)),
+            sums.reshape(blocks, rows * chunks, lanes),
+            jnp.broadcast_to(col_part.reshape(1, chunks, lanes), (blocks, chunks, lanes)),
         ],
         axis=1,
-    ).reshape(blocks * (rows + 1), n_lists)
+    ).reshape(blocks * (rows + 1) * chunks, lanes)
     reduced = sum_scatter(packed)
-    col_total = reduced[rows]
-    return (reduced[:rows] / col_total[None, :], jnp.log(target / col_total))
+    col_total = reduced[rows * chunks :].reshape(n_lists)
+    means = reduced[: rows * chunks].reshape(rows, n_lists) / col_total[None, :]
+    return (means, jnp.log(target / col_total))
 
 
 def solution(mesh):

time: 264 us -> 224 us (0.85); the launches traced: 263 us -> 220 us
  blocking collectives: 179 us -> 165 us
  waiting for transfers between devices: 18.2 us -> 6.41 us
  local copies, waits for them, and re-layouts: 13.8 us -> 5.17 us
  other arithmetic: 30 us -> 26.7 us
  starting transfers between devices: 6.78 us -> 3.68 us
    all_to_all x3, blocking collectives: 107 us -> 78.5 us  [sum_scatter(): value = jnp.sum(lax.all_to_all(blocks, name, 0, 0), axis=0)]
    all_to_all x5 -> x6, blocking collectives: 72.2 us -> 86.3 us  [exchange_sum(): return jnp.sum(lax.all_to_all(copies, names, 0, 0), axis=0)]
    all_to_all x2 -> x1, waiting for transfers between devices: 18.2 us -> 6.41 us  [exchange_sum(): return jnp.sum(lax.all_to_all(copies, names, 0, 0), axis=0)]
    another operation x1 -> x0, local copies, waits for them, and re-layouts: 6.08 us -> none  [sum_scatter(): blocks = value.reshape(n, value.shape[0] // n, value.shape[1])]
    reshape x2 -> x1, local copies, waits for them, and re-layouts: 3.97 us -> 0.03 us  [local(): means = reduced[:rows * chunks].reshape(rows, n_lists) / col_total[None, :]]
    concatenate x1, other arithmetic: 4.22 us -> 0.75 us  [local(): jnp.concatenate([sums.reshape(blocks, rows * chunks, lanes), jnp.broadcas...]
    all_to_all x2 -> x1, starting transfers between devices: 6.78 us -> 3.68 us  [exchange_sum(): return jnp.sum(lax.all_to_all(copies, names, 0, 0), axis=0)]
  transfers between devices with their start and end apart: 2 -> 1, of which waited for: 2 -> 1; matrix products, arithmetic and copies ran while one was open for 0% -> 0% of each run, Pallas kernels for 0% -> 0%
where the time goes in v7:
time: 224 us; the launch traced here: 220 us
  blocking collectives  165 us (74%)
  other arithmetic  26.7 us (12%)
  matrix products  12.6 us (6%)
  waiting for transfers between devices  6.41 us (3%)
  local copies, waits for them, and re-layouts  5.17 us (2%)
  starting transfers between devices  3.68 us (2%)
    all_to_all x6, blocking collectives, exchange_sum(): return jnp.sum(lax.all_to_all(copies, names, 0, 0), axis=0)  86.3 us
    all_to_all x3, blocking collectives, sum_scatter(): value = jnp.sum(lax.all_to_all(blocks, name, 0, 0), axis=0)  78.5 us
    reduce_sum x2, other arithmetic, local(): col_scale = target / list_mass(jnp.sum(kernel * row_scale[:, None], axis=0))  7.32 us
    dot_general x1, matrix products, local(): lax.dot_general(weighted, kernel.reshape(kernel.shape[0], chunks, lanes),...  7.28 us
    reduce_sum x2, other arithmetic, local(): row_scale = 1.0 / point_mass(jnp.sum(kernel * col_scale[None, :], axis=1))  6.63 us
    reduce_sum x3, other arithmetic, sum_scatter(): value = jnp.sum(lax.all_to_all(blocks, name, 0, 0), axis=0)  6.55 us
    all_to_all x1, waiting for transfers between devices, exchange_sum(): return jnp.sum(lax.all_to_all(copies, names, 0, 0), axis=0)  6.41 us
    dot_general x1, matrix products, kernel_tile(): lax.dot_general(points, cent_block, (((1,), (1,)), ((), ())), preferred_e...  5.34 us
  transfers between devices with their start and end apart: 1, of which 1 were waited for; matrix products, arithmetic and copies ran while one was open for 0% of the time, Pallas kernels for 0%

profile of v7, /device:TPU:1, one launch (start us, length us, event | category | flops | bytes accessed | tf_op | source)
XLA Modules:
  0.0 220.3 jit_solution(530122271816718268)
XLA Ops:
  0.6 0.0 copy-start
  0.7 1.6 copy-done
  2.2 5.3 %fusion.6 = (f32[384]{0:T(512)S(1)}, f32[384,4096]{1,0:T(8,128)}) fusion(s32[4096]{0:T(1024)S(1)} %iota_add_fusion, s32[384]{0:T(512)} %param.6, bf16[384,256]{1,0:T(8,128)(2,1)} %param.4, bf16[4096,256]{1,0:T(8,128)(2,1)S(1)} %copy-done), kind=kOutput, calls=%fused_computation.22 | convolution fusion | flops 813170304 | bytes 8604672 | tf_op jit(solution)/shard_map/dot_general | solution.py:10
  7.6 0.0 copy-start.2
  7.6 15.6 %all_to_all.57 = f32[16,1,384]{2,1,0:T(1,128)S(1)} all-to-all(f32[16,1,384]{2,1,0:T(1,128)S(1)} %broadcast_in_dim.18), channel_id=1, replica_groups=mesh['z_hi'=4,'y'=4,'core'=2,'x'=4,'z_lo'=4] {'x','z_lo'}, dimensions={0} | all-to-all | bytes 49152 | tf_op jit(solution)/shard_map/all_to_all | solution.py:27
  23.3 3.6 %multiply_reduce_fusion.4 = f32[4096]{0:T(1024)S(1)} fusion(f32[384,4096]{1,0:T(8,128)} %get-tuple-element.3, f32[384]{0:T(512)S(1)} %broadcast_divide_fusion.3), kind=kLoop, calls=%fused_computation.7 | loop fusion | flops 3141632 | bytes 6309376 | tf_op jit(solution)/shard_map/reduce_sum | solution.py:66
  26.9 0.1 broadcast_in_dim.19
  27.0 11.6 %all_to_all.58 = f32[8,1,4096]{2,1,0:T(1,128)S(1)} all-to-all(f32[8,1,4096]{2,1,0:T(1,128)S(1)} %broadcast_in_dim.19), channel_id=1, replica_groups=mesh['z_hi'=4,'y'=4,'core'=2,'x'=4,'z_lo'=4] {'y','core'}, dimensions={0} | all-to-all | bytes 262144 | tf_op jit(solution)/shard_map/all_to_all | solution.py:27
  38.6 0.1 reduce_sum.147
  38.8 24.2 %all_to_all.59 = f32[4,1,4096]{2,1,0:T(1,128)S(1)} all-to-all(f32[4,1,4096]{2,1,0:T(1,128)S(1)} %broadcast_in_dim.20), channel_id=1, replica_groups=mesh['z_hi'=4,'y'=4,'core'=2,'x'=4,'z_lo'=4] {'z_hi'}, dimensions={0} | all-to-all | bytes 131072 | tf_op jit(solution)/shard_map/all_to_all | solution.py:27
  63.0 0.1 reduce_sum.148
  63.1 0.0 copy-done.2
  63.1 3.3 %multiply_reduce_fusion.3 = f32[384]{0:T(512)S(1)} fusion(f32[384,4096]{1,0:T(8,128)} %get-tuple-element.3, f32[4096]{0:T(1024)S(1)} %fusion.5), kind=kLoop, calls=%fused_computation.6 | loop fusion | flops 3145344 | bytes 6309376 | tf_op jit(solution)/shard_map/reduce_sum | solution.py:65
  66.5 9.4 %all_to_all.60 = f32[16,1,384]{2,1,0:T(1,128)S(1)} all-to-all(f32[16,1,384]{2,1,0:T(1,128)S(1)} %broadcast_in_dim.21), channel_id=1, replica_groups=mesh['z_hi'=4,'y'=4,'core'=2,'x'=4,'z_lo'=4] {'x','z_lo'}, dimensions={0} | all-to-all | bytes 49152 | tf_op jit(solution)/shard_map/all_to_all | solution.py:27
  75.9 0.0 copy-start.1
  75.9 3.7 %multiply_reduce_fusion.2 = f32[4096]{0:T(1024)S(1)} fusion(f32[384,4096]{1,0:T(8,128)} %get-tuple-element.3, f32[384]{0:T(512)S(1)} %broadcast_divide_fusion.2), kind=kLoop, calls=%fused_computation.5 | loop fusion | flops 3141632 | bytes 6309376 | tf_op jit(solution)/shard_map/reduce_sum | solution.py:66
  79.6 0.1 broadcast_in_dim.22
  79.7 11.4 %all_to_all.61 = f32[8,1,4096]{2,1,0:T(1,128)S(1)} all-to-all(f32[8,1,4096]{2,1,0:T(1,128)S(1)} %broadcast_in_dim.22), channel_id=1, replica_groups=mesh['z_hi'=4,'y'=4,'core'=2,'x'=4,'z_lo'=4] {'y','core'}, dimensions={0} | all-to-all | bytes 262144 | tf_op jit(solution)/shard_map/all_to_all | solution.py:27
  91.0 0.1 reduce_sum.152
  91.2 14.1 %all_to_all.62 = f32[4,1,4096]{2,1,0:T(1,128)S(1)} all-to-all(f32[4,1,4096]{2,1,0:T(1,128)S(1)} %broadcast_in_dim.23), channel_id=1, replica_groups=mesh['z_hi'=4,'y'=4,'core'=2,'x'=4,'z_lo'=4] {'z_hi'}, dimensions={0} | all-to-all | bytes 131072 | tf_op jit(solution)/shard_map/all_to_all | solution.py:27
  105.2 0.1 reduce_sum.153
  105.3 3.3 %multiply_reduce_fusion.1 = f32[384]{0:T(512)S(1)} fusion(f32[384,4096]{1,0:T(8,128)} %get-tuple-element.3, f32[4096]{0:T(1024)S(1)} %fusion.4), kind=kLoop, calls=%fused_computation.4 | loop fusion | flops 3145344 | bytes 6309376 | tf_op jit(solution)/shard_map/reduce_sum | solution.py:67
  108.6 0.6 broadcast_in_dim.24
  109.2 3.7 %all-to-all-start.6 = ((f32[16,1,384]{2,1,0:T(1,128)}), f32[16,1,384]{2,1,0:T(1,128)S(1)}, u32[]{:S(2)}, u32[]{:S(2)}) async-start(f32[16,1,384]{2,1,0:T(1,128)} %broadcast_in_dim.24), calls=%async_computation.6 | async-start | bytes 49152 | tf_op jit(solution)/shard_map/all_to_all | solution.py:27
  112.9 0.0 copy-done.1
  112.9 0.2 copy.19
  113.1 6.4 %all-to-all-done.6 = f32[16,1,384]{2,1,0:T(1,128)S(1)} async-done(((f32[16,1,384]{2,1,0:T(1,128)}), f32[16,1,384]{2,1,0:T(1,128)S(1)}, u32[]{:S(2)}, u32[]{:S(2)}) %all-to-all-start.6) | async-done | bytes 24608 | tf_op jit(solution)/shard_map/all_to_all | solution.py:27
  119.5 3.6 %multiply_reduce_fusion = f32[4096]{0:T(1024)S(1)} fusion(f32[384,4096]{1,0:T(8,128)} %get-tuple-element.3, f32[384]{0:T(512)S(1)} %broadcast_divide_fusion.1), kind=kLoop, calls=%fused_computation.3 | loop fusion | flops 3141632 | bytes 6309376 | tf_op jit(solution)/shard_map/reduce_sum | solution.py:68
  123.3 7.3 %fusion = f32[256,8,512]{2,0,1:T(8,128)S(1)} fusion(f32[384,256,1]{0,1,2:T(8,128)S(1)} %bitcast.26, f32[48,8,8,512]{3,2,1,0:T(8,128)} %bitcast.21), kind=kOutput, calls=%fused_computation | convolution fusion | flops 2415919104 | bytes 10878976 | tf_op jit(solution)/shard_map/dot_general | solution.py:73
  130.6 2.4 %copy.29 = f32[256,8,512]{2,1,0:T(8,128)S(1)} copy(f32[256,8,512]{2,0,1:T(8,128)S(1)} %fusion) | data formatting | bytes 8388608 | tf_op jit(solution)/shard_map/dot_general | solution.py:73
  133.0 0.1 broadcast_in_dim.26
  133.1 0.8 pad_maximum_fusion
  133.8 11.7 %all_to_all.63 = f32[2,1152,512]{2,1,0:T(8,128)} all-to-all(f32[2,1152,512]{2,1,0:T(8,128)S(1)} %bitcast.22), channel_id=1, replica_groups=mesh['z_hi'=4,'y'=4,'core'=2,'x'=4,'z_lo'=4] {'core'}, dimensions={0} | all-to-all | bytes 9437184 | tf_op jit(solution)/shard_map/all_to_all | solution.py:50
  145.5 4.5 %reduce_sum.157 = f32[1152,512]{1,0:T(8,128)} reduce(f32[2,1152,512]{2,1,0:T(8,128)} %all_to_all.63, f32[]{:T(128)} %constant.20.clone.1), dimensions={0}, to_apply=%region_13.0 | reduce | flops 589824 | bytes 7077892 | tf_op jit(solution)/shard_map/reduce_sum | solution.py:50
  150.1 33.4 %all_to_all.64 = f32[4,288,512]{2,1,0:T(8,128)} all-to-all(f32[4,288,512]{2,1,0:T(8,128)} %bitcast.24), channel_id=1, replica_groups=mesh['z_hi'=4,'y'=4,'core'=2,'x'=4,'z_lo'=4] {'y'}, dimensions={0} | all-to-all | bytes 4718592 | tf_op jit(solution)/shard_map/all_to_all | solution.py:50
  183.4 2.0 reduce_sum.158
  185.4 33.4 %all_to_all.65 = f32[4,72,512]{2,1,0:T(8,128)S(1)} all-to-all(f32[4,72,512]{2,1,0:T(8,128)S(1)} %bitcast.25), channel_id=1, replica_groups=mesh['z_hi'=4,'y'=4,'core'=2,'x'=4,'z_lo'=4] {'z_hi'}, dimensions={0} | all-to-all | bytes 1179648 | tf_op jit(solution)/shard_map/all_to_all | solution.py:50
  219.0 0.6 divide_log_fusion
  219.6 0.7 broadcast_divide_fusion
  (21 shorter events, 0.4 us)
Async XLA Ops:
  0.6 1.6 copy-start
  7.6 55.5 %copy-start.2 = (s32[4096]{0:T(1024)S(1)}, s32[4096]{0:T(1024)}, u32[]{:S(2)}) copy-start(s32[4096]{0:T(1024)} %param.7) | copy-start | bytes 49156
  75.9 37.0 %copy-start.1 = (bf16[384,256]{1,0:T(8,128)(2,1)S(1)}, bf16[384,256]{1,0:T(8,128)(2,1)}, u32[]{:S(2)}) copy-start(bf16[384,256]{1,0:T(8,128)(2,1)} %param.4) | copy-start | bytes 589828
  109.2 10.3 %all-to-all-start.6 = ((f32[16,1,384]{2,1,0:T(1,128)}), f32[16,1,384]{2,1,0:T(1,128)S(1)}, u32[]{:S(2)}, u32[]{:S(2)}) async-start(f32[16,1,384]{2,1,0:T(1,128)} %broadcast_in_dim.24), calls=%async_computation.6 | async-start | bytes 49152 | tf_op jit(solution)/shard_map/all_to_all | solution.py:27

commit v8 on v7

--- a/solution.py
+++ b/solution.py
@@ -65,24 +65,33 @@
         row_scale = 1.0 / point_mass(jnp.sum(kernel * col_scale[None, :], axis=1))
         col_scale = target / list_mass(jnp.sum(kernel * row_scale[:, None], axis=0))
     row_scale = 1.0 / point_mass(jnp.sum(kernel * col_scale[None, :], axis=1))
-    col_part = jnp.sum(kernel * row_scale[:, None], axis=0)
 
-    weighted = scatter_rows(points).astype(jnp.float32) * row_scale[:, None]
+    n_pts, dim = points.shape
+    weighted = jnp.concatenate(
+        [
+            scatter_rows(points).astype(jnp.float32) * row_scale[:, None],
+            row_scale[:, None],
+            jnp.zeros((n_pts, 7), jnp.float32),
+        ],
+        axis=1,
+    )
     lanes = 512
     chunks = n_lists // lanes
-    sums = lax.dot_general(
+    product = lax.dot_general(
         weighted,
-        kernel.reshape(kernel.shape[0], chunks, lanes),
+        kernel.reshape(n_pts, chunks, lanes),
         (((0,), (0,)), ((), ())),
         precision=lax.Precision.HIGH,
         preferred_element_type=jnp.float32,
     )
+    sums = product[:dim]
+    col_part = product[dim]
     blocks = lax.axis_size(PTS)
     rows = sums.shape[0] // blocks
     packed = jnp.concatenate(
         [
             sums.reshape(blocks, rows * chunks, lanes),
-            jnp.broadcast_to(col_part.reshape(1, chunks, lanes), (blocks, chunks, lanes)),
+            jnp.broadcast_to(col_part[None], (blocks, chunks, lanes)),
         ],
         axis=1,
     ).reshape(blocks * (rows + 1) * chunks, lanes)

time: 224 us -> 222 us (level)
  blocking collectives: 165 us -> 151 us
  waiting for transfers between devices: 6.41 us -> 17.9 us
  other arithmetic: 26.7 us -> 23.1 us
  starting transfers between devices: 3.68 us -> 6.96 us
    all_to_all x6 -> x5, blocking collectives: 86.3 us -> 72.2 us  [exchange_sum(): return jnp.sum(lax.all_to_all(copies, names, 0, 0), axis=0)]
    all_to_all x1 -> x2, waiting for transfers between devices: 6.41 us -> 17.9 us  [exchange_sum(): return jnp.sum(lax.all_to_all(copies, names, 0, 0), axis=0)]
    reduce_sum x1 -> x0, other arithmetic: 3.64 us -> none  [local(): col_part = jnp.sum(kernel * row_scale[:, None], axis=0)]
    all_to_all x1 -> x2, starting transfers between devices: 3.68 us -> 6.96 us  [exchange_sum(): return jnp.sum(lax.all_to_all(copies, names, 0, 0), axis=0)]
    slice x0 -> x3, local copies, waits for them, and re-layouts: none -> 3.08 us  [the longest x2 3.07 us: local(): sums = product[:dim]]
    dot_general x1 -> x0, local copies, waits for them, and re-layouts: 2.43 us -> none  [local(): lax.dot_general(weighted, kernel.reshape(kernel.shape[0], chunks, lanes),...]
  transfers between devices with their start and end apart: 1 -> 2, of which waited for: 1 -> 2; matrix products, arithmetic and copies ran while one was open for 0% -> 0% of each run, Pallas kernels for 0% -> 0%
where the time goes in v8:
time: 222 us; the launch traced here: 219 us
  blocking collectives  151 us (68%)
  other arithmetic  23.1 us (10%)
  waiting for transfers between devices  17.9 us (8%)
  matrix products  12.5 us (6%)
  starting transfers between devices  6.96 us (3%)
  local copies, waits for them, and re-layouts  6.53 us (3%)
    all_to_all x3, blocking collectives, sum_scatter(): value = jnp.sum(lax.all_to_all(blocks, name, 0, 0), axis=0)  78.5 us
    all_to_all x5, blocking collectives, exchange_sum(): return jnp.sum(lax.all_to_all(copies, names, 0, 0), axis=0)  72.2 us
    all_to_all x2, waiting for transfers between devices, exchange_sum(): return jnp.sum(lax.all_to_all(copies, names, 0, 0), axis=0)  17.9 us
    reduce_sum x2, other arithmetic, local(): col_scale = target / list_mass(jnp.sum(kernel * row_scale[:, None], axis=0))  7.28 us
    dot_general x1, matrix products, local(): lax.dot_general(weighted, kernel.reshape(n_pts, chunks, lanes), (((0,), (...  7.18 us
    all_to_all x2, starting transfers between devices, exchange_sum(): return jnp.sum(lax.all_to_all(copies, names, 0, 0), axis=0)  6.96 us
    reduce_sum x2, other arithmetic, local(): row_scale = 1.0 / point_mass(jnp.sum(kernel * col_scale[None, :], axis=1))  6.62 us
    reduce_sum x3, other arithmetic, sum_scatter(): value = jnp.sum(lax.all_to_all(blocks, name, 0, 0), axis=0)  6.55 us
  transfers between devices with their start and end apart: 2, of which 2 were waited for; matrix products, arithmetic and copies ran while one was open for 0% of the time, Pallas kernels for 0%

profile of v8, /device:TPU:1, one launch (start us, length us, event | category | flops | bytes accessed | tf_op | source)
XLA Modules:
  0.0 218.6 jit_solution(9237662073678035893)
XLA Ops:
  0.6 0.0 copy-start
  0.7 1.6 copy-done
  2.2 5.3 %fusion.10 = (f32[384]{0:T(512)S(1)}, f32[384,4096]{1,0:T(8,128)}) fusion(s32[4096]{0:T(1024)S(1)} %iota_add_fusion, s32[384]{0:T(512)} %param.6, bf16[384,256]{1,0:T(8,128)(2,1)} %param.4, bf16[4096,256]{1,0:T(8,128)(2,1)S(1)} %copy-done), kind=kOutput, calls=%fused_computation.28 | convolution fusion | flops 813170304 | bytes 8604672 | tf_op jit(solution)/shard_map/dot_general | solution.py:10
  7.6 0.0 copy-start.2
  7.6 15.6 %all_to_all.57 = f32[16,1,384]{2,1,0:T(1,128)S(1)} all-to-all(f32[16,1,384]{2,1,0:T(1,128)S(1)} %broadcast_in_dim.20), channel_id=1, replica_groups=mesh['z_hi'=4,'y'=4,'core'=2,'x'=4,'z_lo'=4] {'x','z_lo'}, dimensions={0} | all-to-all | bytes 49152 | tf_op jit(solution)/shard_map/all_to_all | solution.py:27
  23.3 3.6 %multiply_reduce_fusion.3 = f32[4096]{0:T(1024)S(1)} fusion(f32[384,4096]{1,0:T(8,128)} %get-tuple-element.3, f32[384]{0:T(512)S(1)} %broadcast_divide_fusion.3), kind=kLoop, calls=%fused_computation.6 | loop fusion | flops 3141632 | bytes 6309376 | tf_op jit(solution)/shard_map/reduce_sum | solution.py:66
  26.9 0.1 broadcast_in_dim.21
  27.0 11.6 %all_to_all.58 = f32[8,1,4096]{2,1,0:T(1,128)S(1)} all-to-all(f32[8,1,4096]{2,1,0:T(1,128)S(1)} %broadcast_in_dim.21), channel_id=1, replica_groups=mesh['z_hi'=4,'y'=4,'core'=2,'x'=4,'z_lo'=4] {'y','core'}, dimensions={0} | all-to-all | bytes 262144 | tf_op jit(solution)/shard_map/all_to_all | solution.py:27
  38.6 0.1 reduce_sum.138
  38.8 24.2 %all_to_all.59 = f32[4,1,4096]{2,1,0:T(1,128)S(1)} all-to-all(f32[4,1,4096]{2,1,0:T(1,128)S(1)} %broadcast_in_dim.22), channel_id=1, replica_groups=mesh['z_hi'=4,'y'=4,'core'=2,'x'=4,'z_lo'=4] {'z_hi'}, dimensions={0} | all-to-all | bytes 131072 | tf_op jit(solution)/shard_map/all_to_all | solution.py:27
  63.0 0.1 reduce_sum.139
  63.1 0.0 copy-done.2
  63.1 0.0 copy-start.1
  63.1 3.3 %multiply_reduce_fusion.2 = f32[384]{0:T(512)S(1)} fusion(f32[384,4096]{1,0:T(8,128)} %get-tuple-element.3, f32[4096]{0:T(1024)S(1)} %fusion.8), kind=kLoop, calls=%fused_computation.5 | loop fusion | flops 3145344 | bytes 6309376 | tf_op jit(solution)/shard_map/reduce_sum | solution.py:65
  66.5 9.4 %all_to_all.60 = f32[16,1,384]{2,1,0:T(1,128)S(1)} all-to-all(f32[16,1,384]{2,1,0:T(1,128)S(1)} %broadcast_in_dim.23), channel_id=1, replica_groups=mesh['z_hi'=4,'y'=4,'core'=2,'x'=4,'z_lo'=4] {'x','z_lo'}, dimensions={0} | all-to-all | bytes 49152 | tf_op jit(solution)/shard_map/all_to_all | solution.py:27
  75.9 3.6 %multiply_reduce_fusion.1 = f32[4096]{0:T(1024)S(1)} fusion(f32[384,4096]{1,0:T(8,128)} %get-tuple-element.3, f32[384]{0:T(512)S(1)} %broadcast_divide_fusion.2), kind=kLoop, calls=%fused_computation.4 | loop fusion | flops 3141632 | bytes 6309376 | tf_op jit(solution)/shard_map/reduce_sum | solution.py:66
  79.5 0.1 broadcast_in_dim.24
  79.6 11.4 %all_to_all.61 = f32[8,1,4096]{2,1,0:T(1,128)S(1)} all-to-all(f32[8,1,4096]{2,1,0:T(1,128)S(1)} %broadcast_in_dim.24), channel_id=1, replica_groups=mesh['z_hi'=4,'y'=4,'core'=2,'x'=4,'z_lo'=4] {'y','core'}, dimensions={0} | all-to-all | bytes 262144 | tf_op jit(solution)/shard_map/all_to_all | solution.py:27
  91.0 0.1 reduce_sum.143
  91.1 0.7 broadcast_in_dim.25
  91.8 3.3 %all-to-all-start.5 = ((f32[4,1,4096]{2,1,0:T(1,128)}), f32[4,1,4096]{2,1,0:T(1,128)S(1)}, u32[]{:S(2)}, u32[]{:S(2)}) async-start(f32[4,1,4096]{2,1,0:T(1,128)} %broadcast_in_dim.25), calls=%async_computation.5 | async-start | bytes 131072 | tf_op jit(solution)/shard_map/all_to_all | solution.py:27
  95.0 0.0 copy-done.1
  95.1 0.2 copy.16
  95.2 11.5 %all-to-all-done.5 = f32[4,1,4096]{2,1,0:T(1,128)S(1)} async-done(((f32[4,1,4096]{2,1,0:T(1,128)}), f32[4,1,4096]{2,1,0:T(1,128)S(1)}, u32[]{:S(2)}, u32[]{:S(2)}) %all-to-all-start.5) | async-done | bytes 65568 | tf_op jit(solution)/shard_map/all_to_all | solution.py:27
  106.7 0.1 reduce_sum.144
  106.8 3.3 %multiply_reduce_fusion = f32[384]{0:T(512)S(1)} fusion(f32[384,4096]{1,0:T(8,128)} %get-tuple-element.3, f32[4096]{0:T(1024)S(1)} %fusion.7), kind=kLoop, calls=%fused_computation.3 | loop fusion | flops 3145344 | bytes 6309376 | tf_op jit(solution)/shard_map/reduce_sum | solution.py:67
  110.1 0.6 broadcast_in_dim.26
  110.7 3.7 %all-to-all-start.6 = ((f32[16,1,384]{2,1,0:T(1,128)}), f32[16,1,384]{2,1,0:T(1,128)S(1)}, u32[]{:S(2)}, u32[]{:S(2)}) async-start(f32[16,1,384]{2,1,0:T(1,128)} %broadcast_in_dim.26), calls=%async_computation.6 | async-start | bytes 49152 | tf_op jit(solution)/shard_map/all_to_all | solution.py:27
  114.5 0.1 pad.4.clone
  114.5 6.4 %all-to-all-done.6 = f32[16,1,384]{2,1,0:T(1,128)S(1)} async-done(((f32[16,1,384]{2,1,0:T(1,128)}), f32[16,1,384]{2,1,0:T(1,128)S(1)}, u32[]{:S(2)}, u32[]{:S(2)}) %all-to-all-start.6) | async-done | bytes 24608 | tf_op jit(solution)/shard_map/all_to_all | solution.py:27
  121.1 7.2 %fusion = f32[264,8,512]{2,0,1:T(8,128)S(1)} fusion(f32[48,8,8,512]{3,2,1,0:T(8,128)} %bitcast.25, f32[384,1]{0,1:T(1,128)S(1)} %div.52, f32[384,256]{0,1:T(8,128)S(1)} %bitcast_multiply_fusion, f32[264]{0:T(512)S(1)} %pad.4.clone), kind=kOutput, calls=%fused_computation | convolution fusion | flops 2491619328 | bytes 11012640 | tf_op jit(solution)/shard_map/dot_general | solution.py:80
  128.3 0.6 slice.16
  128.9 2.4 %copy.26 = f32[256,8,512]{2,1,0:T(8,128)S(1)} copy(f32[256,8,512]{2,0,1:T(8,128)S(1)} %slice.16) | data formatting | bytes 8388608 | tf_op jit(solution)/shard_map/slice | solution.py:87
  131.4 0.1 broadcast_in_dim.29
  131.4 0.8 pad_maximum_fusion
  132.2 11.7 %all_to_all.62 = f32[2,1152,512]{2,1,0:T(8,128)} all-to-all(f32[2,1152,512]{2,1,0:T(8,128)S(1)} %bitcast.26), channel_id=1, replica_groups=mesh['z_hi'=4,'y'=4,'core'=2,'x'=4,'z_lo'=4] {'core'}, dimensions={0} | all-to-all | bytes 9437184 | tf_op jit(solution)/shard_map/all_to_all | solution.py:50
  143.9 4.5 %reduce_sum.147 = f32[1152,512]{1,0:T(8,128)} reduce(f32[2,1152,512]{2,1,0:T(8,128)} %all_to_all.62, f32[]{:T(128)} %constant.21.clone.1), dimensions={0}, to_apply=%region_12.0 | reduce | flops 589824 | bytes 7077892 | tf_op jit(solution)/shard_map/reduce_sum | solution.py:50
  148.4 33.4 %all_to_all.63 = f32[4,288,512]{2,1,0:T(8,128)} all-to-all(f32[4,288,512]{2,1,0:T(8,128)} %bitcast.28), channel_id=1, replica_groups=mesh['z_hi'=4,'y'=4,'core'=2,'x'=4,'z_lo'=4] {'y'}, dimensions={0} | all-to-all | bytes 4718592 | tf_op jit(solution)/shard_map/all_to_all | solution.py:50
  181.8 2.0 reduce_sum.148
  183.8 33.4 %all_to_all.64 = f32[4,72,512]{2,1,0:T(8,128)S(1)} all-to-all(f32[4,72,512]{2,1,0:T(8,128)S(1)} %bitcast.29), channel_id=1, replica_groups=mesh['z_hi'=4,'y'=4,'core'=2,'x'=4,'z_lo'=4] {'z_hi'}, dimensions={0} | all-to-all | bytes 1179648 | tf_op jit(solution)/shard_map/all_to_all | solution.py:50
  217.3 0.6 divide_log_fusion
  217.9 0.7 broadcast_divide_fusion
  (24 shorter events, 0.4 us)
Async XLA Ops:
  0.6 1.6 copy-start
  7.6 55.5 %copy-start.2 = (s32[4096]{0:T(1024)S(1)}, s32[4096]{0:T(1024)}, u32[]{:S(2)}) copy-start(s32[4096]{0:T(1024)} %param.7) | copy-start | bytes 49156
  63.1 31.9 %copy-start.1 = (bf16[384,256]{1,0:T(8,128)(2,1)S(1)}, bf16[384,256]{1,0:T(8,128)(2,1)}, u32[]{:S(2)}) copy-start(bf16[384,256]{1,0:T(8,128)(2,1)} %param.4) | copy-start | bytes 589828
  91.8 14.9 %all-to-all-start.5 = ((f32[4,1,4096]{2,1,0:T(1,128)}), f32[4,1,4096]{2,1,0:T(1,128)S(1)}, u32[]{:S(2)}, u32[]{:S(2)}) async-start(f32[4,1,4096]{2,1,0:T(1,128)} %broadcast_in_dim.25), calls=%async_computation.5 | async-start | bytes 131072 | tf_op jit(solution)/shard_map/all_to_all | solution.py:27
  110.7 10.3 %all-to-all-start.6 = ((f32[16,1,384]{2,1,0:T(1,128)}), f32[16,1,384]{2,1,0:T(1,128)S(1)}, u32[]{:S(2)}, u32[]{:S(2)}) async-start(f32[16,1,384]{2,1,0:T(1,128)} %broadcast_in_dim.26), calls=%async_computation.6 | async-start | bytes 49152 | tf_op jit(solution)/shard_map/all_to_all | solution.py:27

commit v9 on v8

--- a/solution.py
+++ b/solution.py
@@ -43,12 +43,32 @@
     return blocked.transpose(0, 3, 2, 1, 4).reshape(n, points.shape[1])
 
 
+def exchange_scatter(value, name):
+    n = lax.axis_size(name)
+    blocks = value.reshape(n, value.shape[0] // n, value.shape[1])
+    return jnp.sum(lax.all_to_all(blocks, name, 0, 0), axis=0)
+
+
+def permute_scatter(value, name):
+    n = lax.axis_size(name)
+    me = lax.axis_index(name)
+    blocks = value.reshape(n, value.shape[0] // n, value.shape[1])
+    total = lax.dynamic_index_in_dim(blocks, me, 0, keepdims=False)
+    for shift in range(1, n):
+        outgoing = lax.dynamic_index_in_dim(blocks, (me + shift) % n, 0, keepdims=False)
+        total = total + lax.ppermute(outgoing, name, [(i, (i + shift) % n) for i in range(n)])
+    return total
+
+
 def sum_scatter(value):
-    for name in ("core", "y", "z_hi"):
-        n = lax.axis_size(name)
-        blocks = value.reshape(n, value.shape[0] // n, value.shape[1])
-        value = jnp.sum(lax.all_to_all(blocks, name, 0, 0), axis=0)
-    return value
+    value = exchange_scatter(value, "core")
+    width = value.shape[1] // 2
+    first = permute_scatter(value[:, :width], "y")
+    first, rest = lax.optimization_barrier((first, value[:, width:]))
+    second = permute_scatter(rest, "y")
+    first = permute_scatter(first, "z_hi")
+    second = permute_scatter(second, "z_hi")
+    return jnp.concatenate([first, second], axis=1)
 
 
 def local(points, centroids, prior, loads):

time: 222 us -> 230 us (1.036)
  blocking collectives: 151 us -> 84 us
  starting transfers between devices: 6.96 us -> 54.9 us
  waiting for transfers between devices: 17.9 us -> 38.5 us
  local copies, waits for them, and re-layouts: 6.53 us -> 12.2 us
    all_to_all x3 -> x1, blocking collectives: 78.5 us -> 11.7 us  [exchange_scatter(): return jnp.sum(lax.all_to_all(blocks, name, 0, 0), axis=0)]
    ppermute x0 -> x12, starting transfers between devices: none -> 48 us  [permute_scatter(): lax.ppermute(outgoing, name, [(i, (i + shift) % n) for i in range(n)])]
    ppermute x0 -> x12, waiting for transfers between devices: none -> 20.6 us  [permute_scatter(): lax.ppermute(outgoing, name, [(i, (i + shift) % n) for i in range(n)])]
    add x0 -> x4, other arithmetic: none -> 4.17 us  [permute_scatter(): total + lax.ppermute(outgoing, name, [(i, (i + shift) % n) for i in range...]
    squeeze x0 -> x4, local copies, waits for them, and re-layouts: none -> 2.94 us  [permute_scatter(): lax.dynamic_index_in_dim(blocks, (me + shift) % n, 0, keepdims=False)]
    reduce_sum x3 -> x1, other arithmetic: 6.55 us -> 4.54 us  [exchange_scatter(): return jnp.sum(lax.all_to_all(blocks, name, 0, 0), axis=0)]
  transfers between devices with their start and end apart: 2 -> 14, of which waited for: 2 -> 6; matrix products, arithmetic and copies ran while one was open for 0% -> 2% of each run, Pallas kernels for 0% -> 0%
where the time goes in v9:
time: 230 us; the launch traced here: 229 us
  blocking collectives  84 us (37%)
  starting transfers between devices  54.9 us (24%)
  waiting for transfers between devices  38.5 us (17%)
  other arithmetic  25.2 us (11%)
  matrix products  12.5 us (5%)
  local copies, waits for them, and re-layouts  12.2 us (5%)
    all_to_all x5, blocking collectives, exchange_sum(): return jnp.sum(lax.all_to_all(copies, names, 0, 0), axis=0)  72.2 us
    ppermute x12, starting transfers between devices, permute_scatter(): lax.ppermute(outgoing, name, [(i, (i + shift) % n) for i in range(n)])  48 us
    ppermute x12, waiting for transfers between devices, permute_scatter(): lax.ppermute(outgoing, name, [(i, (i + shift) % n) for i in range(n)])  20.6 us
    all_to_all x2, waiting for transfers between devices, exchange_sum(): return jnp.sum(lax.all_to_all(copies, names, 0, 0), axis=0)  17.9 us
    all_to_all x1, blocking collectives, exchange_scatter(): return jnp.sum(lax.all_to_all(blocks, name, 0, 0), axis=0)  11.7 us
    reduce_sum x2, other arithmetic, local(): col_scale = target / list_mass(jnp.sum(kernel * row_scale[:, None], axis=0))  7.28 us
    dot_general x1, matrix products, local(): lax.dot_general(weighted, kernel.reshape(n_pts, chunks, lanes), (((0,), (...  7.18 us
    all_to_all x2, starting transfers between devices, exchange_sum(): return jnp.sum(lax.all_to_all(copies, names, 0, 0), axis=0)  6.96 us
  transfers between devices with their start and end apart: 14, of which 6 were waited for; matrix products, arithmetic and copies ran while one was open for 2% of the time, Pallas kernels for 0%

profile of v9, /device:TPU:1, one launch (start us, length us, event | category | flops | bytes accessed | tf_op | source)
XLA Modules:
  0.0 228.5 jit_solution(11972904901965834319)
XLA Ops:
  0.7 1.6 copy-done
  2.2 5.3 %fusion.21 = (f32[384]{0:T(512)S(1)}, f32[384,4096]{1,0:T(8,128)}) fusion(s32[4096]{0:T(1024)S(1)} %iota_add_fusion, s32[384]{0:T(512)} %param.6, bf16[384,256]{1,0:T(8,128)(2,1)} %param.4, bf16[4096,256]{1,0:T(8,128)(2,1)S(1)} %copy-done), kind=kOutput, calls=%fused_computation.57 | convolution fusion | flops 813170304 | bytes 8604672 | tf_op jit(solution)/shard_map/dot_general | solution.py:10
  7.6 15.6 %all_to_all.47 = f32[16,1,384]{2,1,0:T(1,128)S(1)} all-to-all(f32[16,1,384]{2,1,0:T(1,128)S(1)} %broadcast_in_dim.20), channel_id=1, replica_groups=mesh['z_hi'=4,'y'=4,'core'=2,'x'=4,'z_lo'=4] {'x','z_lo'}, dimensions={0} | all-to-all | bytes 49152 | tf_op jit(solution)/shard_map/all_to_all | solution.py:27
  23.3 3.6 %multiply_reduce_fusion.3 = f32[4096]{0:T(1024)S(1)} fusion(f32[384,4096]{1,0:T(8,128)} %get-tuple-element.21, f32[384]{0:T(512)S(1)} %broadcast_divide_fusion.3), kind=kLoop, calls=%fused_computation.6 | loop fusion | flops 3141632 | bytes 6309376 | tf_op jit(solution)/shard_map/reduce_sum | solution.py:86
  27.0 11.6 %all_to_all.48 = f32[8,1,4096]{2,1,0:T(1,128)S(1)} all-to-all(f32[8,1,4096]{2,1,0:T(1,128)S(1)} %broadcast_in_dim.21), channel_id=1, replica_groups=mesh['z_hi'=4,'y'=4,'core'=2,'x'=4,'z_lo'=4] {'y','core'}, dimensions={0} | all-to-all | bytes 262144 | tf_op jit(solution)/shard_map/all_to_all | solution.py:27
  38.8 24.2 %all_to_all.49 = f32[4,1,4096]{2,1,0:T(1,128)S(1)} all-to-all(f32[4,1,4096]{2,1,0:T(1,128)S(1)} %broadcast_in_dim.22), channel_id=1, replica_groups=mesh['z_hi'=4,'y'=4,'core'=2,'x'=4,'z_lo'=4] {'z_hi'}, dimensions={0} | all-to-all | bytes 131072 | tf_op jit(solution)/shard_map/all_to_all | solution.py:27
  63.1 3.3 %multiply_reduce_fusion.2 = f32[384]{0:T(512)S(1)} fusion(f32[384,4096]{1,0:T(8,128)} %get-tuple-element.21, f32[4096]{0:T(1024)S(1)} %fusion.18), kind=kLoop, calls=%fused_computation.5 | loop fusion | flops 3145344 | bytes 6309376 | tf_op jit(solution)/shard_map/reduce_sum | solution.py:85
  66.5 9.4 %all_to_all.50 = f32[16,1,384]{2,1,0:T(1,128)S(1)} all-to-all(f32[16,1,384]{2,1,0:T(1,128)S(1)} %broadcast_in_dim.23), channel_id=1, replica_groups=mesh['z_hi'=4,'y'=4,'core'=2,'x'=4,'z_lo'=4] {'x','z_lo'}, dimensions={0} | all-to-all | bytes 49152 | tf_op jit(solution)/shard_map/all_to_all | solution.py:27
  75.9 3.6 %multiply_reduce_fusion.1 = f32[4096]{0:T(1024)S(1)} fusion(f32[384,4096]{1,0:T(8,128)} %get-tuple-element.21, f32[384]{0:T(512)S(1)} %broadcast_divide_fusion.2), kind=kLoop, calls=%fused_computation.4 | loop fusion | flops 3141632 | bytes 6309376 | tf_op jit(solution)/shard_map/reduce_sum | solution.py:86
  79.6 11.4 %all_to_all.51 = f32[8,1,4096]{2,1,0:T(1,128)S(1)} all-to-all(f32[8,1,4096]{2,1,0:T(1,128)S(1)} %broadcast_in_dim.24), channel_id=1, replica_groups=mesh['z_hi'=4,'y'=4,'core'=2,'x'=4,'z_lo'=4] {'y','core'}, dimensions={0} | all-to-all | bytes 262144 | tf_op jit(solution)/shard_map/all_to_all | solution.py:27
  91.1 0.7 broadcast_in_dim.25
  91.8 3.3 %all-to-all-start.5 = ((f32[4,1,4096]{2,1,0:T(1,128)}), f32[4,1,4096]{2,1,0:T(1,128)S(1)}, u32[]{:S(2)}, u32[]{:S(2)}) async-start(f32[4,1,4096]{2,1,0:T(1,128)} %broadcast_in_dim.25), calls=%async_computation.5 | async-start | bytes 131072 | tf_op jit(solution)/shard_map/all_to_all | solution.py:27
  95.2 11.5 %all-to-all-done.5 = f32[4,1,4096]{2,1,0:T(1,128)S(1)} async-done(((f32[4,1,4096]{2,1,0:T(1,128)}), f32[4,1,4096]{2,1,0:T(1,128)S(1)}, u32[]{:S(2)}, u32[]{:S(2)}) %all-to-all-start.5) | async-done | bytes 65568 | tf_op jit(solution)/shard_map/all_to_all | solution.py:27
  106.8 3.3 %multiply_reduce_fusion = f32[384]{0:T(512)S(1)} fusion(f32[384,4096]{1,0:T(8,128)} %get-tuple-element.21, f32[4096]{0:T(1024)S(1)} %fusion.17), kind=kLoop, calls=%fused_computation.3 | loop fusion | flops 3145344 | bytes 6309376 | tf_op jit(solution)/shard_map/reduce_sum | solution.py:87
  110.1 0.6 broadcast_in_dim.26
  110.7 3.7 %all-to-all-start.6 = ((f32[16,1,384]{2,1,0:T(1,128)}), f32[16,1,384]{2,1,0:T(1,128)S(1)}, u32[]{:S(2)}, u32[]{:S(2)}) async-start(f32[16,1,384]{2,1,0:T(1,128)} %broadcast_in_dim.26), calls=%async_computation.6 | async-start | bytes 49152 | tf_op jit(solution)/shard_map/all_to_all | solution.py:27
  114.6 6.4 %all-to-all-done.6 = f32[16,1,384]{2,1,0:T(1,128)S(1)} async-done(((f32[16,1,384]{2,1,0:T(1,128)}), f32[16,1,384]{2,1,0:T(1,128)S(1)}, u32[]{:S(2)}, u32[]{:S(2)}) %all-to-all-start.6) | async-done | bytes 24608 | tf_op jit(solution)/shard_map/all_to_all | solution.py:27
  121.1 7.2 %fusion = f32[264,8,512]{2,0,1:T(8,128)S(1)} fusion(f32[48,8,8,512]{3,2,1,0:T(8,128)} %bitcast.75, f32[384,1]{0,1:T(1,128)S(1)} %div.52, f32[384,256]{0,1:T(8,128)S(1)} %bitcast_multiply_fusion, f32[264]{0:T(512)S(1)} %pad.6.clone), kind=kOutput, calls=%fused_computation | convolution fusion | flops 2491619328 | bytes 11012640 | tf_op jit(solution)/shard_map/dot_general | solution.py:100
  128.3 0.6 slice.24
  128.9 2.4 %copy.26 = f32[256,8,512]{2,1,0:T(8,128)S(1)} copy(f32[256,8,512]{2,0,1:T(8,128)S(1)} %slice.24) | data formatting | bytes 8388608 | tf_op jit(solution)/shard_map/slice | solution.py:107
  131.4 0.8 pad_maximum_fusion
  132.2 11.7 %all_to_all.52 = f32[2,1152,512]{2,1,0:T(8,128)} all-to-all(f32[2,1152,512]{2,1,0:T(8,128)S(1)} %bitcast.76), channel_id=1, replica_groups=mesh['z_hi'=4,'y'=4,'core'=2,'x'=4,'z_lo'=4] {'core'}, dimensions={0} | all-to-all | bytes 9437184 | tf_op jit(solution)/shard_map/all_to_all | solution.py:49
  143.9 4.5 %reduce_sum.129 = f32[1152,512]{1,0:T(8,128)} reduce(f32[2,1152,512]{2,1,0:T(8,128)} %all_to_all.52, f32[]{:T(128)} %constant.107.clone.1), dimensions={0}, to_apply=%region_12.0 | reduce | flops 589824 | bytes 7077892 | tf_op jit(solution)/shard_map/reduce_sum | solution.py:49
  148.4 1.8 fusion.20
  150.2 1.0 copy-done.1
  151.2 1.0 dynamic-slice_bitcast_fusion.5
  152.2 2.8 %collective-permute-start.2 = (f32[288,256]{1,0:T(8,128)}, f32[288,256]{1,0:T(8,128)}, u32[]{:S(2)}, u32[]{:S(2)}) collective-permute-start(f32[288,256]{1,0:T(8,128)} %get-tuple-element.12), channel_id=1, source_target_pairs={{0,96},{32,0},{64,32},{96,64},{1,97},{33,1},{65,33},{97,65},{2,98}... | collective-permute-start | bytes 884744 | tf_op jit(solution)/shard_map/ppermute | solution.py:59
  155.0 3.1 %collective-permute-start.1 = (f32[288,256]{1,0:T(8,128)}, f32[288,256]{1,0:T(8,128)}, u32[]{:S(2)}, u32[]{:S(2)}) collective-permute-start(f32[288,256]{1,0:T(8,128)} %get-tuple-element.13), channel_id=1, source_target_pairs={{0,64},{32,96},{64,0},{96,32},{1,65},{33,97},{65,1},{97,33},{2,66}... | collective-permute-start | bytes 884744 | tf_op jit(solution)/shard_map/ppermute | solution.py:59
  158.1 1.9 collective-permute-start
  160.0 2.6 %collective-permute-done.2 = f32[288,256]{1,0:T(8,128)} collective-permute-done((f32[288,256]{1,0:T(8,128)}, f32[288,256]{1,0:T(8,128)}, u32[]{:S(2)}, u32[]{:S(2)}) %collective-permute-start.2) | collective-permute-done | bytes 294944 | tf_op jit(solution)/shard_map/ppermute | solution.py:59
  162.6 4.0 %collective-permute-done.1 = f32[288,256]{1,0:T(8,128)} collective-permute-done((f32[288,256]{1,0:T(8,128)}, f32[288,256]{1,0:T(8,128)}, u32[]{:S(2)}, u32[]{:S(2)}) %collective-permute-start.1) | collective-permute-done | bytes 294944 | tf_op jit(solution)/shard_map/ppermute | solution.py:59
  166.7 7.3 %collective-permute-done = f32[288,256]{1,0:T(8,128)} collective-permute-done((f32[288,256]{1,0:T(8,128)}, f32[288,256]{1,0:T(8,128)}, u32[]{:S(2)}, u32[]{:S(2)}) %collective-permute-start) | collective-permute-done | bytes 294944 | tf_op jit(solution)/shard_map/ppermute | solution.py:59
  174.0 2.0 fusion.9
  176.0 1.0 dynamic-slice_bitcast_fusion.2
  176.9 1.9 collective-permute-start.8
  178.9 3.1 %collective-permute-start.7 = (f32[288,256]{1,0:T(8,128)}, f32[288,256]{1,0:T(8,128)}, u32[]{:S(2)}, u32[]{:S(2)}) collective-permute-start(f32[288,256]{1,0:T(8,128)} %get-tuple-element.10), channel_id=1, source_target_pairs={{0,64},{32,96},{64,0},{96,32},{1,65},{33,97},{65,1},{97,33},{2,66}... | collective-permute-start | bytes 884744 | tf_op jit(solution)/shard_map/ppermute | solution.py:59
  182.0 2.8 %collective-permute-start.6 = (f32[288,256]{1,0:T(8,128)}, f32[288,256]{1,0:T(8,128)}, u32[]{:S(2)}, u32[]{:S(2)}) collective-permute-start(f32[288,256]{1,0:T(8,128)} %get-tuple-element.8), channel_id=1, source_target_pairs={{0,32},{32,64},{64,96},{96,0},{1,33},{33,65},{65,97},{97,1},{2,34}... | collective-permute-start | bytes 884744 | tf_op jit(solution)/shard_map/ppermute | solution.py:59
  184.8 1.0 dynamic-slice_bitcast_fusion.11
  185.8 2.0 collective-permute-start.5
  187.7 7.0 %collective-permute-start.4 = (f32[72,256]{1,0:T(8,128)S(1)}, f32[72,256]{1,0:T(8,128)S(1)}, u32[]{:S(2)}, u32[]{:S(2)}) collective-permute-start(f32[72,256]{1,0:T(8,128)S(1)} %get-tuple-element.19), channel_id=1, source_target_pairs={{0,256},{128,384},{256,0},{384,128},{1,257},{129,385},{257,1},{385... | collective-permute-start | bytes 221192 | tf_op jit(solution)/shard_map/ppermute | solution.py:59
  194.8 3.1 %collective-permute-start.3 = (f32[72,256]{1,0:T(8,128)S(1)}, f32[72,256]{1,0:T(8,128)S(1)}, u32[]{:S(2)}, u32[]{:S(2)}) collective-permute-start(f32[72,256]{1,0:T(8,128)S(1)} %get-tuple-element.17), channel_id=1, source_target_pairs={{0,128},{128,256},{256,384},{384,0},{1,129},{129,257},{257,385},{3... | collective-permute-start | bytes 221192 | tf_op jit(solution)/shard_map/ppermute | solution.py:59
  197.9 1.2 fusion.7
  199.2 6.1 %collective-permute-start.11 = (f32[72,256]{1,0:T(8,128)S(1)}, f32[72,256]{1,0:T(8,128)S(1)}, u32[]{:S(2)}, u32[]{:S(2)}) collective-permute-start(f32[72,256]{1,0:T(8,128)S(1)} %get-tuple-element.15), channel_id=1, source_target_pairs={{0,384},{128,0},{256,128},{384,256},{1,385},{129,1},{257,129},{385... | collective-permute-start | bytes 221192 | tf_op jit(solution)/shard_map/ppermute | solution.py:59
  205.3 7.0 %collective-permute-start.10 = (f32[72,256]{1,0:T(8,128)S(1)}, f32[72,256]{1,0:T(8,128)S(1)}, u32[]{:S(2)}, u32[]{:S(2)}) collective-permute-start(f32[72,256]{1,0:T(8,128)S(1)} %get-tuple-element.16), channel_id=1, source_target_pairs={{0,256},{128,384},{256,0},{384,128},{1,257},{129,385},{257,1},{385... | collective-permute-start | bytes 221192 | tf_op jit(solution)/shard_map/ppermute | solution.py:59
  212.3 7.2 %collective-permute-start.9 = (f32[72,256]{1,0:T(8,128)S(1)}, f32[72,256]{1,0:T(8,128)S(1)}, u32[]{:S(2)}, u32[]{:S(2)}) collective-permute-start(f32[72,256]{1,0:T(8,128)S(1)} %get-tuple-element.14), channel_id=1, source_target_pairs={{0,128},{128,256},{256,384},{384,0},{1,129},{129,257},{257,385},{3... | collective-permute-start | bytes 221192 | tf_op jit(solution)/shard_map/ppermute | solution.py:59
  219.5 0.9 fusion.15
  220.4 6.7 %collective-permute-done.9 = f32[72,256]{1,0:T(8,128)S(1)} collective-permute-done((f32[72,256]{1,0:T(8,128)S(1)}, f32[72,256]{1,0:T(8,128)S(1)}, u32[]{:S(2)}, u32[]{:S(2)}) %collective-permute-start.9) | collective-permute-done | bytes 73760 | tf_op jit(solution)/shard_map/ppermute | solution.py:59
  227.9 0.7 broadcast_divide_fusion
  (49 shorter events, 1.9 us)
Async XLA Ops:
  0.6 1.6 copy-start
  7.6 55.5 %copy-start.3 = (s32[4096]{0:T(1024)S(1)}, s32[4096]{0:T(1024)}, u32[]{:S(2)}) copy-start(s32[4096]{0:T(1024)} %param.7) | copy-start | bytes 49156
  63.1 31.9 %copy-start.2 = (bf16[384,256]{1,0:T(8,128)(2,1)S(1)}, bf16[384,256]{1,0:T(8,128)(2,1)}, u32[]{:S(2)}) copy-start(bf16[384,256]{1,0:T(8,128)(2,1)} %param.4) | copy-start | bytes 589828
  91.8 14.9 %all-to-all-start.5 = ((f32[4,1,4096]{2,1,0:T(1,128)}), f32[4,1,4096]{2,1,0:T(1,128)S(1)}, u32[]{:S(2)}, u32[]{:S(2)}) async-start(f32[4,1,4096]{2,1,0:T(1,128)} %broadcast_in_dim.25), calls=%async_computation.5 | async-start | bytes 131072 | tf_op jit(solution)/shard_map/all_to_all | solution.py:27
  110.7 10.3 %all-to-all-start.6 = ((f32[16,1,384]{2,1,0:T(1,128)}), f32[16,1,384]{2,1,0:T(1,128)S(1)}, u32[]{:S(2)}, u32[]{:S(2)}) async-start(f32[16,1,384]{2,1,0:T(1,128)} %broadcast_in_dim.26), calls=%async_computation.6 | async-start | bytes 49152 | tf_op jit(solution)/shard_map/all_to_all | solution.py:27
  150.2 1.0 copy-start.1
  152.2 10.4 %collective-permute-start.2 = (f32[288,256]{1,0:T(8,128)}, f32[288,256]{1,0:T(8,128)}, u32[]{:S(2)}, u32[]{:S(2)}) collective-permute-start(f32[288,256]{1,0:T(8,128)} %get-tuple-element.12), channel_id=1, source_target_pairs={{0,96},{32,0},{64,32},{96,64},{1,97},{33,1},{65,33},{97,65},{2,98}... | collective-permute-start | bytes 884744 | tf_op jit(solution)/shard_map/ppermute | solution.py:59
  155.0 11.7 %collective-permute-start.1 = (f32[288,256]{1,0:T(8,128)}, f32[288,256]{1,0:T(8,128)}, u32[]{:S(2)}, u32[]{:S(2)}) collective-permute-start(f32[288,256]{1,0:T(8,128)} %get-tuple-element.13), channel_id=1, source_target_pairs={{0,64},{32,96},{64,0},{96,32},{1,65},{33,97},{65,1},{97,33},{2,66}... | collective-permute-start | bytes 884744 | tf_op jit(solution)/shard_map/ppermute | solution.py:59
  158.1 15.9 %collective-permute-start = (f32[288,256]{1,0:T(8,128)}, f32[288,256]{1,0:T(8,128)}, u32[]{:S(2)}, u32[]{:S(2)}) collective-permute-start(f32[288,256]{1,0:T(8,128)} %get-tuple-element.11), channel_id=1, source_target_pairs={{0,32},{32,64},{64,96},{96,0},{1,33},{33,65},{65,97},{97,1},{2,34}... | collective-permute-start | bytes 884744 | tf_op jit(solution)/shard_map/ppermute | solution.py:59
  176.9 17.8 %collective-permute-start.8 = (f32[288,256]{1,0:T(8,128)}, f32[288,256]{1,0:T(8,128)}, u32[]{:S(2)}, u32[]{:S(2)}) collective-permute-start(f32[288,256]{1,0:T(8,128)} %get-tuple-element.9), channel_id=1, source_target_pairs={{0,96},{32,0},{64,32},{96,64},{1,97},{33,1},{65,33},{97,65},{2,98}... | collective-permute-start | bytes 884744 | tf_op jit(solution)/shard_map/ppermute | solution.py:59
  178.9 19.0 %collective-permute-start.7 = (f32[288,256]{1,0:T(8,128)}, f32[288,256]{1,0:T(8,128)}, u32[]{:S(2)}, u32[]{:S(2)}) collective-permute-start(f32[288,256]{1,0:T(8,128)} %get-tuple-element.10), channel_id=1, source_target_pairs={{0,64},{32,96},{64,0},{96,32},{1,65},{33,97},{65,1},{97,33},{2,66}... | collective-permute-start | bytes 884744 | tf_op jit(solution)/shard_map/ppermute | solution.py:59
  182.0 15.9 %collective-permute-start.6 = (f32[288,256]{1,0:T(8,128)}, f32[288,256]{1,0:T(8,128)}, u32[]{:S(2)}, u32[]{:S(2)}) collective-permute-start(f32[288,256]{1,0:T(8,128)} %get-tuple-element.8), channel_id=1, source_target_pairs={{0,32},{32,64},{64,96},{96,0},{1,33},{33,65},{65,97},{97,1},{2,34}... | collective-permute-start | bytes 884744 | tf_op jit(solution)/shard_map/ppermute | solution.py:59
  185.8 26.5 %collective-permute-start.5 = (f32[72,256]{1,0:T(8,128)S(1)}, f32[72,256]{1,0:T(8,128)S(1)}, u32[]{:S(2)}, u32[]{:S(2)}) collective-permute-start(f32[72,256]{1,0:T(8,128)S(1)} %get-tuple-element.18), channel_id=1, source_target_pairs={{0,384},{128,0},{256,128},{384,256},{1,385},{129,1},{257,129},{385... | collective-permute-start | bytes 221192 | tf_op jit(solution)/shard_map/ppermute | solution.py:59
  187.7 31.8 %collective-permute-start.4 = (f32[72,256]{1,0:T(8,128)S(1)}, f32[72,256]{1,0:T(8,128)S(1)}, u32[]{:S(2)}, u32[]{:S(2)}) collective-permute-start(f32[72,256]{1,0:T(8,128)S(1)} %get-tuple-element.19), channel_id=1, source_target_pairs={{0,256},{128,384},{256,0},{384,128},{1,257},{129,385},{257,1},{385... | collective-permute-start | bytes 221192 | tf_op jit(solution)/shard_map/ppermute | solution.py:59
  194.8 24.7 %collective-permute-start.3 = (f32[72,256]{1,0:T(8,128)S(1)}, f32[72,256]{1,0:T(8,128)S(1)}, u32[]{:S(2)}, u32[]{:S(2)}) collective-permute-start(f32[72,256]{1,0:T(8,128)S(1)} %get-tuple-element.17), channel_id=1, source_target_pairs={{0,128},{128,256},{256,384},{384,0},{1,129},{129,257},{257,385},{3... | collective-permute-start | bytes 221192 | tf_op jit(solution)/shard_map/ppermute | solution.py:59
  199.2 21.3 %collective-permute-start.11 = (f32[72,256]{1,0:T(8,128)S(1)}, f32[72,256]{1,0:T(8,128)S(1)}, u32[]{:S(2)}, u32[]{:S(2)}) collective-permute-start(f32[72,256]{1,0:T(8,128)S(1)} %get-tuple-element.15), channel_id=1, source_target_pairs={{0,384},{128,0},{256,128},{384,256},{1,385},{129,1},{257,129},{385... | collective-permute-start | bytes 221192 | tf_op jit(solution)/shard_map/ppermute | solution.py:59
  205.3 15.2 %collective-permute-start.10 = (f32[72,256]{1,0:T(8,128)S(1)}, f32[72,256]{1,0:T(8,128)S(1)}, u32[]{:S(2)}, u32[]{:S(2)}) collective-permute-start(f32[72,256]{1,0:T(8,128)S(1)} %get-tuple-element.16), channel_id=1, source_target_pairs={{0,256},{128,384},{256,0},{384,128},{1,257},{129,385},{257,1},{385... | collective-permute-start | bytes 221192 | tf_op jit(solution)/shard_map/ppermute | solution.py:59
  212.3 14.9 %collective-permute-start.9 = (f32[72,256]{1,0:T(8,128)S(1)}, f32[72,256]{1,0:T(8,128)S(1)}, u32[]{:S(2)}, u32[]{:S(2)}) collective-permute-start(f32[72,256]{1,0:T(8,128)S(1)} %get-tuple-element.14), channel_id=1, source_target_pairs={{0,128},{128,256},{256,384},{384,0},{1,129},{129,257},{257,385},{3... | collective-permute-start | bytes 221192 | tf_op jit(solution)/shard_map/ppermute | solution.py:59

commit v10 on v8

--- a/solution.py
+++ b/solution.py
@@ -68,22 +68,24 @@
 
     n_pts, dim = points.shape
     weighted = jnp.concatenate(
-        [
-            scatter_rows(points).astype(jnp.float32) * row_scale[:, None],
-            row_scale[:, None],
-            jnp.zeros((n_pts, 7), jnp.float32),
-        ],
+        [scatter_rows(points), jnp.ones((n_pts, 1), points.dtype), jnp.zeros((n_pts, 7), points.dtype)],
         axis=1,
     )
+    scaled = kernel * row_scale[:, None]
+    high = scaled.astype(jnp.bfloat16)
+    low = (scaled - high.astype(jnp.float32)).astype(jnp.bfloat16)
     lanes = 512
     chunks = n_lists // lanes
-    product = lax.dot_general(
-        weighted,
-        kernel.reshape(n_pts, chunks, lanes),
-        (((0,), (0,)), ((), ())),
-        precision=lax.Precision.HIGH,
-        preferred_element_type=jnp.float32,
-    )
+
+    def times(part):
+        return lax.dot_general(
+            weighted,
+            part.reshape(n_pts, chunks, lanes),
+            (((0,), (0,)), ((), ())),
+            preferred_element_type=jnp.float32,
+        )
+
+    product = times(high) + times(low)
     sums = product[:dim]
     col_part = product[dim]
     blocks = lax.axis_size(PTS)

time: 222 us -> 220 us (level)
  blocking collectives: 151 us -> 165 us
  waiting for transfers between devices: 17.9 us -> 6.28 us
  matrix products: 12.5 us -> 8.11 us
  other arithmetic: 23.1 us -> 27.1 us
  starting transfers between devices: 6.96 us -> 3.68 us
    all_to_all x5 -> x6, blocking collectives: 72.2 us -> 86.3 us  [exchange_sum(): return jnp.sum(lax.all_to_all(copies, names, 0, 0), axis=0)]
    all_to_all x2 -> x1, waiting for transfers between devices: 17.9 us -> 6.28 us  [exchange_sum(): return jnp.sum(lax.all_to_all(copies, names, 0, 0), axis=0)]
    dot_general x1 -> x2, matrix products: 7.18 us -> 2.77 us  [times(): lax.dot_general(weighted, part.reshape(n_pts, chunks, lanes), (((0,), (0,...]
    convert_element_type x1, other arithmetic: 0.03 us -> 4.09 us  [local(): high = scaled.astype(jnp.bfloat16)]
    all_to_all x2 -> x1, starting transfers between devices: 6.96 us -> 3.68 us  [exchange_sum(): return jnp.sum(lax.all_to_all(copies, names, 0, 0), axis=0)]
  transfers between devices with their start and end apart: 2 -> 1, of which waited for: 2 -> 1; matrix products, arithmetic and copies ran while one was open for 0% -> 0% of each run, Pallas kernels for 0% -> 0%
where the time goes in v10:
time: 220 us; the launch traced here: 217 us
  blocking collectives  165 us (75%)
  other arithmetic  27.1 us (12%)
  matrix products  8.11 us (4%)
  waiting for transfers between devices  6.28 us (3%)
  local copies, waits for them, and re-layouts  5.9 us (3%)
  starting transfers between devices  3.68 us (2%)
    all_to_all x6, blocking collectives, exchange_sum(): return jnp.sum(lax.all_to_all(copies, names, 0, 0), axis=0)  86.3 us
    all_to_all x3, blocking collectives, sum_scatter(): value = jnp.sum(lax.all_to_all(blocks, name, 0, 0), axis=0)  78.5 us
    reduce_sum x2, other arithmetic, local(): col_scale = target / list_mass(jnp.sum(kernel * row_scale[:, None], axis=0))  7.28 us
    reduce_sum x2, other arithmetic, local(): row_scale = 1.0 / point_mass(jnp.sum(kernel * col_scale[None, :], axis=1))  6.63 us
    reduce_sum x3, other arithmetic, sum_scatter(): value = jnp.sum(lax.all_to_all(blocks, name, 0, 0), axis=0)  6.55 us
    all_to_all x1, waiting for transfers between devices, exchange_sum(): return jnp.sum(lax.all_to_all(copies, names, 0, 0), axis=0)  6.28 us
    dot_general x1, matrix products, kernel_tile(): lax.dot_general(points, cent_block, (((1,), (1,)), ((), ())), preferred_e...  5.34 us
  transfers between devices with their start and end apart: 1, of which 1 were waited for; matrix products, arithmetic and copies ran while one was open for 0% of the time, Pallas kernels for 0%

profile of v10, /device:TPU:1, one launch (start us, length us, event | category | flops | bytes accessed | tf_op | source)
XLA Modules:
  0.0 216.8 jit_solution(9742807282717976041)
XLA Ops:
  0.6 0.0 copy-start
  0.7 1.6 copy-done
  2.2 5.3 %fusion.17 = (f32[384]{0:T(512)S(1)}, f32[384,4096]{1,0:T(8,128)}) fusion(s32[4096]{0:T(1024)S(1)} %iota_add_fusion, s32[384]{0:T(512)} %param.6, bf16[384,256]{1,0:T(8,128)(2,1)} %param.4, bf16[4096,256]{1,0:T(8,128)(2,1)S(1)} %copy-done), kind=kOutput, calls=%fused_computation.33 | convolution fusion | flops 813170304 | bytes 8604672 | tf_op jit(solution)/shard_map/dot_general | solution.py:10
  7.6 0.0 copy-start.2
  7.6 15.6 %all_to_all.57 = f32[16,1,384]{2,1,0:T(1,128)S(1)} all-to-all(f32[16,1,384]{2,1,0:T(1,128)S(1)} %broadcast_in_dim.24), channel_id=1, replica_groups=mesh['z_hi'=4,'y'=4,'core'=2,'x'=4,'z_lo'=4] {'x','z_lo'}, dimensions={0} | all-to-all | bytes 49152 | tf_op jit(solution)/shard_map/all_to_all | solution.py:27
  23.3 3.6 %multiply_reduce_fusion.3 = f32[4096]{0:T(1024)S(1)} fusion(f32[384,4096]{1,0:T(8,128)} %get-tuple-element.5, f32[384]{0:T(512)S(1)} %broadcast_divide_fusion.3), kind=kLoop, calls=%fused_computation.4 | loop fusion | flops 3141632 | bytes 6309376 | tf_op jit(solution)/shard_map/reduce_sum | solution.py:66
  26.9 0.1 broadcast_in_dim.25
  27.0 11.6 %all_to_all.58 = f32[8,1,4096]{2,1,0:T(1,128)S(1)} all-to-all(f32[8,1,4096]{2,1,0:T(1,128)S(1)} %broadcast_in_dim.25), channel_id=1, replica_groups=mesh['z_hi'=4,'y'=4,'core'=2,'x'=4,'z_lo'=4] {'y','core'}, dimensions={0} | all-to-all | bytes 262144 | tf_op jit(solution)/shard_map/all_to_all | solution.py:27
  38.6 0.1 reduce_sum.138
  38.8 24.2 %all_to_all.59 = f32[4,1,4096]{2,1,0:T(1,128)S(1)} all-to-all(f32[4,1,4096]{2,1,0:T(1,128)S(1)} %broadcast_in_dim.26), channel_id=1, replica_groups=mesh['z_hi'=4,'y'=4,'core'=2,'x'=4,'z_lo'=4] {'z_hi'}, dimensions={0} | all-to-all | bytes 131072 | tf_op jit(solution)/shard_map/all_to_all | solution.py:27
  63.0 0.1 reduce_sum.139
  63.1 0.0 copy-done.2
  63.1 3.3 %multiply_reduce_fusion.2 = f32[384]{0:T(512)S(1)} fusion(f32[384,4096]{1,0:T(8,128)} %get-tuple-element.5, f32[4096]{0:T(1024)S(1)} %fusion.14), kind=kLoop, calls=%fused_computation.3 | loop fusion | flops 3145344 | bytes 6309376 | tf_op jit(solution)/shard_map/reduce_sum | solution.py:65
  66.5 9.4 %all_to_all.60 = f32[16,1,384]{2,1,0:T(1,128)S(1)} all-to-all(f32[16,1,384]{2,1,0:T(1,128)S(1)} %broadcast_in_dim.27), channel_id=1, replica_groups=mesh['z_hi'=4,'y'=4,'core'=2,'x'=4,'z_lo'=4] {'x','z_lo'}, dimensions={0} | all-to-all | bytes 49152 | tf_op jit(solution)/shard_map/all_to_all | solution.py:27
  75.9 3.6 %multiply_reduce_fusion.1 = f32[4096]{0:T(1024)S(1)} fusion(f32[384,4096]{1,0:T(8,128)} %get-tuple-element.5, f32[384]{0:T(512)S(1)} %broadcast_divide_fusion.2), kind=kLoop, calls=%fused_computation.2 | loop fusion | flops 3141632 | bytes 6309376 | tf_op jit(solution)/shard_map/reduce_sum | solution.py:66
  79.5 0.0 copy-start.1
  79.6 0.1 broadcast_in_dim.28
  79.6 11.4 %all_to_all.61 = f32[8,1,4096]{2,1,0:T(1,128)S(1)} all-to-all(f32[8,1,4096]{2,1,0:T(1,128)S(1)} %broadcast_in_dim.28), channel_id=1, replica_groups=mesh['z_hi'=4,'y'=4,'core'=2,'x'=4,'z_lo'=4] {'y','core'}, dimensions={0} | all-to-all | bytes 262144 | tf_op jit(solution)/shard_map/all_to_all | solution.py:27
  91.0 0.1 reduce_sum.143
  91.1 14.1 %all_to_all.62 = f32[4,1,4096]{2,1,0:T(1,128)S(1)} all-to-all(f32[4,1,4096]{2,1,0:T(1,128)S(1)} %broadcast_in_dim.29), channel_id=1, replica_groups=mesh['z_hi'=4,'y'=4,'core'=2,'x'=4,'z_lo'=4] {'z_hi'}, dimensions={0} | all-to-all | bytes 131072 | tf_op jit(solution)/shard_map/all_to_all | solution.py:27
  105.2 0.1 reduce_sum.144
  105.3 3.3 %multiply_reduce_fusion = f32[384]{0:T(512)S(1)} fusion(f32[384,4096]{1,0:T(8,128)} %get-tuple-element.5, f32[4096]{0:T(1024)S(1)} %fusion.13), kind=kLoop, calls=%fused_computation.1 | loop fusion | flops 3145344 | bytes 6309376 | tf_op jit(solution)/shard_map/reduce_sum | solution.py:67
  108.6 0.6 broadcast_in_dim.30
  109.2 3.7 %all-to-all-start.6 = ((f32[16,1,384]{2,1,0:T(1,128)}), f32[16,1,384]{2,1,0:T(1,128)S(1)}, u32[]{:S(2)}, u32[]{:S(2)}) async-start(f32[16,1,384]{2,1,0:T(1,128)} %broadcast_in_dim.30), calls=%async_computation.6 | async-start | bytes 49152 | tf_op jit(solution)/shard_map/all_to_all | solution.py:27
  112.9 0.0 copy-done.1
  112.9 0.2 copy.19
  113.1 0.1 pad.4.clone
  113.2 6.3 %all-to-all-done.6 = f32[16,1,384]{2,1,0:T(1,128)S(1)} async-done(((f32[16,1,384]{2,1,0:T(1,128)}), f32[16,1,384]{2,1,0:T(1,128)S(1)}, u32[]{:S(2)}, u32[]{:S(2)}) %all-to-all-start.6) | async-done | bytes 24608 | tf_op jit(solution)/shard_map/all_to_all | solution.py:27
  119.5 4.1 %multiply_convert_fusion = (bf16[384,4096]{1,0:T(8,128)(2,1)S(1)}, bf16[384,4096]{1,0:T(8,128)(2,1)S(1)}) fusion(f32[384,4096]{1,0:T(8,128)} %get-tuple-element.5, f32[384]{0:T(512)S(1)} %broadcast_divide_fusion.1), kind=kLoop, calls=%fused_computation.6 | loop fusion | flops 7864320 | bytes 12584448 | tf_op jit(solution)/shard_map/convert_element_type | solution.py:75
  123.6 1.3 fusion
  125.0 1.4 fusion.6
  126.4 0.6 slice.16
  127.1 2.4 %copy.30 = f32[256,8,512]{2,1,0:T(8,128)S(1)} copy(f32[256,8,512]{2,0,1:T(8,128)S(1)} %slice.16) | data formatting | bytes 8388608 | tf_op jit(solution)/shard_map/slice | solution.py:89
  129.5 0.1 broadcast_in_dim.32
  129.6 0.8 pad_maximum_fusion
  130.3 11.7 %all_to_all.63 = f32[2,1152,512]{2,1,0:T(8,128)} all-to-all(f32[2,1152,512]{2,1,0:T(8,128)S(1)} %bitcast.31), channel_id=1, replica_groups=mesh['z_hi'=4,'y'=4,'core'=2,'x'=4,'z_lo'=4] {'core'}, dimensions={0} | all-to-all | bytes 9437184 | tf_op jit(solution)/shard_map/all_to_all | solution.py:50
  142.1 4.5 %reduce_sum.147 = f32[1152,512]{1,0:T(8,128)} reduce(f32[2,1152,512]{2,1,0:T(8,128)} %all_to_all.63, f32[]{:T(128)} %constant.23.clone.1), dimensions={0}, to_apply=%region_12.0 | reduce | flops 589824 | bytes 7077892 | tf_op jit(solution)/shard_map/reduce_sum | solution.py:50
  146.6 33.4 %all_to_all.64 = f32[4,288,512]{2,1,0:T(8,128)} all-to-all(f32[4,288,512]{2,1,0:T(8,128)} %bitcast.35), channel_id=1, replica_groups=mesh['z_hi'=4,'y'=4,'core'=2,'x'=4,'z_lo'=4] {'y'}, dimensions={0} | all-to-all | bytes 4718592 | tf_op jit(solution)/shard_map/all_to_all | solution.py:50
  179.9 2.0 reduce_sum.148
  181.9 33.4 %all_to_all.65 = f32[4,72,512]{2,1,0:T(8,128)S(1)} all-to-all(f32[4,72,512]{2,1,0:T(8,128)S(1)} %bitcast.36), channel_id=1, replica_groups=mesh['z_hi'=4,'y'=4,'core'=2,'x'=4,'z_lo'=4] {'z_hi'}, dimensions={0} | all-to-all | bytes 1179648 | tf_op jit(solution)/shard_map/all_to_all | solution.py:50
  215.5 0.6 divide_log_fusion
  216.1 0.7 broadcast_divide_fusion
  (23 shorter events, 0.4 us)
Async XLA Ops:
  0.6 1.6 copy-start
  7.6 55.5 %copy-start.2 = (s32[4096]{0:T(1024)S(1)}, s32[4096]{0:T(1024)}, u32[]{:S(2)}) copy-start(s32[4096]{0:T(1024)} %param.7) | copy-start | bytes 49156
  79.5 33.3 %copy-start.1 = (bf16[384,256]{1,0:T(8,128)(2,1)S(1)}, bf16[384,256]{1,0:T(8,128)(2,1)}, u32[]{:S(2)}) copy-start(bf16[384,256]{1,0:T(8,128)(2,1)} %param.4) | copy-start | bytes 589828
  109.2 10.3 %all-to-all-start.6 = ((f32[16,1,384]{2,1,0:T(1,128)}), f32[16,1,384]{2,1,0:T(1,128)S(1)}, u32[]{:S(2)}, u32[]{:S(2)}) async-start(f32[16,1,384]{2,1,0:T(1,128)} %broadcast_in_dim.30), calls=%async_computation.6 | async-start | bytes 49152 | tf_op jit(solution)/shard_map/all_to_all | solution.py:27

commit v11 on v8

--- a/solution.py
+++ b/solution.py
@@ -58,13 +58,29 @@
     total_lists = n_lists * lax.axis_size(LISTS)
     target = loads.astype(jnp.float32) * (total_pts / (8.0 * total_lists))
 
-    kernel = kernel_tile(points, centroids, prior, offset)
+    pieces = 2
+    width = n_lists // pieces
+    kernel = [
+        kernel_tile(points, centroids[part * width : (part + 1) * width], prior, offset + part * width)
+        for part in range(pieces)
+    ]
+    lanes = 512
+    chunks = n_lists // lanes
+
+    def row_totals(col_scale):
+        return sum(
+            jnp.sum(block * col_scale[None, part * width : (part + 1) * width], axis=1)
+            for part, block in enumerate(kernel)
+        )
+
+    def col_totals(row_scale):
+        return jnp.concatenate([jnp.sum(block * row_scale[:, None], axis=0) for block in kernel])
 
     col_scale = jnp.ones((n_lists,), jnp.float32)
     for step in range(ITERS - 1):
-        row_scale = 1.0 / point_mass(jnp.sum(kernel * col_scale[None, :], axis=1))
-        col_scale = target / list_mass(jnp.sum(kernel * row_scale[:, None], axis=0))
-    row_scale = 1.0 / point_mass(jnp.sum(kernel * col_scale[None, :], axis=1))
+        row_scale = 1.0 / point_mass(row_totals(col_scale))
+        col_scale = target / list_mass(col_totals(row_scale))
+    row_scale = 1.0 / point_mass(row_totals(col_scale))
 
     n_pts, dim = points.shape
     weighted = jnp.concatenate(
@@ -75,14 +91,18 @@
         ],
         axis=1,
     )
-    lanes = 512
-    chunks = n_lists // lanes
-    product = lax.dot_general(
-        weighted,
-        kernel.reshape(n_pts, chunks, lanes),
-        (((0,), (0,)), ((), ())),
-        precision=lax.Precision.HIGH,
-        preferred_element_type=jnp.float32,
+    product = jnp.concatenate(
+        [
+            lax.dot_general(
+                weighted,
+                block.reshape(n_pts, width // lanes, lanes),
+                (((0,), (0,)), ((), ())),
+                precision=lax.Precision.HIGH,
+                preferred_element_type=jnp.float32,
+            )
+            for block in kernel
+        ],
+        axis=1,
     )
     sums = product[:dim]
     col_part = product[dim]

time: 222 us -> 214 us (0.964)
  other arithmetic: 23.1 us -> 18.6 us
  matrix products: 12.5 us -> 9.96 us
    reduce_sum x4 -> x5, other arithmetic: 13.9 us -> 8.33 us  [the longest x2 5.34 us: col_totals(): jnp.sum(block * row_scale[:, None], axis=0)]
    dot_general x1 -> x2, matrix products: 7.18 us -> 4.96 us  [local(): lax.dot_general(weighted, block.reshape(n_pts, width // lanes, lanes), ((...]
    dot_general x1 -> x2, matrix products: 5.34 us -> 5 us  [kernel_tile(): lax.dot_general(points, cent_block, (((1,), (1,)), ((), ())), preferred_e...]
  transfers between devices with their start and end apart: 2 -> 2, of which waited for: 2 -> 2; matrix products, arithmetic and copies ran while one was open for 0% -> 1% of each run, Pallas kernels for 0% -> 0%
where the time goes in v11:
time: 214 us; the launch traced here: 210 us
  blocking collectives  149 us (70%)
  other arithmetic  18.6 us (9%)
  waiting for transfers between devices  16.4 us (8%)
  matrix products  9.96 us (5%)
  starting transfers between devices  7.59 us (4%)
  local copies, waits for them, and re-layouts  7.41 us (3%)
    all_to_all x3, blocking collectives, sum_scatter(): value = jnp.sum(lax.all_to_all(blocks, name, 0, 0), axis=0)  77.1 us
    all_to_all x5, blocking collectives, exchange_sum(): return jnp.sum(lax.all_to_all(copies, names, 0, 0), axis=0)  72.2 us
    all_to_all x2, waiting for transfers between devices, exchange_sum(): return jnp.sum(lax.all_to_all(copies, names, 0, 0), axis=0)  16.4 us
    all_to_all x2, starting transfers between devices, exchange_sum(): return jnp.sum(lax.all_to_all(copies, names, 0, 0), axis=0)  7.59 us
    reduce_sum x2, other arithmetic, col_totals(): jnp.sum(block * row_scale[:, None], axis=0)  5.34 us
    reduce_sum x3, other arithmetic, sum_scatter(): value = jnp.sum(lax.all_to_all(blocks, name, 0, 0), axis=0)  5.11 us
    dot_general x2, matrix products, kernel_tile(): lax.dot_general(points, cent_block, (((1,), (1,)), ((), ())), preferred_e...  5 us
    dot_general x2, matrix products, local(): lax.dot_general(weighted, block.reshape(n_pts, width // lanes, lanes), ((...  4.96 us
  transfers between devices with their start and end apart: 2, of which 2 were waited for; matrix products, arithmetic and copies ran while one was open for 1% of the time, Pallas kernels for 0%

profile of v11, /device:TPU:1, one launch (start us, length us, event | category | flops | bytes accessed | tf_op | source)
XLA Modules:
  0.0 210.4 jit_solution(16777460768112090584)
XLA Ops:
  0.7 0.0 copy-start.2
  0.7 0.0 copy-start.5
  0.7 0.0 copy-start.6
  0.7 2.4 %fusion.18 = (f32[384]{0:T(512)S(1)}, f32[384,2048]{1,0:T(8,128)S(1)}) fusion(s32[2048]{0:T(1024)S(1)} %iota_add_fusion, s32[384]{0:T(512)} %param.6, bf16[384,256]{1,0:T(8,128)(2,1)} %param.4, bf16[4096,256]{1,0:T(8,128)(2,1)} %param.5), kind=kOutput, calls=%fused_computation.47 | convolution fusion | flops 406584960 | bytes 4402688 | tf_op jit(solution)/shard_map/dot_general | solution.py:10
  3.1 0.0 copy-done.5
  3.1 0.0 copy-done.6
  3.1 2.6 %fusion.17 = (f32[384]{0:T(512)S(1)}, f32[384,2048]{1,0:T(8,128)}) fusion(s32[2048]{0:T(1024)S(1)} %iota_add_fusion.1, s32[384]{0:T(512)S(1)} %copy-done.6, bf16[384,256]{1,0:T(8,128)(2,1)S(1)} %copy-done.2, bf16[4096,256]{1,0:T(8,128)(2,1)S(1)} %copy-done.5), kind=kOutput, calls=%fused_computation.46 | convolution fusion | flops 406584960 | bytes 4402688 | tf_op jit(solution)/shard_map/dot_general | solution.py:10
  5.8 15.6 %all_to_all.57 = f32[16,1,384]{2,1,0:T(1,128)S(1)} all-to-all(f32[16,1,384]{2,1,0:T(1,128)S(1)} %broadcast_in_dim.20), channel_id=1, replica_groups=mesh['z_hi'=4,'y'=4,'core'=2,'x'=4,'z_lo'=4] {'x','z_lo'}, dimensions={0} | all-to-all | bytes 49152 | tf_op jit(solution)/shard_map/all_to_all | solution.py:27
  21.5 2.7 %multiply_reduce_fusion.7 = (f32[2048]{0:T(1024)S(1)}, f32[2048]{0:T(1024)S(1)}) fusion(f32[384,2048]{1,0:T(8,128)} %get-tuple-element.11, f32[384]{0:T(512)S(1)} %broadcast_divide_fusion.3, f32[384,2048]{1,0:T(8,128)S(1)} %get-tuple-element.13), kind=kLoop, calls=%fused_computation.17 | loop fusion | flops 3141632 | bytes 6309376 | tf_op jit(solution)/shard_map/reduce_sum | solution.py:77
  24.1 0.1 broadcast_in_dim.21
  24.2 11.6 %all_to_all.58 = f32[8,1,4096]{2,1,0:T(1,128)S(1)} all-to-all(f32[8,1,4096]{2,1,0:T(1,128)S(1)} %broadcast_in_dim.21), channel_id=1, replica_groups=mesh['z_hi'=4,'y'=4,'core'=2,'x'=4,'z_lo'=4] {'y','core'}, dimensions={0} | all-to-all | bytes 262144 | tf_op jit(solution)/shard_map/all_to_all | solution.py:27
  35.9 0.1 reduce_sum.185
  36.0 24.2 %all_to_all.59 = f32[4,1,4096]{2,1,0:T(1,128)S(1)} all-to-all(f32[4,1,4096]{2,1,0:T(1,128)S(1)} %broadcast_in_dim.22), channel_id=1, replica_groups=mesh['z_hi'=4,'y'=4,'core'=2,'x'=4,'z_lo'=4] {'z_hi'}, dimensions={0} | all-to-all | bytes 131072 | tf_op jit(solution)/shard_map/all_to_all | solution.py:27
  60.2 0.1 reduce_sum.186
  60.3 2.4 %multiply_reduce_fusion.4 = (f32[384]{0:T(512)S(1)}, f32[384]{0:T(512)S(1)}) fusion(f32[384,2048]{1,0:T(8,128)S(1)} %get-tuple-element.13, f32[2048]{0:T(1024)S(1)} %get-tuple-element.8, f32[384,2048]{1,0:T(8,128)} %get-tuple-element.11, f32[2048]{0:T(1024)S(1)} %get-tuple-element.9), kind=kLoop, calls=%fused_computation.14 | loop fusion | flops 3144960 | bytes 6310912 | tf_op jit(solution)/shard_map/reduce_sum | solution.py:72
  62.8 9.4 %all_to_all.60 = f32[16,1,384]{2,1,0:T(1,128)S(1)} all-to-all(f32[16,1,384]{2,1,0:T(1,128)S(1)} %broadcast_in_dim.23), channel_id=1, replica_groups=mesh['z_hi'=4,'y'=4,'core'=2,'x'=4,'z_lo'=4] {'x','z_lo'}, dimensions={0} | all-to-all | bytes 49152 | tf_op jit(solution)/shard_map/all_to_all | solution.py:27
  72.2 2.7 %multiply_reduce_fusion.3 = (f32[2048]{0:T(1024)S(1)}, f32[2048]{0:T(1024)S(1)}) fusion(f32[384,2048]{1,0:T(8,128)} %get-tuple-element.11, f32[384]{0:T(512)S(1)} %broadcast_divide_fusion.2, f32[384,2048]{1,0:T(8,128)S(1)} %get-tuple-element.13), kind=kLoop, calls=%fused_computation.13 | loop fusion | flops 3141632 | bytes 6309376 | tf_op jit(solution)/shard_map/reduce_sum | solution.py:77
  74.9 0.1 broadcast_in_dim.24
  74.9 11.4 %all_to_all.61 = f32[8,1,4096]{2,1,0:T(1,128)S(1)} all-to-all(f32[8,1,4096]{2,1,0:T(1,128)S(1)} %broadcast_in_dim.24), channel_id=1, replica_groups=mesh['z_hi'=4,'y'=4,'core'=2,'x'=4,'z_lo'=4] {'y','core'}, dimensions={0} | all-to-all | bytes 262144 | tf_op jit(solution)/shard_map/all_to_all | solution.py:27
  86.3 0.1 reduce_sum.192
  86.4 0.7 broadcast_in_dim.25
  87.1 3.3 %all-to-all-start.5 = ((f32[4,1,4096]{2,1,0:T(1,128)}), f32[4,1,4096]{2,1,0:T(1,128)S(1)}, u32[]{:S(2)}, u32[]{:S(2)}) async-start(f32[4,1,4096]{2,1,0:T(1,128)} %broadcast_in_dim.25), calls=%async_computation.5 | async-start | bytes 131072 | tf_op jit(solution)/shard_map/all_to_all | solution.py:27
  90.4 1.1 copy.19
  91.5 10.6 %all-to-all-done.5 = f32[4,1,4096]{2,1,0:T(1,128)S(1)} async-done(((f32[4,1,4096]{2,1,0:T(1,128)}), f32[4,1,4096]{2,1,0:T(1,128)S(1)}, u32[]{:S(2)}, u32[]{:S(2)}) %all-to-all-start.5) | async-done | bytes 65568 | tf_op jit(solution)/shard_map/all_to_all | solution.py:27
  102.0 0.1 reduce_sum.193
  102.1 0.0 copy-start
  102.1 0.3 multiply_reduce_fusion
  102.4 1.6 copy-done
  104.0 0.3 multiply_reduce_fusion.1
  104.3 0.6 broadcast_in_dim.26
  104.9 4.3 %all-to-all-start.6 = ((f32[16,1,384]{2,1,0:T(1,128)}), f32[16,1,384]{2,1,0:T(1,128)}, u32[]{:S(2)}, u32[]{:S(2)}) async-start(f32[16,1,384]{2,1,0:T(1,128)} %broadcast_in_dim.26), calls=%async_computation.6 | async-start | bytes 49152 | tf_op jit(solution)/shard_map/all_to_all | solution.py:27
  109.3 0.7 pad.6.clone
  110.0 5.9 %all-to-all-done.6 = f32[16,1,384]{2,1,0:T(1,128)} async-done(((f32[16,1,384]{2,1,0:T(1,128)}), f32[16,1,384]{2,1,0:T(1,128)}, u32[]{:S(2)}, u32[]{:S(2)}) %all-to-all-start.6) | async-done | bytes 24608 | tf_op jit(solution)/shard_map/all_to_all | solution.py:27
  115.9 1.3 reduce_sum.196
  117.2 0.7 broadcast_divide_fusion.1
  117.9 2.9 %fusion.1 = f32[264,4,512]{2,0,1:T(8,128)S(1)} fusion(f32[48,4,8,512]{3,2,1,0:T(8,128)S(1)} %bitcast.30, f32[384,1]{0,1:T(1,128)S(1)} %div.52, f32[384,256]{0,1:T(8,128)S(1)} %bitcast_multiply_fusion, f32[264]{0:T(512)} %pad.6.clone), kind=kOutput, calls=%fused_computation.4 | convolution fusion | flops 1245911040 | bytes 5704224 | tf_op jit(solution)/shard_map/dot_general | solution.py:96
  120.8 2.1 %fusion.4 = f32[264,4,512]{2,0,1:T(8,128)S(1)} fusion(f32[48,4,8,512]{3,2,1,0:T(8,128)S(1)} %bitcast.31, f32[384,1]{0,1:T(1,128)S(1)} %div.52, f32[384,256]{0,1:T(8,128)S(1)} %bitcast_multiply_fusion, f32[264]{0:T(512)S(1)} %copy-done.4), kind=kOutput, calls=%fused_computation.7 | convolution fusion | flops 1245911040 | bytes 5704224 | tf_op jit(solution)/shard_map/dot_general | solution.py:96
  123.0 0.6 fusion
  123.5 2.4 %copy.30 = f32[256,8,512]{2,1,0:T(8,128)S(1)} copy(f32[256,8,512]{2,0,1:T(8,128)S(1)} %fusion) | data formatting | bytes 8388608 | tf_op jit(solution)/shard_map/slice | solution.py:107
  126.0 0.1 broadcast_in_dim.29
  126.0 0.8 pad_maximum_fusion
  126.8 11.6 %all_to_all.62 = f32[2,1152,512]{2,1,0:T(8,128)} all-to-all(f32[2,1152,512]{2,1,0:T(8,128)S(1)} %bitcast.32), channel_id=1, replica_groups=mesh['z_hi'=4,'y'=4,'core'=2,'x'=4,'z_lo'=4] {'core'}, dimensions={0} | all-to-all | bytes 9437184 | tf_op jit(solution)/shard_map/all_to_all | solution.py:50
  138.4 3.1 %reduce_sum.197 = f32[1152,512]{1,0:T(8,128)S(1)} reduce(f32[2,1152,512]{2,1,0:T(8,128)} %all_to_all.62, f32[]{:T(128)} %constant.23.clone.1), dimensions={0}, to_apply=%region_17.0 | reduce | flops 589824 | bytes 7077892 | tf_op jit(solution)/shard_map/reduce_sum | solution.py:50
  141.5 32.1 %all_to_all.63 = f32[4,288,512]{2,1,0:T(8,128)} all-to-all(f32[4,288,512]{2,1,0:T(8,128)S(1)} %bitcast.34), channel_id=1, replica_groups=mesh['z_hi'=4,'y'=4,'core'=2,'x'=4,'z_lo'=4] {'y'}, dimensions={0} | all-to-all | bytes 4718592 | tf_op jit(solution)/shard_map/all_to_all | solution.py:50
  173.6 2.0 reduce_sum.198
  175.6 33.4 %all_to_all.64 = f32[4,72,512]{2,1,0:T(8,128)S(1)} all-to-all(f32[4,72,512]{2,1,0:T(8,128)S(1)} %bitcast.35), channel_id=1, replica_groups=mesh['z_hi'=4,'y'=4,'core'=2,'x'=4,'z_lo'=4] {'z_hi'}, dimensions={0} | all-to-all | bytes 1179648 | tf_op jit(solution)/shard_map/all_to_all | solution.py:50
  209.1 0.6 divide_log_fusion
  209.7 0.7 broadcast_divide_fusion
  (37 shorter events, 0.4 us)
Async XLA Ops:
  0.7 2.4 %copy-start.2 = (bf16[384,256]{1,0:T(8,128)(2,1)S(1)}, bf16[384,256]{1,0:T(8,128)(2,1)}, u32[]{:S(2)}) copy-start(bf16[384,256]{1,0:T(8,128)(2,1)} %param.4) | copy-start | bytes 589828
  0.7 2.4 %copy-start.5 = (bf16[4096,256]{1,0:T(8,128)(2,1)S(1)}, bf16[4096,256]{1,0:T(8,128)(2,1)}, u32[]{:S(2)}) copy-start(bf16[4096,256]{1,0:T(8,128)(2,1)} %param.5) | copy-start | bytes 6291460
  0.7 2.4 %copy-start.6 = (s32[384]{0:T(512)S(1)}, s32[384]{0:T(512)}, u32[]{:S(2)}) copy-start(s32[384]{0:T(512)} %param.6) | copy-start | bytes 4612
  21.4 38.8 %copy-start.3 = (s32[4096]{0:T(1024)S(1)}, s32[4096]{0:T(1024)}, u32[]{:S(2)}) copy-start(s32[4096]{0:T(1024)} %param.7) | copy-start | bytes 49156
  87.1 14.9 %all-to-all-start.5 = ((f32[4,1,4096]{2,1,0:T(1,128)}), f32[4,1,4096]{2,1,0:T(1,128)S(1)}, u32[]{:S(2)}, u32[]{:S(2)}) async-start(f32[4,1,4096]{2,1,0:T(1,128)} %broadcast_in_dim.25), calls=%async_computation.5 | async-start | bytes 131072 | tf_op jit(solution)/shard_map/all_to_all | solution.py:27
  102.1 1.9 copy-start
  104.9 11.0 %all-to-all-start.6 = ((f32[16,1,384]{2,1,0:T(1,128)}), f32[16,1,384]{2,1,0:T(1,128)}, u32[]{:S(2)}, u32[]{:S(2)}) async-start(f32[16,1,384]{2,1,0:T(1,128)} %broadcast_in_dim.26), calls=%async_computation.6 | async-start | bytes 49152 | tf_op jit(solution)/shard_map/all_to_all | solution.py:27
  117.9 2.9 %copy-start.1 = (f32[384,2048]{1,0:T(8,128)S(1)}, f32[384,2048]{1,0:T(8,128)}, u32[]{:S(2)}) copy-start(f32[384,2048]{1,0:T(8,128)} %get-tuple-element.11) | copy-start | bytes 9437188
  117.9 2.9 %copy-start.4 = (f32[264]{0:T(512)S(1)}, f32[264]{0:T(512)}, u32[]{:S(2)}) copy-start(f32[264]{0:T(512)} %pad.6.clone) | copy-start | bytes 3172

commit v12 on v11

--- a/solution.py
+++ b/solution.py
@@ -80,7 +80,10 @@
     for step in range(ITERS - 1):
         row_scale = 1.0 / point_mass(row_totals(col_scale))
         col_scale = target / list_mass(col_totals(row_scale))
-    row_scale = 1.0 / point_mass(row_totals(col_scale))
+    last_rows = row_totals(col_scale)
+    high = lax.optimization_barrier([block.astype(jnp.bfloat16) for block in kernel])
+    low = [(block - part.astype(jnp.float32)).astype(jnp.bfloat16) for block, part in zip(kernel, high)]
+    row_scale = 1.0 / point_mass(last_rows)
 
     n_pts, dim = points.shape
     weighted = jnp.concatenate(
@@ -91,16 +94,21 @@
         ],
         axis=1,
     )
+    weighted_high = lax.optimization_barrier(weighted.astype(jnp.bfloat16))
+    weighted_low = (weighted - weighted_high.astype(jnp.float32)).astype(jnp.bfloat16)
+
+    def times(left, right):
+        return lax.dot_general(
+            left,
+            right.reshape(n_pts, right.shape[1] // lanes, lanes),
+            (((0,), (0,)), ((), ())),
+            preferred_element_type=jnp.float32,
+        )
+
     product = jnp.concatenate(
         [
-            lax.dot_general(
-                weighted,
-                block.reshape(n_pts, width // lanes, lanes),
-                (((0,), (0,)), ((), ())),
-                precision=lax.Precision.HIGH,
-                preferred_element_type=jnp.float32,
-            )
-            for block in kernel
+            times(weighted_high, big) + times(weighted_high, small) + times(weighted_low, big)
+            for big, small in zip(high, low)
         ],
         axis=1,
     )

time: 214 us -> 219 us (1.023)
  other arithmetic: 18.6 us -> 24.8 us
    convert_element_type x0 -> x3, other arithmetic: none -> 5.83 us  [the longest x2 5.73 us: local(): (block - part.astype(jnp.float32)).astype(jnp.bfloat16)]
    reduce_sum x2, other arithmetic: 5.34 us -> 8.2 us  [col_totals(): jnp.sum(block * row_scale[:, None], axis=0)]
    dot_general x2 -> x6, matrix products: 4.96 us -> 4.56 us  [times(): lax.dot_general(left, right.reshape(n_pts, right.shape[1] // lanes, lanes...]
where the time goes in v12:
time: 219 us; the launch traced here: 215 us
  blocking collectives  150 us (68%)
  other arithmetic  24.8 us (11%)
  waiting for transfers between devices  17 us (8%)
  matrix products  9.56 us (4%)
  starting transfers between devices  6.96 us (3%)
  local copies, waits for them, and re-layouts  6.53 us (3%)
    all_to_all x3, blocking collectives, sum_scatter(): value = jnp.sum(lax.all_to_all(blocks, name, 0, 0), axis=0)  77.3 us
    all_to_all x5, blocking collectives, exchange_sum(): return jnp.sum(lax.all_to_all(copies, names, 0, 0), axis=0)  72.2 us
    all_to_all x2, waiting for transfers between devices, exchange_sum(): return jnp.sum(lax.all_to_all(copies, names, 0, 0), axis=0)  17 us
    reduce_sum x2, other arithmetic, col_totals(): jnp.sum(block * row_scale[:, None], axis=0)  8.2 us
    all_to_all x2, starting transfers between devices, exchange_sum(): return jnp.sum(lax.all_to_all(copies, names, 0, 0), axis=0)  6.96 us
    convert_element_type x2, other arithmetic, local(): (block - part.astype(jnp.float32)).astype(jnp.bfloat16)  5.73 us
    reduce_sum x3, other arithmetic, sum_scatter(): value = jnp.sum(lax.all_to_all(blocks, name, 0, 0), axis=0)  5.11 us
    dot_general x2, matrix products, kernel_tile(): lax.dot_general(points, cent_block, (((1,), (1,)), ((), ())), preferred_e...  5 us
  transfers between devices with their start and end apart: 2, of which 2 were waited for; matrix products, arithmetic and copies ran while one was open for 1% of the time, Pallas kernels for 0%

profile of v12, /device:TPU:1, one launch (start us, length us, event | category | flops | bytes accessed | tf_op | source)
XLA Modules:
  0.0 215.4 jit_solution(2617111345747158515)
XLA Ops:
  0.7 0.0 copy-start.7
  0.7 4.0 %fusion.31 = (f32[384]{0:T(512)S(1)}, f32[384,2048]{1,0:T(8,128)}) fusion(s32[2048]{0:T(1024)S(1)} %iota_add_fusion.1, s32[384]{0:T(512)} %param.6, bf16[384,256]{1,0:T(8,128)(2,1)} %param.4, bf16[4096,256]{1,0:T(8,128)(2,1)} %param.5), kind=kOutput, calls=%fused_computation.63 | convolution fusion | flops 406584960 | bytes 4402688 | tf_op jit(solution)/shard_map/dot_general | solution.py:10
  4.7 1.0 fusion.32
  5.7 15.6 %all_to_all.57 = f32[16,1,384]{2,1,0:T(1,128)S(1)} all-to-all(f32[16,1,384]{2,1,0:T(1,128)S(1)} %broadcast_in_dim.20), channel_id=1, replica_groups=mesh['z_hi'=4,'y'=4,'core'=2,'x'=4,'z_lo'=4] {'x','z_lo'}, dimensions={0} | all-to-all | bytes 49152 | tf_op jit(solution)/shard_map/all_to_all | solution.py:27
  21.4 2.7 %multiply_reduce_fusion.7 = (f32[2048]{0:T(1024)S(1)}, f32[2048]{0:T(1024)S(1)}) fusion(f32[384,2048]{1,0:T(8,128)} %get-tuple-element.21, f32[384]{0:T(512)S(1)} %broadcast_divide_fusion.3, f32[384,2048]{1,0:T(8,128)S(1)} %get-tuple-element.23), kind=kLoop, calls=%fused_computation.13 | loop fusion | flops 3141632 | bytes 6309376 | tf_op jit(solution)/shard_map/reduce_sum | solution.py:77
  24.1 0.1 broadcast_in_dim.21
  24.2 11.7 %all_to_all.58 = f32[8,1,4096]{2,1,0:T(1,128)S(1)} all-to-all(f32[8,1,4096]{2,1,0:T(1,128)S(1)} %broadcast_in_dim.21), channel_id=1, replica_groups=mesh['z_hi'=4,'y'=4,'core'=2,'x'=4,'z_lo'=4] {'y','core'}, dimensions={0} | all-to-all | bytes 262144 | tf_op jit(solution)/shard_map/all_to_all | solution.py:27
  35.9 0.1 reduce_sum.185
  36.0 24.2 %all_to_all.59 = f32[4,1,4096]{2,1,0:T(1,128)S(1)} all-to-all(f32[4,1,4096]{2,1,0:T(1,128)S(1)} %broadcast_in_dim.22), channel_id=1, replica_groups=mesh['z_hi'=4,'y'=4,'core'=2,'x'=4,'z_lo'=4] {'z_hi'}, dimensions={0} | all-to-all | bytes 131072 | tf_op jit(solution)/shard_map/all_to_all | solution.py:27
  60.2 0.1 reduce_sum.186
  60.3 2.4 %multiply_reduce_fusion.4 = (f32[384]{0:T(512)S(1)}, f32[384]{0:T(512)S(1)}) fusion(f32[384,2048]{1,0:T(8,128)S(1)} %get-tuple-element.23, f32[2048]{0:T(1024)S(1)} %get-tuple-element.18, f32[384,2048]{1,0:T(8,128)} %get-tuple-element.21, f32[2048]{0:T(1024)S(1)} %get-tuple-element.19), kind=kLoop, calls=%fused_computation.10 | loop fusion | flops 3144960 | bytes 6310912 | tf_op jit(solution)/shard_map/reduce_sum | solution.py:72
  62.7 9.4 %all_to_all.60 = f32[16,1,384]{2,1,0:T(1,128)S(1)} all-to-all(f32[16,1,384]{2,1,0:T(1,128)S(1)} %broadcast_in_dim.23), channel_id=1, replica_groups=mesh['z_hi'=4,'y'=4,'core'=2,'x'=4,'z_lo'=4] {'x','z_lo'}, dimensions={0} | all-to-all | bytes 49152 | tf_op jit(solution)/shard_map/all_to_all | solution.py:27
  72.2 5.5 %multiply_reduce_fusion.3 = (f32[2048]{0:T(1024)S(1)}, f32[2048]{0:T(1024)S(1)}, bf16[384,2048]{1,0:T(8,128)(2,1)}, bf16[384,2048]{1,0:T(8,128)(2,1)}) fusion(f32[384,2048]{1,0:T(8,128)} %get-tuple-element.21, f32[384]{0:T(512)S(1)} %broadcast_divide_fusion.2, f32[384,2048]{1,0:T(8,128)S(1)} %get-tuple-element.23), kind=kLoop, calls=%fused_computation.9 | loop fusion | flops 4714496 | bytes 9455104 | tf_op jit(solution)/shard_map/reduce_sum | solution.py:77
  77.7 0.1 broadcast_in_dim.24
  77.8 11.4 %all_to_all.61 = f32[8,1,4096]{2,1,0:T(1,128)S(1)} all-to-all(f32[8,1,4096]{2,1,0:T(1,128)S(1)} %broadcast_in_dim.24), channel_id=1, replica_groups=mesh['z_hi'=4,'y'=4,'core'=2,'x'=4,'z_lo'=4] {'y','core'}, dimensions={0} | all-to-all | bytes 262144 | tf_op jit(solution)/shard_map/all_to_all | solution.py:27
  89.1 0.1 reduce_sum.192
  89.2 0.7 broadcast_in_dim.25
  89.9 3.3 %all-to-all-start.5 = ((f32[4,1,4096]{2,1,0:T(1,128)}), f32[4,1,4096]{2,1,0:T(1,128)S(1)}, u32[]{:S(2)}, u32[]{:S(2)}) async-start(f32[4,1,4096]{2,1,0:T(1,128)} %broadcast_in_dim.25), calls=%async_computation.5 | async-start | bytes 131072 | tf_op jit(solution)/shard_map/all_to_all | solution.py:27
  93.2 1.1 copy.39
  94.3 10.6 %all-to-all-done.5 = f32[4,1,4096]{2,1,0:T(1,128)S(1)} async-done(((f32[4,1,4096]{2,1,0:T(1,128)}), f32[4,1,4096]{2,1,0:T(1,128)S(1)}, u32[]{:S(2)}, u32[]{:S(2)}) %all-to-all-start.5) | async-done | bytes 65568 | tf_op jit(solution)/shard_map/all_to_all | solution.py:27
  104.8 0.1 reduce_sum.193
  105.0 4.1 %subtract_convert_fusion.1 = (bf16[384,2048]{1,0:T(8,128)(2,1)}, f32[384]{0:T(512)S(1)}) fusion(f32[384,2048]{1,0:T(8,128)} %get-tuple-element.21, bf16[384,2048]{1,0:T(8,128)(2,1)} %get-tuple-element.4, f32[2048]{0:T(1024)S(1)} %get-tuple-element.17), kind=kLoop, calls=%fused_computation.5 | loop fusion | flops 3931776 | bytes 6301184 | tf_op jit(solution)/shard_map/convert_element_type | solution.py:85
  109.1 1.6 subtract_convert_fusion
  110.7 0.6 broadcast_in_dim.26
  111.3 3.7 %all-to-all-start.6 = ((f32[16,1,384]{2,1,0:T(1,128)}), f32[16,1,384]{2,1,0:T(1,128)S(1)}, u32[]{:S(2)}, u32[]{:S(2)}) async-start(f32[16,1,384]{2,1,0:T(1,128)} %broadcast_in_dim.26), calls=%async_computation.6 | async-start | bytes 49152 | tf_op jit(solution)/shard_map/all_to_all | solution.py:27
  115.1 0.1 pad.6.clone
  115.2 6.4 %all-to-all-done.6 = f32[16,1,384]{2,1,0:T(1,128)S(1)} async-done(((f32[16,1,384]{2,1,0:T(1,128)}), f32[16,1,384]{2,1,0:T(1,128)S(1)}, u32[]{:S(2)}, u32[]{:S(2)}) %all-to-all-start.6) | async-done | bytes 24608 | tf_op jit(solution)/shard_map/all_to_all | solution.py:27
  121.7 0.1 fusion.19
  121.8 0.7 fusion.5
  122.6 0.5 copy-done.4
  123.1 0.7 fusion.1
  123.8 0.2 copy-done
  124.1 0.7 fusion.11
  124.8 0.5 copy-done.3
  125.3 0.7 fusion.7
  126.0 0.8 add_add_fusion
  126.8 0.9 add_add_fusion.1
  127.7 0.6 fusion
  128.4 2.4 %copy.54 = f32[256,8,512]{2,1,0:T(8,128)S(1)} copy(f32[256,8,512]{2,0,1:T(8,128)S(1)} %fusion) | data formatting | bytes 8388608 | tf_op jit(solution)/shard_map/slice | solution.py:115
  130.8 0.1 broadcast_in_dim.29
  130.9 0.8 pad_maximum_fusion
  131.6 11.7 %all_to_all.62 = f32[2,1152,512]{2,1,0:T(8,128)} all-to-all(f32[2,1152,512]{2,1,0:T(8,128)S(1)} %bitcast.55), channel_id=1, replica_groups=mesh['z_hi'=4,'y'=4,'core'=2,'x'=4,'z_lo'=4] {'core'}, dimensions={0} | all-to-all | bytes 9437184 | tf_op jit(solution)/shard_map/all_to_all | solution.py:50
  143.3 3.1 %reduce_sum.197 = f32[1152,512]{1,0:T(8,128)S(1)} reduce(f32[2,1152,512]{2,1,0:T(8,128)} %all_to_all.62, f32[]{:T(128)} %constant.23.clone.1), dimensions={0}, to_apply=%region_17.0 | reduce | flops 589824 | bytes 7077892 | tf_op jit(solution)/shard_map/reduce_sum | solution.py:50
  146.4 32.1 %all_to_all.63 = f32[4,288,512]{2,1,0:T(8,128)} all-to-all(f32[4,288,512]{2,1,0:T(8,128)S(1)} %bitcast.57), channel_id=1, replica_groups=mesh['z_hi'=4,'y'=4,'core'=2,'x'=4,'z_lo'=4] {'y'}, dimensions={0} | all-to-all | bytes 4718592 | tf_op jit(solution)/shard_map/all_to_all | solution.py:50
  178.6 2.0 reduce_sum.198
  180.6 33.4 %all_to_all.64 = f32[4,72,512]{2,1,0:T(8,128)S(1)} all-to-all(f32[4,72,512]{2,1,0:T(8,128)S(1)} %bitcast.60), channel_id=1, replica_groups=mesh['z_hi'=4,'y'=4,'core'=2,'x'=4,'z_lo'=4] {'z_hi'}, dimensions={0} | all-to-all | bytes 1179648 | tf_op jit(solution)/shard_map/all_to_all | solution.py:50
  214.1 0.6 divide_log_fusion
  214.7 0.7 broadcast_divide_fusion
  (46 shorter events, 0.5 us)
Async XLA Ops:
  0.7 4.0 %copy-start.5 = (bf16[384,256]{1,0:T(8,128)(2,1)S(1)}, bf16[384,256]{1,0:T(8,128)(2,1)}, u32[]{:S(2)}) copy-start(bf16[384,256]{1,0:T(8,128)(2,1)} %param.4) | copy-start | bytes 589828
  0.7 4.0 %copy-start.7 = (bf16[4096,256]{1,0:T(8,128)(2,1)S(1)}, bf16[4096,256]{1,0:T(8,128)(2,1)}, u32[]{:S(2)}) copy-start(bf16[4096,256]{1,0:T(8,128)(2,1)} %param.5) | copy-start | bytes 6291460
  0.7 4.0 %copy-start.8 = (s32[384]{0:T(512)S(1)}, s32[384]{0:T(512)}, u32[]{:S(2)}) copy-start(s32[384]{0:T(512)} %param.6) | copy-start | bytes 4612
  21.4 38.8 %copy-start.6 = (s32[4096]{0:T(1024)S(1)}, s32[4096]{0:T(1024)}, u32[]{:S(2)}) copy-start(s32[4096]{0:T(1024)} %param.7) | copy-start | bytes 49156
  89.9 14.9 %all-to-all-start.5 = ((f32[4,1,4096]{2,1,0:T(1,128)}), f32[4,1,4096]{2,1,0:T(1,128)S(1)}, u32[]{:S(2)}, u32[]{:S(2)}) async-start(f32[4,1,4096]{2,1,0:T(1,128)} %broadcast_in_dim.25), calls=%async_computation.5 | async-start | bytes 131072 | tf_op jit(solution)/shard_map/all_to_all | solution.py:27
  104.9 4.1 %copy-start.1 = (bf16[384,2048]{1,0:T(8,128)(2,1)S(1)}, bf16[384,2048]{1,0:T(8,128)(2,1)}, u32[]{:S(2)}) copy-start(bf16[384,2048]{1,0:T(8,128)(2,1)} %get-tuple-element.5) | copy-start | bytes 4718596
  110.7 11.1 %copy-start.2 = (bf16[384,2048]{1,0:T(8,128)(2,1)S(1)}, bf16[384,2048]{1,0:T(8,128)(2,1)}, u32[]{:S(2)}) copy-start(bf16[384,2048]{1,0:T(8,128)(2,1)} %get-tuple-element.5) | copy-start | bytes 4718596
  111.3 10.3 %all-to-all-start.6 = ((f32[16,1,384]{2,1,0:T(1,128)}), f32[16,1,384]{2,1,0:T(1,128)S(1)}, u32[]{:S(2)}, u32[]{:S(2)}) async-start(f32[16,1,384]{2,1,0:T(1,128)} %broadcast_in_dim.26), calls=%async_computation.6 | async-start | bytes 49152 | tf_op jit(solution)/shard_map/all_to_all | solution.py:27
  121.7 1.4 copy-start.4
  122.5 1.5 copy-start
  123.8 1.5 copy-start.3
